TPU v7x, 256 devices: a whole 4x4x8 slice. The times are simulated.
256 devices in a mesh: gz: 32 (over z, y_hi, core), ch: 8 (over y_lo, x).
Axes of the slice: x: 4, y: 4 (y_hi: 2, y_lo: 2; y = y_hi * 2 + y_lo), z: 8, core: 2. Of those that a mesh axis runs over, the one named last changes fastest.
Arguments:
- volume: bfloat16 [64, 1024, 512], P('ch', 'gz'), may hold values from -6 to 6
- plane_a: bfloat16 [2, 64, 64, 3, 3], P(None, 'ch'), may hold values from -0.375 to 0.375
- plane_b: bfloat16 [2, 64, 64, 3, 3], P(None, 'ch'), may hold values from -0.375 to 0.375
- depth: bfloat16 [2, 64, 64, 3], P(None, 'ch'), may hold values from -0.625 to 0.625
Outputs:
- features: bfloat16 [64, 1024, 512], P('ch', 'gz')
All inputs are finite; a program needn't handle non-finite values.
Results may differ from a plain program's by a relative error of at most 0.015.
Values may be sent and summed in bfloat16 or wider, within the bound.
No kernel may reach another device: no remote copies, remote signals or barrier semaphores. Data moves between devices by JAX's collectives and lax.ppermute only.
A program may use at most 64 MiB of HBM per device.

v0:
```python
import jax
import jax.numpy as jnp
from jax import lax
from jax.sharding import PartitionSpec as P

Y = 8


def from_behind(block, axis, distance):
    devices = range(lax.axis_size(axis))
    route = [(i - distance, i) for i in devices if i - distance in devices]
    return lax.ppermute(block, axis, route)


def plane_taps(filter_weight, widened, out_len, y_len, base):
    y_pos = lax.iota(jnp.int32, out_len) % y_len
    low_ok = y_pos >= 1
    high_ok = y_pos <= y_len - 2
    total = None
    for tap_a in range(3):
        for tap_b in range(3):
            offset = base + (tap_a - 1) * y_len + (tap_b - 1)
            moved = widened[:, :, offset : offset + out_len]
            term = jnp.einsum(
                "oi,isp->osp",
                filter_weight[:, :, tap_a, tap_b],
                moved,
                preferred_element_type=jnp.float32,
            )
            if tap_b == 0:
                term = jnp.where(low_ok, term, 0.0)
            elif tap_b == 2:
                term = jnp.where(high_ok, term, 0.0)
            total = term if total is None else total + term
    return total


def plane_terms(piece, filter_weight):
    plane_len = piece.shape[2]
    widened = jnp.pad(piece, ((0, 0), (0, 0), (Y + 1, Y + 1)))
    return plane_taps(filter_weight, widened, plane_len, Y, Y + 1)


def depth_products(piece, filter_weight):
    return jnp.einsum("oit,isp->tosp", filter_weight, piece, preferred_element_type=jnp.float32)


def local(volume, plane_a, plane_b, depth):
    layers = plane_a.shape[0]
    running_state = volume
    for layer_index in range(layers):
        summed = plane_terms(
            lax.all_gather(running_state, "ch", axis=0, tiled=True),
            filter_weight=plane_a[layer_index],
        )
        first = jnp.maximum(summed, 0.0).astype(jnp.bfloat16)
        summed = plane_terms(
            lax.all_gather(first, "ch", axis=0, tiled=True), filter_weight=plane_b[layer_index]
        )
        second = jnp.maximum(summed, 0.0).astype(jnp.bfloat16)
        products = depth_products(
            lax.all_gather(second, "ch", axis=0, tiled=True), filter_weight=depth[layer_index]
        )
        lower = from_behind(products[0].astype(jnp.bfloat16), "gz", 2).astype(jnp.float32)
        upper = from_behind(products[2].astype(jnp.bfloat16), "gz", -2).astype(jnp.float32)
        running_state = jnp.maximum(lower + products[1] + upper, 0.0).astype(jnp.bfloat16)
    return running_state


def solution(mesh):
    return jax.shard_map(
        local,
        mesh=mesh,
        in_specs=(
            P("ch", "gz", None),
            P(None, "ch", None, None, None),
            P(None, "ch", None, None, None),
            P(None, "ch", None, None),
        ),
        out_specs=P("ch", "gz", None),
        check_vma=False,
    )
```

profile of v0, /device:TPU:96, one launch (start us, length us, event | category | flops | bytes accessed | tf_op | source)
XLA Modules:
  0.0 352.6 jit_solution(16705611944146706218)
XLA Ops:
  6.5 1.8 copy.5
  9.2 45.6 %all-gather.7.cloned.1.call-done = bf16[64,32,512]{2,0,1:T(8,128)(2,1)} async-done(((bf16[8,32,512]{2,0,1:T(8,128)(2,1)}), bf16[64,32,512]{2,0,1:T(8,128)(2,1)}) %all-gather.7.cloned.1.call-update) | async-done | bytes 2097168 | tf_op jit(solution)/shard_map/all_gather | solution.py:53
  54.8 2.6 fusion.1
  60.3 0.9 fusion.70
  62.9 1.6 fusion.110
  64.8 43.1 %all-gather.9.cloned.1.call-done = bf16[64,32,512]{2,0,1:T(8,128)(2,1)} async-done(((bf16[8,32,512]{2,0,1:T(8,128)(2,1)}), bf16[64,32,512]{2,0,1:T(8,128)(2,1)}) %all-gather.9.cloned.1.call-update) | async-done | bytes 2097168 | tf_op jit(solution)/shard_map/all_gather | solution.py:58
  107.9 2.6 fusion.9
  112.5 0.9 fusion.79
  113.4 0.9 fusion.81
  116.0 1.6 fusion.111
  117.7 43.3 %all-gather.11.cloned.1.call-done = bf16[64,32,512]{2,0,1:T(8,128)(2,1)} async-done(((bf16[8,32,512]{2,0,1:T(8,128)(2,1)}), bf16[64,32,512]{2,0,1:T(8,128)(2,1)}) %all-gather.11.cloned.1.call-update) | async-done | bytes 2097168 | tf_op jit(solution)/shard_map/all_gather | solution.py:62
  161.0 2.0 fusion.167
  163.1 4.6 %collective-permute-start = (bf16[8,32,512]{2,0,1:T(8,128)(2,1)S(1)}, bf16[8,32,512]{2,0,1:T(8,128)(2,1)S(1)}, u32[]{:S(2)}, u32[]{:S(2)}) collective-permute-start(bf16[8,32,512]{2,0,1:T(8,128)(2,1)S(1)} %get-tuple-element.7), channel_id=1, source_target_pairs={{0,16},{8,24},{16,32},{24,40},{32,48},{40,56},{48,64},{56,72},{64,... | collective-permute-start | bytes 786440 | tf_op jit(solution)/shard_map/ppermute | solution.py:12
  167.7 3.6 %collective-permute-start.1 = (bf16[8,32,512]{2,0,1:T(8,128)(2,1)S(1)}, bf16[8,32,512]{2,0,1:T(8,128)(2,1)S(1)}, u32[]{:S(2)}, u32[]{:S(2)}) collective-permute-start(bf16[8,32,512]{2,0,1:T(8,128)(2,1)S(1)} %get-tuple-element.8), channel_id=1, source_target_pairs={{16,0},{24,8},{32,16},{40,24},{48,32},{56,40},{64,48},{72,56},{80,... | collective-permute-start | bytes 786440 | tf_op jit(solution)/shard_map/ppermute | solution.py:12
  171.3 3.1 collective-permute-done
  174.4 3.1 collective-permute-done.1
  178.6 43.6 %all-gather.13.cloned.1.call-done = bf16[64,32,512]{2,0,1:T(8,128)(2,1)} async-done(((bf16[8,32,512]{2,0,1:T(8,128)(2,1)}), bf16[64,32,512]{2,0,1:T(8,128)(2,1)}) %all-gather.13.cloned.1.call-update) | async-done | bytes 2097168 | tf_op jit(solution)/shard_map/all_gather | solution.py:53
  222.2 2.6 fusion.17
  226.9 0.9 fusion.87
  227.8 0.9 fusion.89
  230.4 1.6 fusion.112
  232.3 43.0 %all-gather.15.cloned.1.call-done = bf16[64,32,512]{2,0,1:T(8,128)(2,1)} async-done(((bf16[8,32,512]{2,0,1:T(8,128)(2,1)}), bf16[64,32,512]{2,0,1:T(8,128)(2,1)}) %all-gather.15.cloned.1.call-update) | async-done | bytes 2097168 | tf_op jit(solution)/shard_map/all_gather | solution.py:58
  275.3 2.6 fusion.25
  279.9 0.9 fusion.95
  280.8 0.9 fusion.97
  283.4 1.6 fusion.113
  285.0 43.3 %all-gather.17.cloned.1.call-done = bf16[64,32,512]{2,0,1:T(8,128)(2,1)} async-done(((bf16[8,32,512]{2,0,1:T(8,128)(2,1)}), bf16[64,32,512]{2,0,1:T(8,128)(2,1)}) %all-gather.17.cloned.1.call-update) | async-done | bytes 2097168 | tf_op jit(solution)/shard_map/all_gather | solution.py:62
  328.4 2.0 fusion.168
  330.5 4.6 %collective-permute-start.2 = (bf16[8,32,512]{2,0,1:T(8,128)(2,1)S(1)}, bf16[8,32,512]{2,0,1:T(8,128)(2,1)S(1)}, u32[]{:S(2)}, u32[]{:S(2)}) collective-permute-start(bf16[8,32,512]{2,0,1:T(8,128)(2,1)S(1)} %get-tuple-element.5), channel_id=1, source_target_pairs={{0,16},{8,24},{16,32},{24,40},{32,48},{40,56},{48,64},{56,72},{64,... | collective-permute-start | bytes 786440 | tf_op jit(solution)/shard_map/ppermute | solution.py:12
  335.1 3.6 %collective-permute-start.3 = (bf16[8,32,512]{2,0,1:T(8,128)(2,1)S(1)}, bf16[8,32,512]{2,0,1:T(8,128)(2,1)S(1)}, u32[]{:S(2)}, u32[]{:S(2)}) collective-permute-start(bf16[8,32,512]{2,0,1:T(8,128)(2,1)S(1)} %get-tuple-element.6), channel_id=1, source_target_pairs={{16,0},{24,8},{32,16},{40,24},{48,32},{56,40},{64,48},{72,56},{80,... | collective-permute-start | bytes 786440 | tf_op jit(solution)/shard_map/ppermute | solution.py:12
  338.7 3.1 collective-permute-done.2
  341.8 3.1 collective-permute-done.3
  (54 shorter events, 19.7 us)
Async XLA Ops:
  6.5 48.2 %all-gather.7.cloned.1.call-start = ((), (), s32[]{:S(2)}) async-start(), calls=%async_computation | async-start | bytes 2359296 | tf_op jit(solution)/shard_map/all_gather | solution.py:53
  8.4 99.5 %all-gather.9.cloned.1.call-start = ((), (), s32[]{:S(2)}) async-start(), calls=%async_computation.1 | async-start | bytes 2359296 | tf_op jit(solution)/shard_map/all_gather | solution.py:58
  54.8 2.6 copy-start
  62.9 1.8 copy-start.4
  64.5 96.4 %all-gather.11.cloned.1.call-start = ((), (), s32[]{:S(2)}) async-start(), calls=%async_computation.2 | async-start | bytes 2359296 | tf_op jit(solution)/shard_map/all_gather | solution.py:62
  107.9 2.6 copy-start.2
  116.0 44.9 %copy-start.5 = (bf16[2,8,64,3]{2,1,3,0:T(8,128)(2,1)S(1)}, bf16[2,8,64,3]{2,1,3,0:T(8,128)(2,1)}, u32[]{:S(2)}) copy-start(bf16[2,8,64,3]{2,1,3,0:T(8,128)(2,1)} %param.7) | copy-start | bytes 18436
  117.6 104.6 %all-gather.13.cloned.1.call-start = ((), (), s32[]{:S(2)}) async-start(), calls=%async_computation.3 | async-start | bytes 2359296 | tf_op jit(solution)/shard_map/all_gather | solution.py:53
  163.1 11.3 %collective-permute-start = (bf16[8,32,512]{2,0,1:T(8,128)(2,1)S(1)}, bf16[8,32,512]{2,0,1:T(8,128)(2,1)S(1)}, u32[]{:S(2)}, u32[]{:S(2)}) collective-permute-start(bf16[8,32,512]{2,0,1:T(8,128)(2,1)S(1)} %get-tuple-element.7), channel_id=1, source_target_pairs={{0,16},{8,24},{16,32},{24,40},{32,48},{40,56},{48,64},{56,72},{64,... | collective-permute-start | bytes 786440 | tf_op jit(solution)/shard_map/ppermute | solution.py:12
  167.7 9.8 %collective-permute-start.1 = (bf16[8,32,512]{2,0,1:T(8,128)(2,1)S(1)}, bf16[8,32,512]{2,0,1:T(8,128)(2,1)S(1)}, u32[]{:S(2)}, u32[]{:S(2)}) collective-permute-start(bf16[8,32,512]{2,0,1:T(8,128)(2,1)S(1)} %get-tuple-element.8), channel_id=1, source_target_pairs={{16,0},{24,8},{32,16},{40,24},{48,32},{56,40},{64,48},{72,56},{80,... | collective-permute-start | bytes 786440 | tf_op jit(solution)/shard_map/ppermute | solution.py:12
  178.3 97.0 %all-gather.15.cloned.1.call-start = ((), (), s32[]{:S(2)}) async-start(), calls=%async_computation.4 | async-start | bytes 2359296 | tf_op jit(solution)/shard_map/all_gather | solution.py:58
  222.2 2.6 copy-start.3
  232.0 96.4 %all-gather.17.cloned.1.call-start = ((), (), s32[]{:S(2)}) async-start(), calls=%async_computation.5 | async-start | bytes 2359296 | tf_op jit(solution)/shard_map/all_gather | solution.py:62
  275.3 2.6 copy-start.1
  330.5 11.3 %collective-permute-start.2 = (bf16[8,32,512]{2,0,1:T(8,128)(2,1)S(1)}, bf16[8,32,512]{2,0,1:T(8,128)(2,1)S(1)}, u32[]{:S(2)}, u32[]{:S(2)}) collective-permute-start(bf16[8,32,512]{2,0,1:T(8,128)(2,1)S(1)} %get-tuple-element.5), channel_id=1, source_target_pairs={{0,16},{8,24},{16,32},{24,40},{32,48},{40,56},{48,64},{56,72},{64,... | collective-permute-start | bytes 786440 | tf_op jit(solution)/shard_map/ppermute | solution.py:12
  335.1 9.8 %collective-permute-start.3 = (bf16[8,32,512]{2,0,1:T(8,128)(2,1)S(1)}, bf16[8,32,512]{2,0,1:T(8,128)(2,1)S(1)}, u32[]{:S(2)}, u32[]{:S(2)}) collective-permute-start(bf16[8,32,512]{2,0,1:T(8,128)(2,1)S(1)} %get-tuple-element.6), channel_id=1, source_target_pairs={{16,0},{24,8},{32,16},{40,24},{48,32},{56,40},{64,48},{72,56},{80,... | collective-permute-start | bytes 786440 | tf_op jit(solution)/shard_map/ppermute | solution.py:12
Sparse Core Ops, SparseCore 0:
  9.1 45.6 all-gather.6
  64.7 43.1 all-gather.8
  117.7 43.1 all-gather.10
  178.4 43.7 all-gather.12
  232.1 43.1 all-gather.14
  285.2 43.1 all-gather.16
where the time goes:
time: 355 us; the launch traced here: 353 us
  waiting for transfers between devices  274 us (77%)
  matrix products  42.9 us (12%)
  starting transfers between devices  17.4 us (5%)
  between operations  13.6 us (4%)
    all_gather x2, waiting for transfers between devices, local(): lax.all_gather(running_state, 'ch', axis=0, tiled=True)  89.2 us
    all_gather x2, waiting for transfers between devices, local(): lax.all_gather(second, 'ch', axis=0, tiled=True)  86.6 us
    all_gather x2, waiting for transfers between devices, local(): lax.all_gather(first, 'ch', axis=0, tiled=True)  86.1 us
    dot_general x36, matrix products, plane_taps(): jnp.einsum('oi,isp->osp', filter_weight[:, :, tap_a, tap_b], moved, prefe...  38.9 us
    ppermute x4, starting transfers between devices, from_behind(): return lax.ppermute(block, axis, route)  16.5 us
    ppermute x4, waiting for transfers between devices, from_behind(): return lax.ppermute(block, axis, route)  12.3 us
  transfers between devices with their start and end apart: 10, of which 10 were waited for; matrix products, arithmetic and copies ran while one was open for 0% of the time, Pallas kernels for 0%

commit v1 on v0

v1 whole, which is shorter than its diff:
```python
import jax
import jax.numpy as jnp
from jax import lax
from jax.sharding import PartitionSpec as P

X = 64
Y = 8


def from_behind(block, axis, distance):
    devices = range(lax.axis_size(axis))
    route = [(i - distance, i) for i in devices if i - distance in devices]
    return lax.ppermute(block, axis, route)


def gather_weights(plane_a, plane_b, depth):
    layers, out_part, chans = plane_a.shape[:3]
    packed = jnp.concatenate(
        [
            plane_a.reshape(layers, out_part, -1),
            plane_b.reshape(layers, out_part, -1),
            depth.reshape(layers, out_part, -1),
        ],
        axis=2,
    )
    packed = lax.all_gather(packed, "ch", axis=1, tiled=True)
    cut_a = chans * 9
    full_a = packed[:, :, :cut_a].reshape(layers, -1, chans, 3, 3)
    full_b = packed[:, :, cut_a : 2 * cut_a].reshape(layers, -1, chans, 3, 3)
    full_d = packed[:, :, 2 * cut_a :].reshape(layers, -1, chans, 3)
    return full_a, full_b, full_d


def plane_conv(h, weight):
    out = lax.conv_general_dilated(
        h,
        weight,
        (1, 1),
        ((1, 1), (1, 1)),
        dimension_numbers=("CNHW", "OIHW", "CNHW"),
        preferred_element_type=jnp.float32,
    )
    return jnp.maximum(out, 0.0).astype(jnp.bfloat16)


def depth_conv(second, weight):
    lower = from_behind(second, "gz", 2)
    upper = from_behind(second, "gz", -2)
    total = jnp.einsum("oi,isxy->osxy", weight[:, :, 1], second, preferred_element_type=jnp.float32)
    total = total + jnp.einsum("oi,isxy->osxy", weight[:, :, 0], lower, preferred_element_type=jnp.float32)
    total = total + jnp.einsum("oi,isxy->osxy", weight[:, :, 2], upper, preferred_element_type=jnp.float32)
    return jnp.maximum(total, 0.0).astype(jnp.bfloat16)


def local(volume, plane_a, plane_b, depth):
    full_a, full_b, full_d = gather_weights(plane_a, plane_b, depth)
    part, slab, flat = volume.shape
    h = lax.all_to_all(volume, "ch", split_axis=1, concat_axis=0, tiled=True)
    chans, slices = h.shape[:2]
    h = h.reshape(chans, slices, X, Y)
    for layer_index in range(plane_a.shape[0]):
        first = plane_conv(h, full_a[layer_index])
        second = plane_conv(first, full_b[layer_index])
        h = depth_conv(second, full_d[layer_index])
    h = h.reshape(chans, slices, flat)
    return lax.all_to_all(h, "ch", split_axis=0, concat_axis=1, tiled=True)


def solution(mesh):
    return jax.shard_map(
        local,
        mesh=mesh,
        in_specs=(
            P("ch", "gz", None),
            P(None, "ch", None, None, None),
            P(None, "ch", None, None, None),
            P(None, "ch", None, None),
        ),
        out_specs=P("ch", "gz", None),
        check_vma=False,
    )
```

time: 355 us -> 153 us (0.43)
  waiting for transfers between devices: 274 us -> 27.3 us
  blocking collectives: 0 us -> 40.5 us
  local copies, waits for them, and re-layouts: 3.43 us -> 33.4 us
  matrix products: 42.9 us -> 20.1 us
  between operations: 13.6 us -> 0.26 us
  other arithmetic: 0.99 us -> 10.7 us
    all_gather x6 -> x0, waiting for transfers between devices: 262 us -> none  [the longest x2 89.2 us: local(): lax.all_gather(running_state, 'ch', axis=0, tiled=True)]
    dot_general x38 -> x6, matrix products: 42.9 us -> 11.1 us  [the longest x2 4.35 us: depth_conv(): jnp.einsum('oi,isxy->osxy', weight[:, :, 0], lower, preferred_element_typ...]
    all_gather x0 -> x1, blocking collectives: none -> 29.6 us  [gather_weights(): packed = lax.all_gather(packed, 'ch', axis=1, tiled=True)]
    ppermute x4, waiting for transfers between devices: 12.3 us -> 27.3 us  [from_behind(): return lax.ppermute(block, axis, route)]
    reshape x0 -> x3, local copies, waits for them, and re-layouts: none -> 13 us  [the longest x2 11.6 us: local(): h = h.reshape(chans, slices, X, Y)]
    all_to_all x0 -> x1, blocking collectives: none -> 10.9 us  [local(): return lax.all_to_all(h, 'ch', split_axis=0, concat_axis=1, tiled=True)]
    concatenate x0 -> x1, other arithmetic: none -> 9.21 us  [gather_weights(): jnp.concatenate([plane_a.reshape(layers, out_part, -1), plane_b.reshape(l...]
    conv_general_dilated x0 -> x2, matrix products: none -> 8.99 us  [plane_conv(): lax.conv_general_dilated(h, weight, (1, 1), ((1, 1), (1, 1)), dimension_n...]
  transfers between devices with their start and end apart: 10 -> 5, of which waited for: 10 -> 2; matrix products, arithmetic and copies ran while one was open for 0% -> 19% of each run, Pallas kernels for 0% -> 0%
where the time goes in v1:
time: 153 us; the launch traced here: 152 us
  blocking collectives  40.5 us (26%)
  local copies, waits for them, and re-layouts  33.4 us (22%)
  waiting for transfers between devices  27.3 us (18%)
  starting transfers between devices  20.2 us (13%)
  matrix products  20.1 us (13%)
  other arithmetic  10.7 us (7%)
    all_gather x1, blocking collectives, gather_weights(): packed = lax.all_gather(packed, 'ch', axis=1, tiled=True)  29.6 us
    ppermute x4, waiting for transfers between devices, from_behind(): return lax.ppermute(block, axis, route)  27.3 us
    ppermute x4, starting transfers between devices, from_behind(): return lax.ppermute(block, axis, route)  14.9 us
    reshape x2, local copies, waits for them, and re-layouts, local(): h = h.reshape(chans, slices, X, Y)  11.6 us
    all_to_all x1, blocking collectives, local(): return lax.all_to_all(h, 'ch', split_axis=0, concat_axis=1, tiled=True)  10.9 us
    concatenate x1, other arithmetic, gather_weights(): jnp.concatenate([plane_a.reshape(layers, out_part, -1), plane_b.reshape(l...  9.21 us
    conv_general_dilated x2, matrix products, plane_conv(): lax.conv_general_dilated(h, weight, (1, 1), ((1, 1), (1, 1)), dimension_n...  8.99 us
    unnamed x12, local copies, waits for them, and re-layouts  7.47 us
  transfers between devices with their start and end apart: 5, of which 2 were waited for; matrix products, arithmetic and copies ran while one was open for 19% of the time, Pallas kernels for 0%

profile of v1, /device:TPU:96, one launch (start us, length us, event | category | flops | bytes accessed | tf_op | source)
XLA Modules:
  0.0 152.4 jit_solution(14980409646776555535)
XLA Ops:
  0.0 1.8 %copy.127 = bf16[8,32,512]{2,0,1:T(8,128)(2,1)} copy(bf16[8,32,512]{2,1,0:T(8,128)(2,1)} %param.4) | data formatting | bytes 524288 | tf_op args[0]
  1.8 5.3 %all-to-all-start = ((bf16[8,32,512]{2,0,1:T(8,128)(2,1)}), bf16[8,32,512]{2,0,1:T(8,128)(2,1)S(1)}, u32[]{:S(2)}, u32[]{:S(2)}) async-start(bf16[8,32,512]{2,0,1:T(8,128)(2,1)} %copy.127), calls=%async_computation | async-start | bytes 524288 | tf_op jit(solution)/shard_map/all_to_all | solution.py:58
  7.9 0.9 copy.120
  8.9 0.9 copy.119
  9.8 9.2 %pad_maximum_fusion = bf16[2,8,1344]{1,0,2:T(2,128)(2,1)S(1)} fusion(bf16[2,8,192]{1,0,2:T(2,128)(2,1)S(1)} %bitcast.80, bf16[2,8,576]{1,0,2:T(2,128)(2,1)S(1)} %bitcast.74, bf16[2,8,576]{1,0,2:T(2,128)(2,1)S(1)} %bitcast.75), kind=kLoop, calls=%fused_computation.10 | loop fusion | flops 43008 | bytes 86016 | tf_op jit(solution)/shard_map/concatenate | solution.py:18
  19.9 29.6 %all_gather.3 = bf16[2,64,1344]{2,0,1:T(2,128)(2,1)S(1)} all-gather(bf16[2,8,1344]{2,0,1:T(2,128)(2,1)S(1)} %copy.122), channel_id=1, replica_groups=mesh['gz'=32,'ch'=8] {'ch'}, dimensions={1}, use_global_device_ids=true | all-gather | bytes 387072 | tf_op jit(solution)/shard_map/all_gather | solution.py:26
  49.5 0.9 fusion.35
  55.2 5.9 %reshape.34 = bf16[64,4,64,8]{3,2,0,1:T(8,128)(2,1)} reshape(bf16[8,8,4,512]{3,1,0,2:T(8,128)(2,1)S(1)} %bitcast.76) | data formatting | bytes 524288 | tf_op jit(solution)/shard_map/reshape | solution.py:60
  61.1 5.7 %copy.130 = bf16[64,4,64,8]{0,1,3,2:T(4,128)(2,1)S(1)} copy(bf16[64,4,64,8]{3,2,0,1:T(8,128)(2,1)} %reshape.34) | data formatting | bytes 524288 | tf_op jit(solution)/shard_map/reshape | solution.py:60
  66.7 3.7 %fusion.1 = bf16[64,4,64,8]{0,1,3,2:T(4,128)(2,1)} fusion(bf16[64,4,64,8]{0,1,3,2:T(4,128)(2,1)S(1)} %copy.130, bf16[64,64,3,3]{0,3,2,1:T(4,128)(2,1)S(1)} %squeeze.41, bf16[64,64,3,3]{0,3,2,1:T(4,128)(2,1)S(1)} %squeeze.40), kind=kOutput, calls=%fused_computation.5 | convolution fusion | flops 274464768 | bytes 671744 | tf_op jit(solution)/shard_map/conv_general_dilated | solution.py:35
  70.5 4.3 %collective-permute-start.1 = (bf16[64,4,64,8]{0,1,3,2:T(4,128)(2,1)}, bf16[64,4,64,8]{0,1,3,2:T(4,128)(2,1)}, u32[]{:S(2)}, u32[]{:S(2)}) collective-permute-start(bf16[64,4,64,8]{0,1,3,2:T(4,128)(2,1)} %fusion.1), channel_id=1, source_target_pairs={{16,0},{24,8},{32,16},{40,24},{48,32},{56,40},{64,48},{72,56},{80,... | collective-permute-start | bytes 786440 | tf_op jit(solution)/shard_map/ppermute | solution.py:13
  74.8 3.2 %collective-permute-start = (bf16[64,4,64,8]{0,1,3,2:T(4,128)(2,1)}, bf16[64,4,64,8]{0,1,3,2:T(4,128)(2,1)}, u32[]{:S(2)}, u32[]{:S(2)}) collective-permute-start(bf16[64,4,64,8]{0,1,3,2:T(4,128)(2,1)} %fusion.1), channel_id=1, source_target_pairs={{0,16},{8,24},{16,32},{24,40},{32,48},{40,56},{48,64},{56,72},{64,... | collective-permute-start | bytes 786440 | tf_op jit(solution)/shard_map/ppermute | solution.py:13
  78.0 1.7 %fusion.14 = f32[64,4,64,8]{2,0,3,1:T(8,128)S(1)} fusion(bf16[64,4,64,8]{0,1,3,2:T(4,128)(2,1)} %fusion.1, bf16[64,64,1]{1,0,2:T(8,128)(2,1)S(1)} %copy.165), kind=kOutput, calls=%fused_computation.21 | convolution fusion | flops 16777216 | bytes 794624 | tf_op jit(solution)/shard_map/oi,isxy->osxy/dot_general | solution.py:49
  79.7 1.1 copy.137
  80.8 11.7 %collective-permute-done.1 = bf16[64,4,64,8]{0,1,3,2:T(4,128)(2,1)} collective-permute-done((bf16[64,4,64,8]{0,1,3,2:T(4,128)(2,1)}, bf16[64,4,64,8]{0,1,3,2:T(4,128)(2,1)}, u32[]{:S(2)}, u32[]{:S(2)}) %collective-permute-start.1) | collective-permute-done | bytes 262176 | tf_op jit(solution)/shard_map/ppermute | solution.py:13
  92.5 1.7 %fusion.10 = f32[64,4,64,8]{2,0,3,1:T(8,128)S(1)} fusion(bf16[64,4,64,8]{0,1,3,2:T(4,128)(2,1)} %collective-permute-done.1, bf16[64,64,1]{1,0,2:T(8,128)(2,1)} %copy.167), kind=kOutput, calls=%fused_computation.17 | convolution fusion | flops 16777216 | bytes 794624 | tf_op jit(solution)/shard_map/oi,isxy->osxy/dot_general | solution.py:51
  94.2 1.1 copy.141
  95.4 1.7 %fusion.12 = f32[64,4,64,8]{2,0,3,1:T(8,128)S(1)} fusion(bf16[64,4,64,8]{0,1,3,2:T(4,128)(2,1)} %collective-permute-done, bf16[64,64,1]{1,0,2:T(8,128)(2,1)} %copy.166), kind=kOutput, calls=%fused_computation.19 | convolution fusion | flops 16777216 | bytes 794624 | tf_op jit(solution)/shard_map/oi,isxy->osxy/dot_general | solution.py:50
  97.1 1.8 %copy.138 = f32[64,4,64,8]{0,1,3,2:T(4,128)} copy(f32[64,4,64,8]{2,0,3,1:T(8,128)S(1)} %fusion.12) | data formatting | bytes 1048576 | tf_op jit(solution)/shard_map/oi,isxy->osxy/dot_general | solution.py:50
  98.8 5.3 %fusion.3 = bf16[64,4,64,8]{0,1,3,2:T(4,128)(2,1)} fusion(f32[64,4,64,8]{0,1,3,2:T(4,128)S(1)} %copy.141, f32[64,4,64,8]{0,1,3,2:T(4,128)S(1)} %copy.137, f32[64,4,64,8]{0,1,3,2:T(4,128)} %copy.138, bf16[64,64,3,3]{0,3,2,1:T(4,128)(2,1)S(1)} %squeeze.45, bf16[64,64,3,3]{0,3,2,1:T(4,128)(2,1)S(1)} %squeeze.44), kind=kOutput, calls=%fused_computation.7 | convolution fusion | flops 274989056 | bytes 1982464 | tf_op jit(solution)/shard_map/conv_general_dilated | solution.py:35
  104.1 2.4 %collective-permute-start.3 = (bf16[64,4,64,8]{0,1,3,2:T(4,128)(2,1)}, bf16[64,4,64,8]{0,1,3,2:T(4,128)(2,1)}, u32[]{:S(2)}, u32[]{:S(2)}) collective-permute-start(bf16[64,4,64,8]{0,1,3,2:T(4,128)(2,1)} %fusion.3), channel_id=1, source_target_pairs={{16,0},{24,8},{32,16},{40,24},{48,32},{56,40},{64,48},{72,56},{80,... | collective-permute-start | bytes 786440 | tf_op jit(solution)/shard_map/ppermute | solution.py:13
  106.5 4.9 %collective-permute-start.2 = (bf16[64,4,64,8]{0,1,3,2:T(4,128)(2,1)}, bf16[64,4,64,8]{0,1,3,2:T(4,128)(2,1)}, u32[]{:S(2)}, u32[]{:S(2)}) collective-permute-start(bf16[64,4,64,8]{0,1,3,2:T(4,128)(2,1)} %fusion.3), channel_id=1, source_target_pairs={{0,16},{8,24},{16,32},{24,40},{32,48},{40,56},{48,64},{56,72},{64,... | collective-permute-start | bytes 786440 | tf_op jit(solution)/shard_map/ppermute | solution.py:13
  111.5 1.7 %fusion.8 = f32[64,4,64,8]{2,0,3,1:T(8,128)S(1)} fusion(bf16[64,4,64,8]{0,1,3,2:T(4,128)(2,1)} %fusion.3, bf16[64,64,1]{1,0,2:T(8,128)(2,1)S(1)} %copy-done), kind=kOutput, calls=%fused_computation.15 | convolution fusion | flops 16777216 | bytes 794624 | tf_op jit(solution)/shard_map/oi,isxy->osxy/dot_general | solution.py:49
  113.2 1.1 copy.149
  114.3 15.5 %collective-permute-done.3 = bf16[64,4,64,8]{0,1,3,2:T(4,128)(2,1)} collective-permute-done((bf16[64,4,64,8]{0,1,3,2:T(4,128)(2,1)}, bf16[64,4,64,8]{0,1,3,2:T(4,128)(2,1)}, u32[]{:S(2)}, u32[]{:S(2)}) %collective-permute-start.3) | collective-permute-done | bytes 262176 | tf_op jit(solution)/shard_map/ppermute | solution.py:13
  129.8 1.7 %fusion.4 = f32[64,4,64,8]{2,0,3,1:T(8,128)S(1)} fusion(bf16[64,4,64,8]{0,1,3,2:T(4,128)(2,1)} %collective-permute-done.3, bf16[64,64,1]{1,0,2:T(8,128)(2,1)} %copy.169), kind=kOutput, calls=%fused_computation.11 | convolution fusion | flops 16777216 | bytes 794624 | tf_op jit(solution)/shard_map/oi,isxy->osxy/dot_general | solution.py:51
  131.5 1.1 copy.153
  132.6 2.7 %fusion.6 = f32[64,4,64,8]{2,0,3,1:T(8,128)} fusion(bf16[64,4,64,8]{0,1,3,2:T(4,128)(2,1)} %collective-permute-done.2, bf16[64,64,1]{1,0,2:T(8,128)(2,1)S(1)} %copy.168), kind=kOutput, calls=%fused_computation.13 | convolution fusion | flops 16777216 | bytes 794624 | tf_op jit(solution)/shard_map/oi,isxy->osxy/dot_general | solution.py:50
  135.3 2.3 %copy.150 = f32[64,4,64,8]{0,1,3,2:T(4,128)S(1)} copy(f32[64,4,64,8]{2,0,3,1:T(8,128)} %fusion.6) | data formatting | bytes 1048576 | tf_op jit(solution)/shard_map/oi,isxy->osxy/dot_general | solution.py:50
  137.6 1.5 maximum_convert_fusion
  139.2 1.4 copy.154
  140.6 10.9 %all_to_all.33 = bf16[64,4,512]{2,1,0:T(4,128)(2,1)S(1)} all-to-all(bf16[64,4,512]{2,1,0:T(4,128)(2,1)S(1)} %copy.154), channel_id=1, replica_groups=mesh['gz'=32,'ch'=8] {'ch'}, dimensions={0} | all-to-all | bytes 524288 | tf_op jit(solution)/shard_map/all_to_all | solution.py:66
  (32 shorter events, 7.2 us)
Async XLA Ops:
  1.8 53.3 %all-to-all-start = ((bf16[8,32,512]{2,0,1:T(8,128)(2,1)}), bf16[8,32,512]{2,0,1:T(8,128)(2,1)S(1)}, u32[]{:S(2)}, u32[]{:S(2)}) async-start(bf16[8,32,512]{2,0,1:T(8,128)(2,1)} %copy.127), calls=%async_computation | async-start | bytes 524288 | tf_op jit(solution)/shard_map/all_to_all | solution.py:58
  70.5 22.1 %collective-permute-start.1 = (bf16[64,4,64,8]{0,1,3,2:T(4,128)(2,1)}, bf16[64,4,64,8]{0,1,3,2:T(4,128)(2,1)}, u32[]{:S(2)}, u32[]{:S(2)}) collective-permute-start(bf16[64,4,64,8]{0,1,3,2:T(4,128)(2,1)} %fusion.1), channel_id=1, source_target_pairs={{16,0},{24,8},{32,16},{40,24},{48,32},{56,40},{64,48},{72,56},{80,... | collective-permute-start | bytes 786440 | tf_op jit(solution)/shard_map/ppermute | solution.py:13
  74.8 20.6 %collective-permute-start = (bf16[64,4,64,8]{0,1,3,2:T(4,128)(2,1)}, bf16[64,4,64,8]{0,1,3,2:T(4,128)(2,1)}, u32[]{:S(2)}, u32[]{:S(2)}) collective-permute-start(bf16[64,4,64,8]{0,1,3,2:T(4,128)(2,1)} %fusion.1), channel_id=1, source_target_pairs={{0,16},{8,24},{16,32},{24,40},{32,48},{40,56},{48,64},{56,72},{64,... | collective-permute-start | bytes 786440 | tf_op jit(solution)/shard_map/ppermute | solution.py:13
  98.8 12.6 %copy-start = (bf16[64,64,1]{1,0,2:T(8,128)(2,1)S(1)}, bf16[64,64,1]{1,0,2:T(8,128)(2,1)}, u32[]{:S(2)}) copy-start(bf16[64,64,1]{1,0,2:T(8,128)(2,1)} %copy.164) | copy-start | bytes 24580
  104.1 25.7 %collective-permute-start.3 = (bf16[64,4,64,8]{0,1,3,2:T(4,128)(2,1)}, bf16[64,4,64,8]{0,1,3,2:T(4,128)(2,1)}, u32[]{:S(2)}, u32[]{:S(2)}) collective-permute-start(bf16[64,4,64,8]{0,1,3,2:T(4,128)(2,1)} %fusion.3), channel_id=1, source_target_pairs={{16,0},{24,8},{32,16},{40,24},{48,32},{56,40},{64,48},{72,56},{80,... | collective-permute-start | bytes 786440 | tf_op jit(solution)/shard_map/ppermute | solution.py:13
  106.5 26.1 %collective-permute-start.2 = (bf16[64,4,64,8]{0,1,3,2:T(4,128)(2,1)}, bf16[64,4,64,8]{0,1,3,2:T(4,128)(2,1)}, u32[]{:S(2)}, u32[]{:S(2)}) collective-permute-start(bf16[64,4,64,8]{0,1,3,2:T(4,128)(2,1)} %fusion.3), channel_id=1, source_target_pairs={{0,16},{8,24},{16,32},{24,40},{32,48},{40,56},{48,64},{56,72},{64,... | collective-permute-start | bytes 786440 | tf_op jit(solution)/shard_map/ppermute | solution.py:13

commit v2 on v1

--- a/solution.py
+++ b/solution.py
@@ -14,21 +14,11 @@
 
 
 def gather_weights(plane_a, plane_b, depth):
-    layers, out_part, chans = plane_a.shape[:3]
-    packed = jnp.concatenate(
-        [
-            plane_a.reshape(layers, out_part, -1),
-            plane_b.reshape(layers, out_part, -1),
-            depth.reshape(layers, out_part, -1),
-        ],
-        axis=2,
+    return (
+        lax.all_gather(plane_a, "ch", axis=1, tiled=True),
+        lax.all_gather(plane_b, "ch", axis=1, tiled=True),
+        lax.all_gather(depth, "ch", axis=1, tiled=True),
     )
-    packed = lax.all_gather(packed, "ch", axis=1, tiled=True)
-    cut_a = chans * 9
-    full_a = packed[:, :, :cut_a].reshape(layers, -1, chans, 3, 3)
-    full_b = packed[:, :, cut_a : 2 * cut_a].reshape(layers, -1, chans, 3, 3)
-    full_d = packed[:, :, 2 * cut_a :].reshape(layers, -1, chans, 3)
-    return full_a, full_b, full_d
 
 
 def plane_conv(h, weight):

time: 153 us -> 165 us (1.078)
  blocking collectives: 40.5 us -> 85.4 us
  local copies, waits for them, and re-layouts: 33.4 us -> 14.9 us
  other arithmetic: 10.7 us -> 0 us
  matrix products: 20.1 us -> 13.4 us
  starting transfers between devices: 20.2 us -> 22 us
    all_gather x1 -> x3, blocking collectives: 29.6 us -> 74.6 us  [the longest x1 25.9 us: gather_weights(): lax.all_gather(plane_b, 'ch', axis=1, tiled=True)]
    concatenate x1 -> x0, other arithmetic: 9.21 us -> none  [gather_weights(): jnp.concatenate([plane_a.reshape(layers, out_part, -1), plane_b.reshape(l...]
    dot_general x6 -> x0, local copies, waits for them, and re-layouts: 8.58 us -> none  [the longest x2 4.1 us: depth_conv(): jnp.einsum('oi,isxy->osxy', weight[:, :, 0], lower, preferred_element_typ...]
    unnamed x12 -> x1, local copies, waits for them, and re-layouts: 7.47 us -> 1.8 us
    dot_general x2, matrix products: 4.35 us -> 0.82 us  [depth_conv(): jnp.einsum('oi,isxy->osxy', weight[:, :, 0], lower, preferred_element_typ...]
    dot_general x2, matrix products: 3.38 us -> 0.84 us  [depth_conv(): jnp.einsum('oi,isxy->osxy', weight[:, :, 2], upper, preferred_element_typ...]
    dot_general x2, matrix products: 3.35 us -> 0.81 us  [depth_conv(): jnp.einsum('oi,isxy->osxy', weight[:, :, 1], second, preferred_element_ty...]
    slice x10 -> x0, local copies, waits for them, and re-layouts: 2.09 us -> none  [the longest x3 1.23 us: local(): first = plane_conv(h, full_a[layer_index])]
  transfers between devices with their start and end apart: 5 -> 5, of which waited for: 2 -> 4; matrix products, arithmetic and copies ran while one was open for 19% -> 1% of each run, Pallas kernels for 0% -> 0%
where the time goes in v2:
time: 165 us; the launch traced here: 164 us
  blocking collectives  85.4 us (52%)
  waiting for transfers between devices  28.4 us (17%)
  starting transfers between devices  22 us (13%)
  local copies, waits for them, and re-layouts  14.9 us (9%)
  matrix products  13.4 us (8%)
    ppermute x4, waiting for transfers between devices, from_behind(): return lax.ppermute(block, axis, route)  28.4 us
    all_gather x1, blocking collectives, gather_weights(): lax.all_gather(plane_b, 'ch', axis=1, tiled=True)  25.9 us
    all_gather x1, blocking collectives, gather_weights(): lax.all_gather(plane_a, 'ch', axis=1, tiled=True)  24.8 us
    all_gather x1, blocking collectives, gather_weights(): lax.all_gather(depth, 'ch', axis=1, tiled=True)  23.9 us
    ppermute x4, starting transfers between devices, from_behind(): return lax.ppermute(block, axis, route)  16.7 us
    reshape x2, local copies, waits for them, and re-layouts, local(): h = h.reshape(chans, slices, X, Y)  11.6 us
    conv_general_dilated x2, matrix products, plane_conv(): lax.conv_general_dilated(h, weight, (1, 1), ((1, 1), (1, 1)), dimension_n...  11 us
    all_to_all x1, blocking collectives, local(): return lax.all_to_all(h, 'ch', split_axis=0, concat_axis=1, tiled=True)  10.8 us
  transfers between devices with their start and end apart: 5, of which 4 were waited for; matrix products, arithmetic and copies ran while one was open for 1% of the time, Pallas kernels for 0%

profile of v2, /device:TPU:96, one launch (start us, length us, event | category | flops | bytes accessed | tf_op | source)
XLA Modules:
  0.0 164.3 jit_solution(17486440112829499366)
XLA Ops:
  0.0 1.8 %copy.37 = bf16[8,32,512]{2,0,1:T(8,128)(2,1)} copy(bf16[8,32,512]{2,1,0:T(8,128)(2,1)} %param.4) | data formatting | bytes 524288 | tf_op args[0]
  1.8 5.3 %all-to-all-start = ((bf16[8,32,512]{2,0,1:T(8,128)(2,1)}), bf16[8,32,512]{2,0,1:T(8,128)(2,1)S(1)}, u32[]{:S(2)}, u32[]{:S(2)}) async-start(bf16[8,32,512]{2,0,1:T(8,128)(2,1)} %copy.37), calls=%async_computation | async-start | bytes 524288 | tf_op jit(solution)/shard_map/all_to_all | solution.py:48
  7.1 25.9 %all_gather.10 = bf16[2,64,64,3,3]{2,1,4,3,0:T(8,128)(2,1)S(1)} all-gather(bf16[2,8,64,3,3]{2,1,4,3,0:T(8,128)(2,1)} %param.6), channel_id=1, replica_groups=mesh['gz'=32,'ch'=8] {'ch'}, dimensions={1}, use_global_device_ids=true | all-gather | bytes 165888 | tf_op jit(solution)/shard_map/all_gather | solution.py:19
  33.0 24.8 %all_gather.9 = bf16[2,64,64,3,3]{2,1,4,3,0:T(8,128)(2,1)S(1)} all-gather(bf16[2,8,64,3,3]{2,1,4,3,0:T(8,128)(2,1)} %param.5), channel_id=1, replica_groups=mesh['gz'=32,'ch'=8] {'ch'}, dimensions={1}, use_global_device_ids=true | all-gather | bytes 165888 | tf_op jit(solution)/shard_map/all_gather | solution.py:18
  57.9 23.9 %all_gather.11 = bf16[2,64,64,3]{2,1,3,0:T(8,128)(2,1)S(1)} all-gather(bf16[2,8,64,3]{2,1,3,0:T(8,128)(2,1)} %param.7), channel_id=1, replica_groups=mesh['gz'=32,'ch'=8] {'ch'}, dimensions={1}, use_global_device_ids=true | all-gather | bytes 55296 | tf_op jit(solution)/shard_map/all_gather | solution.py:20
  81.8 0.0 all-to-all-done
  81.8 5.9 %reshape.7 = bf16[64,4,64,8]{3,2,0,1:T(8,128)(2,1)} reshape(bf16[8,8,4,512]{3,1,0,2:T(8,128)(2,1)S(1)} %bitcast.81) | data formatting | bytes 524288 | tf_op jit(solution)/shard_map/reshape | solution.py:50
  87.7 5.7 %copy.39 = bf16[64,4,64,8]{0,1,3,2:T(4,128)(2,1)S(1)} copy(bf16[64,4,64,8]{3,2,0,1:T(8,128)(2,1)} %reshape.7) | data formatting | bytes 524288 | tf_op jit(solution)/shard_map/reshape | solution.py:50
  93.4 5.5 %fusion.5 = bf16[64,4,64,8]{0,1,3,2:T(4,128)(2,1)S(1)} fusion(bf16[64,4,64,8]{0,1,3,2:T(4,128)(2,1)S(1)} %copy.39, bf16[2,64,64,3,3]{2,1,4,3,0:T(8,128)(2,1)S(1)} %all_gather.10, bf16[2,64,64,3,3]{2,1,4,3,0:T(8,128)(2,1)S(1)} %all_gather.9), kind=kOutput, calls=%fused_computation.13 | convolution fusion | flops 274464768 | bytes 1081344 | tf_op jit(solution)/shard_map/conv_general_dilated | solution.py:25
  98.8 4.8 %collective-permute-start = (bf16[64,4,64,8]{0,1,3,2:T(4,128)(2,1)S(1)}, bf16[64,4,64,8]{0,1,3,2:T(4,128)(2,1)S(1)}, u32[]{:S(2)}, u32[]{:S(2)}) collective-permute-start(bf16[64,4,64,8]{0,1,3,2:T(4,128)(2,1)S(1)} %fusion.5), channel_id=1, source_target_pairs={{0,16},{8,24},{16,32},{24,40},{32,48},{40,56},{48,64},{56,72},{64,... | collective-permute-start | bytes 786440 | tf_op jit(solution)/shard_map/ppermute | solution.py:13
  103.7 3.6 %collective-permute-start.1 = (bf16[64,4,64,8]{0,1,3,2:T(4,128)(2,1)S(1)}, bf16[64,4,64,8]{0,1,3,2:T(4,128)(2,1)S(1)}, u32[]{:S(2)}, u32[]{:S(2)}) collective-permute-start(bf16[64,4,64,8]{0,1,3,2:T(4,128)(2,1)S(1)} %fusion.5), channel_id=1, source_target_pairs={{16,0},{24,8},{32,16},{40,24},{48,32},{56,40},{64,48},{72,56},{80,... | collective-permute-start | bytes 786440 | tf_op jit(solution)/shard_map/ppermute | solution.py:13
  107.3 0.4 fusion.16
  107.7 4.7 %collective-permute-done = bf16[64,4,64,8]{0,1,3,2:T(4,128)(2,1)S(1)} collective-permute-done((bf16[64,4,64,8]{0,1,3,2:T(4,128)(2,1)S(1)}, bf16[64,4,64,8]{0,1,3,2:T(4,128)(2,1)S(1)}, u32[]{:S(2)}, u32[]{:S(2)}) %collective-permute-start) | collective-permute-done | bytes 262176 | tf_op jit(solution)/shard_map/ppermute | solution.py:13
  112.4 0.4 convolution_add_fusion.3
  112.8 12.6 %collective-permute-done.1 = bf16[64,4,64,8]{0,1,3,2:T(4,128)(2,1)S(1)} collective-permute-done((bf16[64,4,64,8]{0,1,3,2:T(4,128)(2,1)S(1)}, bf16[64,4,64,8]{0,1,3,2:T(4,128)(2,1)S(1)}, u32[]{:S(2)}, u32[]{:S(2)}) %collective-permute-start.1) | collective-permute-done | bytes 262176 | tf_op jit(solution)/shard_map/ppermute | solution.py:13
  125.5 0.4 fusion.2
  125.9 5.5 %fusion.7 = bf16[64,4,64,8]{0,1,3,2:T(4,128)(2,1)S(1)} fusion(bf16[4,64,8,64]{3,1,2,0:T(8,128)(2,1)S(1)} %fusion.2, bf16[2,64,64,3,3]{2,1,4,3,0:T(8,128)(2,1)S(1)} %all_gather.10, bf16[2,64,64,3,3]{2,1,4,3,0:T(8,128)(2,1)S(1)} %all_gather.9), kind=kOutput, calls=%fused_computation.15 | convolution fusion | flops 274464768 | bytes 1081344 | tf_op jit(solution)/shard_map/conv_general_dilated | solution.py:25
  131.4 1.9 %collective-permute-start.2 = (bf16[64,4,64,8]{0,1,3,2:T(4,128)(2,1)S(1)}, bf16[64,4,64,8]{0,1,3,2:T(4,128)(2,1)S(1)}, u32[]{:S(2)}, u32[]{:S(2)}) collective-permute-start(bf16[64,4,64,8]{0,1,3,2:T(4,128)(2,1)S(1)} %fusion.7), channel_id=1, source_target_pairs={{0,16},{8,24},{16,32},{24,40},{32,48},{40,56},{48,64},{56,72},{64,... | collective-permute-start | bytes 786440 | tf_op jit(solution)/shard_map/ppermute | solution.py:13
  133.4 6.3 %collective-permute-start.3 = (bf16[64,4,64,8]{0,1,3,2:T(4,128)(2,1)S(1)}, bf16[64,4,64,8]{0,1,3,2:T(4,128)(2,1)S(1)}, u32[]{:S(2)}, u32[]{:S(2)}) collective-permute-start(bf16[64,4,64,8]{0,1,3,2:T(4,128)(2,1)S(1)} %fusion.7), channel_id=1, source_target_pairs={{16,0},{24,8},{32,16},{40,24},{48,32},{56,40},{64,48},{72,56},{80,... | collective-permute-start | bytes 786440 | tf_op jit(solution)/shard_map/ppermute | solution.py:13
  139.7 0.4 fusion.11
  140.1 6.0 %collective-permute-done.2 = bf16[64,4,64,8]{0,1,3,2:T(4,128)(2,1)S(1)} collective-permute-done((bf16[64,4,64,8]{0,1,3,2:T(4,128)(2,1)S(1)}, bf16[64,4,64,8]{0,1,3,2:T(4,128)(2,1)S(1)}, u32[]{:S(2)}, u32[]{:S(2)}) %collective-permute-start.2) | collective-permute-done | bytes 262176 | tf_op jit(solution)/shard_map/ppermute | solution.py:13
  146.1 0.4 convolution_add_fusion.1
  146.5 5.1 %collective-permute-done.3 = bf16[64,4,64,8]{0,1,3,2:T(4,128)(2,1)S(1)} collective-permute-done((bf16[64,4,64,8]{0,1,3,2:T(4,128)(2,1)S(1)}, bf16[64,4,64,8]{0,1,3,2:T(4,128)(2,1)S(1)}, u32[]{:S(2)}, u32[]{:S(2)}) %collective-permute-start.3) | collective-permute-done | bytes 262176 | tf_op jit(solution)/shard_map/ppermute | solution.py:13
  151.6 0.4 fusion.8
  152.0 0.3 copy.77
  152.4 0.3 copy.48
  152.6 10.8 %all_to_all.33 = bf16[64,4,512]{2,1,0:T(4,128)(2,1)S(1)} all-to-all(bf16[64,4,512]{2,1,0:T(4,128)(2,1)S(1)} %copy.48), channel_id=1, replica_groups=mesh['gz'=32,'ch'=8] {'ch'}, dimensions={0} | all-to-all | bytes 524288 | tf_op jit(solution)/shard_map/all_to_all | solution.py:56
  163.5 0.8 copy.51
  (4 shorter events, 0.1 us)
Async XLA Ops:
  1.8 80.0 %all-to-all-start = ((bf16[8,32,512]{2,0,1:T(8,128)(2,1)}), bf16[8,32,512]{2,0,1:T(8,128)(2,1)S(1)}, u32[]{:S(2)}, u32[]{:S(2)}) async-start(bf16[8,32,512]{2,0,1:T(8,128)(2,1)} %copy.37), calls=%async_computation | async-start | bytes 524288 | tf_op jit(solution)/shard_map/all_to_all | solution.py:48
  98.8 13.6 %collective-permute-start = (bf16[64,4,64,8]{0,1,3,2:T(4,128)(2,1)S(1)}, bf16[64,4,64,8]{0,1,3,2:T(4,128)(2,1)S(1)}, u32[]{:S(2)}, u32[]{:S(2)}) collective-permute-start(bf16[64,4,64,8]{0,1,3,2:T(4,128)(2,1)S(1)} %fusion.5), channel_id=1, source_target_pairs={{0,16},{8,24},{16,32},{24,40},{32,48},{40,56},{48,64},{56,72},{64,... | collective-permute-start | bytes 786440 | tf_op jit(solution)/shard_map/ppermute | solution.py:13
  103.7 21.8 %collective-permute-start.1 = (bf16[64,4,64,8]{0,1,3,2:T(4,128)(2,1)S(1)}, bf16[64,4,64,8]{0,1,3,2:T(4,128)(2,1)S(1)}, u32[]{:S(2)}, u32[]{:S(2)}) collective-permute-start(bf16[64,4,64,8]{0,1,3,2:T(4,128)(2,1)S(1)} %fusion.5), channel_id=1, source_target_pairs={{16,0},{24,8},{32,16},{40,24},{48,32},{56,40},{64,48},{72,56},{80,... | collective-permute-start | bytes 786440 | tf_op jit(solution)/shard_map/ppermute | solution.py:13
  131.4 14.6 %collective-permute-start.2 = (bf16[64,4,64,8]{0,1,3,2:T(4,128)(2,1)S(1)}, bf16[64,4,64,8]{0,1,3,2:T(4,128)(2,1)S(1)}, u32[]{:S(2)}, u32[]{:S(2)}) collective-permute-start(bf16[64,4,64,8]{0,1,3,2:T(4,128)(2,1)S(1)} %fusion.7), channel_id=1, source_target_pairs={{0,16},{8,24},{16,32},{24,40},{32,48},{40,56},{48,64},{56,72},{64,... | collective-permute-start | bytes 786440 | tf_op jit(solution)/shard_map/ppermute | solution.py:13
  133.4 18.2 %collective-permute-start.3 = (bf16[64,4,64,8]{0,1,3,2:T(4,128)(2,1)S(1)}, bf16[64,4,64,8]{0,1,3,2:T(4,128)(2,1)S(1)}, u32[]{:S(2)}, u32[]{:S(2)}) collective-permute-start(bf16[64,4,64,8]{0,1,3,2:T(4,128)(2,1)S(1)} %fusion.7), channel_id=1, source_target_pairs={{16,0},{24,8},{32,16},{40,24},{48,32},{56,40},{64,48},{72,56},{80,... | collective-permute-start | bytes 786440 | tf_op jit(solution)/shard_map/ppermute | solution.py:13

commit v3 on v2

--- a/solution.py
+++ b/solution.py
@@ -11,14 +11,6 @@
     devices = range(lax.axis_size(axis))
     route = [(i - distance, i) for i in devices if i - distance in devices]
     return lax.ppermute(block, axis, route)
-
-
-def gather_weights(plane_a, plane_b, depth):
-    return (
-        lax.all_gather(plane_a, "ch", axis=1, tiled=True),
-        lax.all_gather(plane_b, "ch", axis=1, tiled=True),
-        lax.all_gather(depth, "ch", axis=1, tiled=True),
-    )
 
 
 def plane_conv(h, weight):
@@ -42,17 +34,41 @@
     return jnp.maximum(total, 0.0).astype(jnp.bfloat16)
 
 
+def pack_weights(plane_a, plane_b, depth):
+    layers, out_part, chans = plane_a.shape[:3]
+    taps_a = jnp.transpose(plane_a, (0, 3, 4, 1, 2)).reshape(-1, out_part, chans)
+    taps_b = jnp.transpose(plane_b, (0, 3, 4, 1, 2)).reshape(-1, out_part, chans)
+    taps_d = jnp.transpose(depth, (0, 3, 1, 2)).reshape(-1, out_part, chans)
+    return jnp.concatenate([taps_a, taps_b, taps_d], axis=0)
+
+
 def local(volume, plane_a, plane_b, depth):
-    full_a, full_b, full_d = gather_weights(plane_a, plane_b, depth)
+    layers, out_part, chans = plane_a.shape[:3]
     part, slab, flat = volume.shape
-    h = lax.all_to_all(volume, "ch", split_axis=1, concat_axis=0, tiled=True)
-    chans, slices = h.shape[:2]
-    h = h.reshape(chans, slices, X, Y)
-    for layer_index in range(plane_a.shape[0]):
+    parts = lax.axis_size("ch")
+    slices = slab // parts
+    weights = pack_weights(plane_a, plane_b, depth)
+    taps = weights.shape[0]
+    sent_volume = jnp.transpose(volume.reshape(part, parts, slices, flat), (1, 0, 2, 3))
+    sent_volume = sent_volume.reshape(parts, part * slices, flat)
+    sent_weights = jnp.broadcast_to(
+        weights.reshape(1, -1, flat), (parts, taps * out_part * chans // flat, flat)
+    )
+    sent = jnp.concatenate([sent_volume, sent_weights], axis=1)
+    got = lax.all_to_all(sent, "ch", split_axis=0, concat_axis=0, tiled=True)
+    got = got.reshape(parts, -1, flat)
+    h = got[:, : part * slices].reshape(parts * part, slices, X, Y)
+    w = got[:, part * slices :].reshape(parts, taps, out_part, chans)
+    w = jnp.transpose(w, (1, 0, 2, 3)).reshape(taps, parts * out_part, chans)
+    nine = 9 * layers
+    full_a = w[:nine].reshape(layers, 3, 3, parts * out_part, chans).transpose(0, 3, 4, 1, 2)
+    full_b = w[nine : 2 * nine].reshape(layers, 3, 3, parts * out_part, chans).transpose(0, 3, 4, 1, 2)
+    full_d = w[2 * nine :].reshape(layers, 3, parts * out_part, chans).transpose(0, 2, 3, 1)
+    for layer_index in range(layers):
         first = plane_conv(h, full_a[layer_index])
         second = plane_conv(first, full_b[layer_index])
         h = depth_conv(second, full_d[layer_index])
-    h = h.reshape(chans, slices, flat)
+    h = h.reshape(parts * part, slices, flat)
     return lax.all_to_all(h, "ch", split_axis=0, concat_axis=1, tiled=True)
 
 

time: 165 us -> 131 us (0.79)
  blocking collectives: 85.4 us -> 26.3 us
  local copies, waits for them, and re-layouts: 14.9 us -> 27.7 us
  matrix products: 13.4 us -> 24.8 us
  starting transfers between devices: 22 us -> 15.1 us
  waiting for transfers between devices: 28.4 us -> 34.8 us
    all_gather x3 -> x0, blocking collectives: 74.6 us -> none  [the longest x1 25.9 us: gather_weights(): lax.all_gather(plane_b, 'ch', axis=1, tiled=True)]
    all_to_all x0 -> x1, blocking collectives: none -> 16.6 us  [local(): got = lax.all_to_all(sent, 'ch', split_axis=0, concat_axis=0, tiled=True)]
    dot_general x0 -> x6, local copies, waits for them, and re-layouts: none -> 8.57 us  [the longest x2 4.1 us: depth_conv(): jnp.einsum('oi,isxy->osxy', weight[:, :, 0], lower, preferred_element_typ...]
    ppermute x4, waiting for transfers between devices: 28.4 us -> 34.8 us  [from_behind(): return lax.ppermute(block, axis, route)]
    all_to_all x1 -> x0, starting transfers between devices: 5.31 us -> none  [local(): h = lax.all_to_all(volume, 'ch', split_axis=1, concat_axis=0, tiled=True)]
    dot_general x2, matrix products: 0.82 us -> 4.32 us  [depth_conv(): jnp.einsum('oi,isxy->osxy', weight[:, :, 0], lower, preferred_element_typ...]
    conv_general_dilated x2, matrix products: 11 us -> 13.8 us  [plane_conv(): lax.conv_general_dilated(h, weight, (1, 1), ((1, 1), (1, 1)), dimension_n...]
    dot_general x2, matrix products: 0.81 us -> 3.35 us  [depth_conv(): jnp.einsum('oi,isxy->osxy', weight[:, :, 1], second, preferred_element_ty...]
  transfers between devices with their start and end apart: 5 -> 4, of which waited for: 4 -> 2; matrix products, arithmetic and copies ran while one was open for 1% -> 9% of each run, Pallas kernels for 0% -> 0%
where the time goes in v3:
time: 131 us
  waiting for transfers between devices  34.8 us (27%)
  local copies, waits for them, and re-layouts  27.7 us (21%)
  blocking collectives  26.3 us (20%)
  matrix products  24.8 us (19%)
  starting transfers between devices  15.1 us (12%)
  other arithmetic  1.6 us (1%)
    ppermute x4, waiting for transfers between devices, from_behind(): return lax.ppermute(block, axis, route)  34.8 us
    all_to_all x1, blocking collectives, local(): got = lax.all_to_all(sent, 'ch', split_axis=0, concat_axis=0, tiled=True)  16.6 us
    ppermute x4, starting transfers between devices, from_behind(): return lax.ppermute(block, axis, route)  15.1 us
    conv_general_dilated x2, matrix products, plane_conv(): lax.conv_general_dilated(h, weight, (1, 1), ((1, 1), (1, 1)), dimension_n...  13.8 us
    reshape x2, local copies, waits for them, and re-layouts, local(): h = got[:, :part * slices].reshape(parts * part, slices, X, Y)  12.4 us
    all_to_all x1, blocking collectives, local(): return lax.all_to_all(h, 'ch', split_axis=0, concat_axis=1, tiled=True)  9.7 us
    dot_general x2, matrix products, depth_conv(): jnp.einsum('oi,isxy->osxy', weight[:, :, 0], lower, preferred_element_typ...  4.32 us
    dot_general x2, local copies, waits for them, and re-layouts, depth_conv(): jnp.einsum('oi,isxy->osxy', weight[:, :, 0], lower, preferred_element_typ...  4.1 us
  transfers between devices with their start and end apart: 4, of which 2 were waited for; matrix products, arithmetic and copies ran while one was open for 9% of the time, Pallas kernels for 0%

profile of v3, /device:TPU:96, one launch (start us, length us, event | category | flops | bytes accessed | tf_op | source)
XLA Modules:
  0.0 130.6 jit_solution(4550030304154901560)
XLA Ops:
  0.0 0.8 concatenate.15
  0.8 0.9 concatenate.14
  1.7 0.9 concatenate.13
  2.5 1.1 copy.54
  4.0 16.6 %all_to_all.23 = bf16[8,74,512]{2,1,0:T(8,128)(2,1)S(1)} all-to-all(bf16[8,74,512]{2,1,0:T(8,128)(2,1)S(1)} %pad_maximum_fusion), channel_id=1, replica_groups=mesh['gz'=32,'ch'=8] {'ch'}, dimensions={0} | all-to-all | bytes 1212416 | tf_op jit(solution)/shard_map/all_to_all | solution.py:58
  20.8 0.3 reshape.43
  21.3 5.9 %reshape.45 = bf16[64,4,64,8]{3,2,1,0:T(8,128)(2,1)} reshape(bf16[8,32,512]{2,1,0:T(8,128)(2,1)S(1)} %slice.77) | data formatting | bytes 524288 | tf_op jit(solution)/shard_map/reshape | solution.py:60
  27.2 6.4 %copy.58 = bf16[64,4,64,8]{0,1,3,2:T(4,128)(2,1)S(1)} copy(bf16[64,4,64,8]{3,2,1,0:T(8,128)(2,1)} %reshape.45) | data formatting | bytes 524288 | tf_op jit(solution)/shard_map/reshape | solution.py:60
  33.6 6.3 %fusion.1 = bf16[64,4,64,8]{0,1,3,2:T(4,128)(2,1)} fusion(bf16[64,4,64,8]{0,1,3,2:T(4,128)(2,1)S(1)} %copy.58, bf16[2,64,64,3,3]{2,1,4,3,0:T(8,128)(2,1)S(1)} %bitcast.105, bf16[2,64,64,3,3]{2,1,4,3,0:T(8,128)(2,1)S(1)} %bitcast.103), kind=kOutput, calls=%fused_computation.5 | convolution fusion | flops 274464768 | bytes 1081344 | tf_op jit(solution)/shard_map/conv_general_dilated | solution.py:17
  39.9 4.3 %collective-permute-start.1 = (bf16[64,4,64,8]{0,1,3,2:T(4,128)(2,1)}, bf16[64,4,64,8]{0,1,3,2:T(4,128)(2,1)}, u32[]{:S(2)}, u32[]{:S(2)}) collective-permute-start(bf16[64,4,64,8]{0,1,3,2:T(4,128)(2,1)} %fusion.1), channel_id=1, source_target_pairs={{16,0},{24,8},{32,16},{40,24},{48,32},{56,40},{64,48},{72,56},{80,... | collective-permute-start | bytes 786440 | tf_op jit(solution)/shard_map/ppermute | solution.py:13
  44.3 3.2 %collective-permute-start = (bf16[64,4,64,8]{0,1,3,2:T(4,128)(2,1)}, bf16[64,4,64,8]{0,1,3,2:T(4,128)(2,1)}, u32[]{:S(2)}, u32[]{:S(2)}) collective-permute-start(bf16[64,4,64,8]{0,1,3,2:T(4,128)(2,1)} %fusion.1), channel_id=1, source_target_pairs={{0,16},{8,24},{16,32},{24,40},{32,48},{40,56},{48,64},{56,72},{64,... | collective-permute-start | bytes 786440 | tf_op jit(solution)/shard_map/ppermute | solution.py:13
  47.5 1.7 %fusion.14 = f32[64,4,64,8]{2,0,3,1:T(8,128)S(1)} fusion(bf16[64,4,64,8]{0,1,3,2:T(4,128)(2,1)} %fusion.1, bf16[64,64,3]{1,0,2:T(8,128)(2,1)S(1)} %get-tuple-element.8), kind=kOutput, calls=%fused_computation.21 | convolution fusion | flops 16777216 | bytes 802816 | tf_op jit(solution)/shard_map/oi,isxy->osxy/dot_general | solution.py:31
  49.1 1.1 copy.61
  50.3 17.4 %collective-permute-done.1 = bf16[64,4,64,8]{0,1,3,2:T(4,128)(2,1)} collective-permute-done((bf16[64,4,64,8]{0,1,3,2:T(4,128)(2,1)}, bf16[64,4,64,8]{0,1,3,2:T(4,128)(2,1)}, u32[]{:S(2)}, u32[]{:S(2)}) %collective-permute-start.1) | collective-permute-done | bytes 262176 | tf_op jit(solution)/shard_map/ppermute | solution.py:13
  67.7 1.7 %fusion.10 = f32[64,4,64,8]{2,0,3,1:T(8,128)S(1)} fusion(bf16[64,4,64,8]{0,1,3,2:T(4,128)(2,1)} %collective-permute-done.1, bf16[64,64,3]{1,0,2:T(8,128)(2,1)S(1)} %get-tuple-element.8), kind=kOutput, calls=%fused_computation.17 | convolution fusion | flops 16777216 | bytes 802816 | tf_op jit(solution)/shard_map/oi,isxy->osxy/dot_general | solution.py:33
  69.3 1.1 copy.64
  70.5 1.7 %fusion.12 = f32[64,4,64,8]{2,0,3,1:T(8,128)S(1)} fusion(bf16[64,4,64,8]{0,1,3,2:T(4,128)(2,1)} %collective-permute-done, bf16[64,64,3]{1,0,2:T(8,128)(2,1)S(1)} %get-tuple-element.8), kind=kOutput, calls=%fused_computation.19 | convolution fusion | flops 16777216 | bytes 802816 | tf_op jit(solution)/shard_map/oi,isxy->osxy/dot_general | solution.py:32
  72.2 1.8 %copy.62 = f32[64,4,64,8]{0,1,3,2:T(4,128)} copy(f32[64,4,64,8]{2,0,3,1:T(8,128)S(1)} %fusion.12) | data formatting | bytes 1048576 | tf_op jit(solution)/shard_map/oi,isxy->osxy/dot_general | solution.py:32
  73.9 7.6 %fusion.3 = bf16[64,4,64,8]{0,1,3,2:T(4,128)(2,1)} fusion(f32[64,4,64,8]{0,1,3,2:T(4,128)S(1)} %copy.64, f32[64,4,64,8]{0,1,3,2:T(4,128)S(1)} %copy.61, f32[64,4,64,8]{0,1,3,2:T(4,128)} %copy.62, bf16[2,64,64,3,3]{2,1,4,3,0:T(8,128)(2,1)} %bitcast.106, bf16[2,64,64,3,3]{2,1,4,3,0:T(8,128)(2,1)S(1)} %bitcast.104), kind=kOutput, calls=%fused_computation.7 | convolution fusion | flops 274989056 | bytes 3702784 | tf_op jit(solution)/shard_map/conv_general_dilated | solution.py:17
  81.5 2.4 %collective-permute-start.3 = (bf16[64,4,64,8]{0,1,3,2:T(4,128)(2,1)}, bf16[64,4,64,8]{0,1,3,2:T(4,128)(2,1)}, u32[]{:S(2)}, u32[]{:S(2)}) collective-permute-start(bf16[64,4,64,8]{0,1,3,2:T(4,128)(2,1)} %fusion.3), channel_id=1, source_target_pairs={{16,0},{24,8},{32,16},{40,24},{48,32},{56,40},{64,48},{72,56},{80,... | collective-permute-start | bytes 786440 | tf_op jit(solution)/shard_map/ppermute | solution.py:13
  83.9 5.1 %collective-permute-start.2 = (bf16[64,4,64,8]{0,1,3,2:T(4,128)(2,1)}, bf16[64,4,64,8]{0,1,3,2:T(4,128)(2,1)}, u32[]{:S(2)}, u32[]{:S(2)}) collective-permute-start(bf16[64,4,64,8]{0,1,3,2:T(4,128)(2,1)} %fusion.3), channel_id=1, source_target_pairs={{0,16},{8,24},{16,32},{24,40},{32,48},{40,56},{48,64},{56,72},{64,... | collective-permute-start | bytes 786440 | tf_op jit(solution)/shard_map/ppermute | solution.py:13
  89.1 1.7 %fusion.8 = f32[64,4,64,8]{2,0,3,1:T(8,128)S(1)} fusion(bf16[64,4,64,8]{0,1,3,2:T(4,128)(2,1)} %fusion.3, bf16[64,64,3]{1,0,2:T(8,128)(2,1)S(1)} %get-tuple-element.7), kind=kOutput, calls=%fused_computation.15 | convolution fusion | flops 16777216 | bytes 802816 | tf_op jit(solution)/shard_map/oi,isxy->osxy/dot_general | solution.py:31
  90.7 1.1 copy.67
  91.9 17.4 %collective-permute-done.3 = bf16[64,4,64,8]{0,1,3,2:T(4,128)(2,1)} collective-permute-done((bf16[64,4,64,8]{0,1,3,2:T(4,128)(2,1)}, bf16[64,4,64,8]{0,1,3,2:T(4,128)(2,1)}, u32[]{:S(2)}, u32[]{:S(2)}) %collective-permute-start.3) | collective-permute-done | bytes 262176 | tf_op jit(solution)/shard_map/ppermute | solution.py:13
  109.2 1.7 %fusion.4 = f32[64,4,64,8]{2,0,3,1:T(8,128)S(1)} fusion(bf16[64,4,64,8]{0,1,3,2:T(4,128)(2,1)} %collective-permute-done.3, bf16[64,64,3]{1,0,2:T(8,128)(2,1)S(1)} %get-tuple-element.7), kind=kOutput, calls=%fused_computation.11 | convolution fusion | flops 16777216 | bytes 802816 | tf_op jit(solution)/shard_map/oi,isxy->osxy/dot_general | solution.py:33
  110.9 1.1 copy.70
  112.0 2.6 %fusion.6 = f32[64,4,64,8]{2,0,3,1:T(8,128)} fusion(bf16[64,4,64,8]{0,1,3,2:T(4,128)(2,1)} %collective-permute-done.2, bf16[64,64,3]{1,0,2:T(8,128)(2,1)S(1)} %get-tuple-element.7), kind=kOutput, calls=%fused_computation.13 | convolution fusion | flops 16777216 | bytes 802816 | tf_op jit(solution)/shard_map/oi,isxy->osxy/dot_general | solution.py:32
  114.7 2.3 %copy.68 = f32[64,4,64,8]{0,1,3,2:T(4,128)S(1)} copy(f32[64,4,64,8]{2,0,3,1:T(8,128)} %fusion.6) | data formatting | bytes 1048576 | tf_op jit(solution)/shard_map/oi,isxy->osxy/dot_general | solution.py:32
  117.0 1.5 %maximum_convert_fusion = bf16[64,4,64,8]{0,1,3,2:T(4,128)(2,1)} fusion(f32[64,4,64,8]{0,1,3,2:T(4,128)S(1)} %copy.70, f32[64,4,64,8]{0,1,3,2:T(4,128)S(1)} %copy.67, f32[64,4,64,8]{0,1,3,2:T(4,128)S(1)} %copy.68), kind=kLoop, calls=%fused_computation.8 | loop fusion | flops 524288 | bytes 1835008 | tf_op jit(solution)/shard_map/convert_element_type | solution.py:34
  118.6 1.4 %copy.71 = bf16[64,4,512]{2,1,0:T(4,128)(2,1)S(1)} copy(bf16[64,4,512]{0,1,2:T(4,128)(2,1)} %bitcast.97) | data formatting | bytes 524288 | tf_op jit(solution)/shard_map/reshape | solution.py:71
  120.0 9.7 %all_to_all.24 = bf16[64,4,512]{2,1,0:T(4,128)(2,1)S(1)} all-to-all(bf16[64,4,512]{2,1,0:T(4,128)(2,1)S(1)} %copy.71), channel_id=1, replica_groups=mesh['gz'=32,'ch'=8] {'ch'}, dimensions={0} | all-to-all | bytes 524288 | tf_op jit(solution)/shard_map/all_to_all | solution.py:72
  129.8 0.8 copy.74
  (17 shorter events, 0.7 us)
Async XLA Ops:
  21.2 12.4 %copy-start = (bf16[18,8,8,64]{3,2,1,0:T(8,128)(2,1)}, bf16[18,8,8,64]{3,2,1,0:T(8,128)(2,1)S(1)}, u32[]{:S(2)}) copy-start(bf16[18,8,8,64]{3,2,1,0:T(8,128)(2,1)S(1)} %get-tuple-element.6) | copy-start | bytes 442372
  39.9 27.8 %collective-permute-start.1 = (bf16[64,4,64,8]{0,1,3,2:T(4,128)(2,1)}, bf16[64,4,64,8]{0,1,3,2:T(4,128)(2,1)}, u32[]{:S(2)}, u32[]{:S(2)}) collective-permute-start(bf16[64,4,64,8]{0,1,3,2:T(4,128)(2,1)} %fusion.1), channel_id=1, source_target_pairs={{16,0},{24,8},{32,16},{40,24},{48,32},{56,40},{64,48},{72,56},{80,... | collective-permute-start | bytes 786440 | tf_op jit(solution)/shard_map/ppermute | solution.py:13
  44.3 26.2 %collective-permute-start = (bf16[64,4,64,8]{0,1,3,2:T(4,128)(2,1)}, bf16[64,4,64,8]{0,1,3,2:T(4,128)(2,1)}, u32[]{:S(2)}, u32[]{:S(2)}) collective-permute-start(bf16[64,4,64,8]{0,1,3,2:T(4,128)(2,1)} %fusion.1), channel_id=1, source_target_pairs={{0,16},{8,24},{16,32},{24,40},{32,48},{40,56},{48,64},{56,72},{64,... | collective-permute-start | bytes 786440 | tf_op jit(solution)/shard_map/ppermute | solution.py:13
  81.5 27.7 %collective-permute-start.3 = (bf16[64,4,64,8]{0,1,3,2:T(4,128)(2,1)}, bf16[64,4,64,8]{0,1,3,2:T(4,128)(2,1)}, u32[]{:S(2)}, u32[]{:S(2)}) collective-permute-start(bf16[64,4,64,8]{0,1,3,2:T(4,128)(2,1)} %fusion.3), channel_id=1, source_target_pairs={{16,0},{24,8},{32,16},{40,24},{48,32},{56,40},{64,48},{72,56},{80,... | collective-permute-start | bytes 786440 | tf_op jit(solution)/shard_map/ppermute | solution.py:13
  83.9 28.1 %collective-permute-start.2 = (bf16[64,4,64,8]{0,1,3,2:T(4,128)(2,1)}, bf16[64,4,64,8]{0,1,3,2:T(4,128)(2,1)}, u32[]{:S(2)}, u32[]{:S(2)}) collective-permute-start(bf16[64,4,64,8]{0,1,3,2:T(4,128)(2,1)} %fusion.3), channel_id=1, source_target_pairs={{0,16},{8,24},{16,32},{24,40},{32,48},{40,56},{48,64},{56,72},{64,... | collective-permute-start | bytes 786440 | tf_op jit(solution)/shard_map/ppermute | solution.py:13

commit v4 on v3

v4 whole, which is shorter than its diff:
```python
import functools

import jax
import jax.numpy as jnp
from jax import lax
from jax.experimental import pallas as pl
from jax.experimental.pallas import tpu as pltpu
from jax.sharding import PartitionSpec as P

X = 64
Y = 8


def from_behind(block, axis, distance):
    devices = range(lax.axis_size(axis))
    route = [(i - distance, i) for i in devices if i - distance in devices]
    return lax.ppermute(block, axis, route)


def pack_weights(plane_a, plane_b, depth):
    layers, out_part, chans = plane_a.shape[:3]
    taps_a = jnp.transpose(plane_a, (0, 3, 4, 1, 2)).reshape(-1, out_part, chans)
    taps_b = jnp.transpose(plane_b, (0, 3, 4, 1, 2)).reshape(-1, out_part, chans)
    taps_d = jnp.transpose(depth, (0, 3, 1, 2)).reshape(-1, out_part, chans)
    return jnp.concatenate([taps_a, taps_b, taps_d], axis=0)


def _plane(x, w_ref, base, ok):
    total = None
    width = x.shape[1]
    for a in range(3):
        for b in range(3):
            term = jnp.dot(w_ref[base + a * 3 + b], x, preferred_element_type=jnp.float32)
            d = (a - 1) * Y + (b - 1)
            if d != 0:
                term = pltpu.roll(term, (-d) % width, 1)
            mask = ok[a][b]
            if mask is not None:
                term = jnp.where(mask, term, 0.0)
            total = term if total is None else total + term
    return total


def _masks(width):
    p = lax.broadcasted_iota(jnp.int32, (1, width), 1)
    yy = p % Y
    xx = (p // Y) % X
    xm = [xx >= 1, None, xx <= X - 2]
    ym = [yy >= 1, None, yy <= Y - 2]
    ok = []
    for a in range(3):
        row = []
        for b in range(3):
            if xm[a] is None:
                row.append(ym[b])
            elif ym[b] is None:
                row.append(xm[a])
            else:
                row.append(jnp.logical_and(xm[a], ym[b]))
        ok.append(row)
    return ok


def _kernel(*refs, depth_base, plane_bases):
    if depth_base is None:
        x_ref, w_ref, o_ref = refs
        h = x_ref[...]
    else:
        lo_ref, mid_ref, up_ref, w_ref, o_ref = refs
        total = jnp.dot(w_ref[depth_base + 1], mid_ref[...], preferred_element_type=jnp.float32)
        total = total + jnp.dot(w_ref[depth_base], lo_ref[...], preferred_element_type=jnp.float32)
        total = total + jnp.dot(w_ref[depth_base + 2], up_ref[...], preferred_element_type=jnp.float32)
        h = jnp.maximum(total, 0.0).astype(jnp.bfloat16)
    if plane_bases:
        ok = _masks(h.shape[1])
        for base in plane_bases:
            h = jnp.maximum(_plane(h, w_ref, base, ok), 0.0).astype(jnp.bfloat16)
    o_ref[...] = h


def layer_kernel(inputs, w, depth_base=None, plane_bases=()):
    shape = inputs[0].shape
    return pl.pallas_call(
        functools.partial(_kernel, depth_base=depth_base, plane_bases=tuple(plane_bases)),
        out_shape=jax.ShapeDtypeStruct(shape, jnp.bfloat16),
    )(*inputs, w)


def local(volume, plane_a, plane_b, depth):
    layers, out_part, chans = plane_a.shape[:3]
    part, slab, flat = volume.shape
    parts = lax.axis_size("ch")
    slices = slab // parts
    weights = pack_weights(plane_a, plane_b, depth)
    taps = weights.shape[0]
    sent_volume = jnp.transpose(volume.reshape(part, parts, slices, flat), (1, 0, 2, 3))
    sent_volume = sent_volume.reshape(parts, part * slices, flat)
    sent_weights = jnp.broadcast_to(
        weights.reshape(1, -1, flat), (parts, taps * out_part * chans // flat, flat)
    )
    sent = jnp.concatenate([sent_volume, sent_weights], axis=1)
    got = lax.all_to_all(sent, "ch", split_axis=0, concat_axis=0, tiled=True)
    got = got.reshape(parts, -1, flat)
    h = got[:, : part * slices].reshape(parts * part, slices * flat)
    w = got[:, part * slices :].reshape(parts, taps, out_part, chans)
    w = jnp.transpose(w, (1, 0, 2, 3)).reshape(taps, parts * out_part, chans)
    nine = 9 * layers

    def bases(layer_index):
        return (layer_index * 9, nine + layer_index * 9)

    second = layer_kernel([h], w, None, bases(0))
    for layer_index in range(layers):
        lower = from_behind(second, "gz", 2)
        upper = from_behind(second, "gz", -2)
        following = bases(layer_index + 1) if layer_index + 1 < layers else ()
        second = layer_kernel(
            [lower, second, upper], w, 2 * nine + layer_index * 3, following
        )
    h = second.reshape(parts * part, slices, flat)
    return lax.all_to_all(h, "ch", split_axis=0, concat_axis=1, tiled=True)


def solution(mesh):
    return jax.shard_map(
        local,
        mesh=mesh,
        in_specs=(
            P("ch", "gz", None),
            P(None, "ch", None, None, None),
            P(None, "ch", None, None, None),
            P(None, "ch", None, None),
        ),
        out_specs=P("ch", "gz", None),
        check_vma=False,
    )
```

time: 131 us -> 87.3 us (0.67)
  matrix products: 24.8 us -> 0 us
  local copies, waits for them, and re-layouts: 27.7 us -> 9.44 us
  Pallas kernels: 0 us -> 13 us
  waiting for transfers between devices: 34.8 us -> 21.9 us
  other arithmetic: 1.6 us -> 0.08 us
    conv_general_dilated x2 -> x0, matrix products: 13.8 us -> none  [plane_conv(): lax.conv_general_dilated(h, weight, (1, 1), ((1, 1), (1, 1)), dimension_n...]
    pallas_call x0 -> x3, Pallas kernels: none -> 13 us  [layer_kernel(): pl.pallas_call(functools.partial(_kernel, depth_base=depth_base, plane_ba...]
    ppermute x4, waiting for transfers between devices: 34.8 us -> 21.9 us  [from_behind(): return lax.ppermute(block, axis, route)]
    dot_general x6 -> x0, matrix products: 11 us -> none  [the longest x2 4.32 us: depth_conv(): jnp.einsum('oi,isxy->osxy', weight[:, :, 0], lower, preferred_element_typ...]
    reshape x3, local copies, waits for them, and re-layouts: 13.8 us -> 3.02 us  [the longest x1 1.13 us: local(): h = second.reshape(parts * part, slices, flat)]
    dot_general x6 -> x0, local copies, waits for them, and re-layouts: 8.57 us -> none  [the longest x2 4.1 us: depth_conv(): jnp.einsum('oi,isxy->osxy', weight[:, :, 0], lower, preferred_element_typ...]
    convert_element_type x1 -> x0, other arithmetic: 1.52 us -> none  [depth_conv(): return jnp.maximum(total, 0.0).astype(jnp.bfloat16)]
  transfers between devices with their start and end apart: 4 -> 4, of which waited for: 2 -> 4; matrix products, arithmetic and copies ran while one was open for 9% -> 0% of each run, Pallas kernels for 0% -> 0%
where the time goes in v4:
time: 87.3 us; the launch traced here: 86.1 us
  blocking collectives  26.6 us (30%)
  waiting for transfers between devices  21.9 us (25%)
  starting transfers between devices  15 us (17%)
  Pallas kernels  13 us (15%)
  local copies, waits for them, and re-layouts  9.44 us (11%)
    ppermute x4, waiting for transfers between devices, from_behind(): return lax.ppermute(block, axis, route)  21.9 us
    all_to_all x1, blocking collectives, local(): got = lax.all_to_all(sent, 'ch', split_axis=0, concat_axis=0, tiled=True)  16.6 us
    ppermute x4, starting transfers between devices, from_behind(): return lax.ppermute(block, axis, route)  15 us
    pallas_call x3, Pallas kernels, layer_kernel(): pl.pallas_call(functools.partial(_kernel, depth_base=depth_base, plane_ba...  13 us
    all_to_all x1, blocking collectives, local(): return lax.all_to_all(h, 'ch', split_axis=0, concat_axis=1, tiled=True)  9.96 us
    concatenate x3, local copies, waits for them, and re-layouts, pack_weights(): return jnp.concatenate([taps_a, taps_b, taps_d], axis=0)  2.52 us
  transfers between devices with their start and end apart: 4, of which 4 were waited for; matrix products, arithmetic and copies ran while one was open for 0% of the time, Pallas kernels for 0%

profile of v4, /device:TPU:96, one launch (start us, length us, event | category | flops | bytes accessed | tf_op | source)
XLA Modules:
  0.0 86.1 jit_solution(7424090902358806650)
XLA Ops:
  0.0 0.8 concatenate.15
  0.8 0.9 %concatenate.13 = bf16[1,18,512]{2,1,0:T(8,128)(2,1)S(1)} reshape(bf16[2,3,3,8,64]{4,3,2,1,0:T(8,128)(2,1)} %bitcast.27) | data formatting | bytes 36864 | tf_op jit(solution)/shard_map/concatenate | solution.py:25
  1.7 0.9 %concatenate.14 = bf16[1,18,512]{2,1,0:T(8,128)(2,1)S(1)} reshape(bf16[2,3,3,8,64]{4,3,2,1,0:T(8,128)(2,1)} %bitcast.28) | data formatting | bytes 36864 | tf_op jit(solution)/shard_map/concatenate | solution.py:25
  2.5 1.0 %reshape.28 = bf16[8,8,4,512]{3,2,1,0:T(4,128)(2,1)S(1)} reshape(bf16[8,32,512]{2,1,0:T(8,128)(2,1)} %param.4) | data formatting | bytes 524288 | tf_op jit(solution)/shard_map/reshape | solution.py:96
  3.5 0.1 copy.5
  3.6 0.1 reshape.29
  3.8 0.1 pad_maximum_fusion
  3.9 16.6 %all_to_all.23 = bf16[8,74,512]{2,1,0:T(8,128)(2,1)S(1)} all-to-all(bf16[8,74,512]{2,1,0:T(8,128)(2,1)S(1)} %pad_maximum_fusion), channel_id=1, replica_groups=mesh['gz'=32,'ch'=8] {'ch'}, dimensions={0} | all-to-all | bytes 1212416 | tf_op jit(solution)/shard_map/all_to_all | solution.py:102
  20.5 0.2 copy.6
  20.7 0.9 %reshape.30.refs_0_ = bf16[64,2048]{1,0:T(8,128)(2,1)} reshape(bf16[8,32,512]{2,1,0:T(8,128)(2,1)S(1)} %slice.8) | data formatting | bytes 524288 | tf_op jit(solution)/shard_map/reshape | solution.py:104
  21.6 1.2 %reshape.31 = bf16[8,42,8,64]{3,2,0,1:T(8,128)(2,1)} reshape(bf16[8,42,512]{2,0,1:T(8,128)(2,1)S(1)} %copy.6) | data formatting | bytes 688128 | tf_op jit(solution)/shard_map/reshape | solution.py:105
  22.8 5.1 %shard_map.46.refs_1_ = bf16[64,2048]{1,0:T(8,128)(2,1)} custom-call(bf16[64,2048]{1,0:T(8,128)(2,1)} %reshape.30.refs_0_, bf16[42,64,64]{2,1,0:T(8,128)(2,1)} %bitcast.21), custom_call_target="tpu_custom_call" | custom-call | tf_op jit(solution)/shard_map/pallas_call | solution.py:83
  27.9 4.4 %collective-permute-start.1 = (bf16[64,2048]{1,0:T(8,128)(2,1)}, bf16[64,2048]{1,0:T(8,128)(2,1)S(1)}, u32[]{:S(2)}, u32[]{:S(2)}) collective-permute-start(bf16[64,2048]{1,0:T(8,128)(2,1)} %shard_map.46.refs_1_), channel_id=1, source_target_pairs={{16,0},{24,8},{32,16},{40,24},{48,32},{56,40},{64,48},{72,56},{80,... | collective-permute-start | bytes 786440 | tf_op jit(solution)/shard_map/ppermute | solution.py:17
  32.3 3.0 %collective-permute-start = (bf16[64,2048]{1,0:T(8,128)(2,1)}, bf16[64,2048]{1,0:T(8,128)(2,1)S(1)}, u32[]{:S(2)}, u32[]{:S(2)}) collective-permute-start(bf16[64,2048]{1,0:T(8,128)(2,1)} %shard_map.46.refs_1_), channel_id=1, source_target_pairs={{0,16},{8,24},{16,32},{24,40},{32,48},{40,56},{48,64},{56,72},{64,... | collective-permute-start | bytes 786440 | tf_op jit(solution)/shard_map/ppermute | solution.py:17
  35.3 9.1 %collective-permute-done.1.refs_2_ = bf16[64,2048]{1,0:T(8,128)(2,1)S(1)} collective-permute-done((bf16[64,2048]{1,0:T(8,128)(2,1)}, bf16[64,2048]{1,0:T(8,128)(2,1)S(1)}, u32[]{:S(2)}, u32[]{:S(2)}) %collective-permute-start.1) | collective-permute-done | bytes 262176 | tf_op jit(solution)/shard_map/ppermute | solution.py:17
  44.3 0.0 copy-start.1
  44.3 1.1 %collective-permute-done.refs_0_ = bf16[64,2048]{1,0:T(8,128)(2,1)S(1)} collective-permute-done((bf16[64,2048]{1,0:T(8,128)(2,1)}, bf16[64,2048]{1,0:T(8,128)(2,1)S(1)}, u32[]{:S(2)}, u32[]{:S(2)}) %collective-permute-start) | collective-permute-done | bytes 262176 | tf_op jit(solution)/shard_map/ppermute | solution.py:17
  45.5 0.0 copy-done.1
  45.5 0.0 copy-start.3
  45.5 0.7 copy-done.3
  46.2 5.4 %shard_map.47.refs_1_ = bf16[64,2048]{1,0:T(8,128)(2,1)} custom-call(bf16[64,2048]{1,0:T(8,128)(2,1)} %copy-done.3, bf16[64,2048]{1,0:T(8,128)(2,1)} %shard_map.46.refs_1_, bf16[64,2048]{1,0:T(8,128)(2,1)} %copy-done.1, bf16[42,64,64]{2,1,0:T(8,128)(2,1)} %bitcast.22), custom_call_target="tpu_custom_call" | custom-call | tf_op jit(solution)/shard_map/pallas_call | solution.py:83
  51.6 4.1 %collective-permute-start.3 = (bf16[64,2048]{1,0:T(8,128)(2,1)}, bf16[64,2048]{1,0:T(8,128)(2,1)S(1)}, u32[]{:S(2)}, u32[]{:S(2)}) collective-permute-start(bf16[64,2048]{1,0:T(8,128)(2,1)} %shard_map.47.refs_1_), channel_id=1, source_target_pairs={{16,0},{24,8},{32,16},{40,24},{48,32},{56,40},{64,48},{72,56},{80,... | collective-permute-start | bytes 786440 | tf_op jit(solution)/shard_map/ppermute | solution.py:17
  55.7 3.6 %collective-permute-start.2 = (bf16[64,2048]{1,0:T(8,128)(2,1)}, bf16[64,2048]{1,0:T(8,128)(2,1)S(1)}, u32[]{:S(2)}, u32[]{:S(2)}) collective-permute-start(bf16[64,2048]{1,0:T(8,128)(2,1)} %shard_map.47.refs_1_), channel_id=1, source_target_pairs={{0,16},{8,24},{16,32},{24,40},{32,48},{40,56},{48,64},{56,72},{64,... | collective-permute-start | bytes 786440 | tf_op jit(solution)/shard_map/ppermute | solution.py:17
  59.3 10.4 %collective-permute-done.3.refs_2_ = bf16[64,2048]{1,0:T(8,128)(2,1)S(1)} collective-permute-done((bf16[64,2048]{1,0:T(8,128)(2,1)}, bf16[64,2048]{1,0:T(8,128)(2,1)S(1)}, u32[]{:S(2)}, u32[]{:S(2)}) %collective-permute-start.3) | collective-permute-done | bytes 262176 | tf_op jit(solution)/shard_map/ppermute | solution.py:17
  69.7 1.3 %collective-permute-done.2.refs_0_ = bf16[64,2048]{1,0:T(8,128)(2,1)S(1)} collective-permute-done((bf16[64,2048]{1,0:T(8,128)(2,1)}, bf16[64,2048]{1,0:T(8,128)(2,1)S(1)}, u32[]{:S(2)}, u32[]{:S(2)}) %collective-permute-start.2) | collective-permute-done | bytes 262176 | tf_op jit(solution)/shard_map/ppermute | solution.py:17
  71.0 0.0 copy-done
  71.0 0.7 copy-done.2
  71.7 2.4 %shard_map.48 = bf16[64,2048]{1,0:T(8,128)(2,1)} custom-call(bf16[64,2048]{1,0:T(8,128)(2,1)} %copy-done.2, bf16[64,2048]{1,0:T(8,128)(2,1)} %shard_map.47.refs_1_, bf16[64,2048]{1,0:T(8,128)(2,1)} %copy-done, bf16[42,64,64]{2,1,0:T(8,128)(2,1)} %bitcast.23), custom_call_target="tpu_custom_call" | custom-call | tf_op jit(solution)/shard_map/pallas_call | solution.py:83
  74.1 1.1 %reshape.33 = bf16[64,4,512]{2,1,0:T(4,128)(2,1)S(1)} reshape(bf16[64,2048]{1,0:T(8,128)(2,1)} %shard_map.48) | data formatting | bytes 524288 | tf_op jit(solution)/shard_map/reshape | solution.py:120
  75.2 10.0 %all_to_all.24 = bf16[64,4,512]{2,1,0:T(4,128)(2,1)S(1)} all-to-all(bf16[64,4,512]{2,1,0:T(4,128)(2,1)S(1)} %reshape.33), channel_id=1, replica_groups=mesh['gz'=32,'ch'=8] {'ch'}, dimensions={0} | all-to-all | bytes 524288 | tf_op jit(solution)/shard_map/all_to_all | solution.py:121
  85.2 0.1 copy.9
  85.3 0.8 all_to_all.20
  (6 shorter events, 0.1 us)
Async XLA Ops:
  27.9 16.4 %collective-permute-start.1 = (bf16[64,2048]{1,0:T(8,128)(2,1)}, bf16[64,2048]{1,0:T(8,128)(2,1)S(1)}, u32[]{:S(2)}, u32[]{:S(2)}) collective-permute-start(bf16[64,2048]{1,0:T(8,128)(2,1)} %shard_map.46.refs_1_), channel_id=1, source_target_pairs={{16,0},{24,8},{32,16},{40,24},{48,32},{56,40},{64,48},{72,56},{80,... | collective-permute-start | bytes 786440 | tf_op jit(solution)/shard_map/ppermute | solution.py:17
  32.3 13.2 %collective-permute-start = (bf16[64,2048]{1,0:T(8,128)(2,1)}, bf16[64,2048]{1,0:T(8,128)(2,1)S(1)}, u32[]{:S(2)}, u32[]{:S(2)}) collective-permute-start(bf16[64,2048]{1,0:T(8,128)(2,1)} %shard_map.46.refs_1_), channel_id=1, source_target_pairs={{0,16},{8,24},{16,32},{24,40},{32,48},{40,56},{48,64},{56,72},{64,... | collective-permute-start | bytes 786440 | tf_op jit(solution)/shard_map/ppermute | solution.py:17
  44.3 1.1 %copy-start.1 = (bf16[64,2048]{1,0:T(8,128)(2,1)}, bf16[64,2048]{1,0:T(8,128)(2,1)S(1)}, u32[]{:S(2)}) copy-start(bf16[64,2048]{1,0:T(8,128)(2,1)S(1)} %collective-permute-done.1.refs_2_) | copy-start | bytes 786436
  45.5 0.7 copy-start.3
  51.6 18.1 %collective-permute-start.3 = (bf16[64,2048]{1,0:T(8,128)(2,1)}, bf16[64,2048]{1,0:T(8,128)(2,1)S(1)}, u32[]{:S(2)}, u32[]{:S(2)}) collective-permute-start(bf16[64,2048]{1,0:T(8,128)(2,1)} %shard_map.47.refs_1_), channel_id=1, source_target_pairs={{16,0},{24,8},{32,16},{40,24},{48,32},{56,40},{64,48},{72,56},{80,... | collective-permute-start | bytes 786440 | tf_op jit(solution)/shard_map/ppermute | solution.py:17
  55.7 15.3 %collective-permute-start.2 = (bf16[64,2048]{1,0:T(8,128)(2,1)}, bf16[64,2048]{1,0:T(8,128)(2,1)S(1)}, u32[]{:S(2)}, u32[]{:S(2)}) collective-permute-start(bf16[64,2048]{1,0:T(8,128)(2,1)} %shard_map.47.refs_1_), channel_id=1, source_target_pairs={{0,16},{8,24},{16,32},{24,40},{32,48},{40,56},{48,64},{56,72},{64,... | collective-permute-start | bytes 786440 | tf_op jit(solution)/shard_map/ppermute | solution.py:17
  69.7 1.3 %copy-start = (bf16[64,2048]{1,0:T(8,128)(2,1)}, bf16[64,2048]{1,0:T(8,128)(2,1)S(1)}, u32[]{:S(2)}) copy-start(bf16[64,2048]{1,0:T(8,128)(2,1)S(1)} %collective-permute-done.3.refs_2_) | copy-start | bytes 786436
  71.0 0.7 copy-start.2

commit v5 on v4

--- a/solution.py
+++ b/solution.py
@@ -11,10 +11,22 @@
 Y = 8
 
 
-def from_behind(block, axis, distance):
-    devices = range(lax.axis_size(axis))
-    route = [(i - distance, i) for i in devices if i - distance in devices]
-    return lax.ppermute(block, axis, route)
+def from_behind(block, distance, swap):
+    slabs, parts = lax.axis_size("gz"), lax.axis_size("ch")
+    route = [
+        ((g - distance) * parts + (c ^ swap), g * parts + c)
+        for g in range(slabs)
+        if 0 <= g - distance < slabs
+        for c in range(parts)
+    ]
+    return lax.ppermute(block, ("gz", "ch"), route)
+
+
+def swap_halves(block, axis, flag):
+    shape = block.shape
+    halves = block.reshape(shape[:axis] + (2, shape[axis] // 2) + shape[axis + 1 :])
+    swapped = jnp.flip(halves, axis)
+    return jnp.where(flag, swapped, halves).reshape(shape)
 
 
 def pack_weights(plane_a, plane_b, depth):
@@ -93,7 +105,10 @@
     slices = slab // parts
     weights = pack_weights(plane_a, plane_b, depth)
     taps = weights.shape[0]
-    sent_volume = jnp.transpose(volume.reshape(part, parts, slices, flat), (1, 0, 2, 3))
+    half = parts // 2
+    flipped = (lax.axis_index("gz") // 2) % 2 == 1
+    chunks = swap_halves(volume.reshape(part, parts, slices, flat), 1, flipped)
+    sent_volume = jnp.transpose(chunks, (1, 0, 2, 3))
     sent_volume = sent_volume.reshape(parts, part * slices, flat)
     sent_weights = jnp.broadcast_to(
         weights.reshape(1, -1, flat), (parts, taps * out_part * chans // flat, flat)
@@ -111,14 +126,16 @@
 
     second = layer_kernel([h], w, None, bases(0))
     for layer_index in range(layers):
-        lower = from_behind(second, "gz", 2)
-        upper = from_behind(second, "gz", -2)
+        lower = from_behind(second, 2, half)
+        upper = from_behind(second, -2, half)
         following = bases(layer_index + 1) if layer_index + 1 < layers else ()
         second = layer_kernel(
             [lower, second, upper], w, 2 * nine + layer_index * 3, following
         )
     h = second.reshape(parts * part, slices, flat)
-    return lax.all_to_all(h, "ch", split_axis=0, concat_axis=1, tiled=True)
+    h = lax.all_to_all(h, "ch", split_axis=0, concat_axis=1, tiled=True)
+    h = swap_halves(h.reshape(part, parts, slices, flat), 1, flipped)
+    return h.reshape(part, slab, flat)
 
 
 def solution(mesh):

time: 87.3 us -> 86.6 us (level)
    another operation x0 -> x2, local copies, waits for them, and re-layouts: none -> 1.79 us  [the longest x1 1.02 us: swap_halves(): block.reshape(shape[:axis] + (2, shape[axis] // 2) + shape[axis + 1:])]
    reshape x1, local copies, waits for them, and re-layouts: 1.02 us -> 0.09 us  [swap_halves(): return jnp.where(flag, swapped, halves).reshape(shape)]
where the time goes in v5:
time: 86.6 us; the launch traced here: 85.1 us
  blocking collectives  26.6 us (31%)
  waiting for transfers between devices  21.3 us (25%)
  starting transfers between devices  14.2 us (16%)
  Pallas kernels  13 us (15%)
  local copies, waits for them, and re-layouts  9.64 us (11%)
    ppermute x4, waiting for transfers between devices, from_behind(): return lax.ppermute(block, ('gz', 'ch'), route)  21.3 us
    all_to_all x1, blocking collectives, local(): got = lax.all_to_all(sent, 'ch', split_axis=0, concat_axis=0, tiled=True)  16.6 us
    ppermute x4, starting transfers between devices, from_behind(): return lax.ppermute(block, ('gz', 'ch'), route)  14.2 us
    pallas_call x3, Pallas kernels, layer_kernel(): pl.pallas_call(functools.partial(_kernel, depth_base=depth_base, plane_ba...  13 us
    all_to_all x1, blocking collectives, local(): h = lax.all_to_all(h, 'ch', split_axis=0, concat_axis=1, tiled=True)  9.97 us
    concatenate x3, local copies, waits for them, and re-layouts, pack_weights(): return jnp.concatenate([taps_a, taps_b, taps_d], axis=0)  2.52 us
  transfers between devices with their start and end apart: 4, of which 4 were waited for; matrix products, arithmetic and copies ran while one was open for 0% of the time, Pallas kernels for 0%

profile of v5, /device:TPU:96, one launch (start us, length us, event | category | flops | bytes accessed | tf_op | source)
XLA Modules:
  0.0 85.1 jit_solution(9773170211482006147)
XLA Ops:
  0.0 0.8 concatenate.15
  0.8 0.9 %concatenate.13 = bf16[1,18,512]{2,1,0:T(8,128)(2,1)S(1)} reshape(bf16[2,3,3,8,64]{4,3,2,1,0:T(8,128)(2,1)} %bitcast.31) | data formatting | bytes 36864 | tf_op jit(solution)/shard_map/concatenate | solution.py:37
  1.7 0.9 %concatenate.14 = bf16[1,18,512]{2,1,0:T(8,128)(2,1)S(1)} reshape(bf16[2,3,3,8,64]{4,3,2,1,0:T(8,128)(2,1)} %bitcast.32) | data formatting | bytes 36864 | tf_op jit(solution)/shard_map/concatenate | solution.py:37
  2.5 1.0 %reshape_reshape.9 = bf16[8,2,4,4,512]{4,3,2,1,0:T(4,128)(2,1)S(1)} reshape(bf16[8,32,512]{2,1,0:T(8,128)(2,1)} %param.4) | data formatting | bytes 524288 | tf_op jit(solution)/shard_map/reshape;reshape | solution.py:27
  3.5 0.1 reverse_select_fusion.1
  3.7 0.1 copy.9
  3.8 0.1 reshape.30
  3.9 0.1 pad_maximum_fusion
  4.0 16.6 %all_to_all.20 = bf16[8,74,512]{2,1,0:T(8,128)(2,1)S(1)} all-to-all(bf16[8,74,512]{2,1,0:T(8,128)(2,1)S(1)} %pad_maximum_fusion), channel_id=1, replica_groups=mesh['gz'=32,'ch'=8] {'ch'}, dimensions={0} | all-to-all | bytes 1212416 | tf_op jit(solution)/shard_map/all_to_all | solution.py:117
  20.6 0.2 copy.6
  20.9 0.9 %reshape.31.refs_0_ = bf16[64,2048]{1,0:T(8,128)(2,1)} reshape(bf16[8,32,512]{2,1,0:T(8,128)(2,1)S(1)} %slice.8) | data formatting | bytes 524288 | tf_op jit(solution)/shard_map/reshape | solution.py:119
  21.7 1.2 %reshape.32 = bf16[8,42,8,64]{3,2,0,1:T(8,128)(2,1)} reshape(bf16[8,42,512]{2,0,1:T(8,128)(2,1)S(1)} %copy.6) | data formatting | bytes 688128 | tf_op jit(solution)/shard_map/reshape | solution.py:120
  22.9 5.2 %shard_map.46.refs_1_ = bf16[64,2048]{1,0:T(8,128)(2,1)} custom-call(bf16[64,2048]{1,0:T(8,128)(2,1)} %reshape.31.refs_0_, bf16[42,64,64]{2,1,0:T(8,128)(2,1)} %bitcast.24), custom_call_target="tpu_custom_call" | custom-call | tf_op jit(solution)/shard_map/pallas_call | solution.py:95
  28.1 3.4 %collective-permute-start.1 = (bf16[64,2048]{1,0:T(8,128)(2,1)}, bf16[64,2048]{1,0:T(8,128)(2,1)S(1)}, u32[]{:S(2)}, u32[]{:S(2)}) collective-permute-start(bf16[64,2048]{1,0:T(8,128)(2,1)} %shard_map.46.refs_1_), channel_id=1, source_target_pairs={{20,0},{21,1},{22,2},{23,3},{16,4},{17,5},{18,6},{19,7},{28,8},{29... | collective-permute-start | bytes 786440 | tf_op jit(solution)/shard_map/ppermute | solution.py:22
  31.5 3.6 %collective-permute-start = (bf16[64,2048]{1,0:T(8,128)(2,1)}, bf16[64,2048]{1,0:T(8,128)(2,1)S(1)}, u32[]{:S(2)}, u32[]{:S(2)}) collective-permute-start(bf16[64,2048]{1,0:T(8,128)(2,1)} %shard_map.46.refs_1_), channel_id=1, source_target_pairs={{4,16},{5,17},{6,18},{7,19},{0,20},{1,21},{2,22},{3,23},{12,24},{1... | collective-permute-start | bytes 786440 | tf_op jit(solution)/shard_map/ppermute | solution.py:22
  35.1 9.1 %collective-permute-done.1.refs_2_ = bf16[64,2048]{1,0:T(8,128)(2,1)S(1)} collective-permute-done((bf16[64,2048]{1,0:T(8,128)(2,1)}, bf16[64,2048]{1,0:T(8,128)(2,1)S(1)}, u32[]{:S(2)}, u32[]{:S(2)}) %collective-permute-start.1) | collective-permute-done | bytes 262176 | tf_op jit(solution)/shard_map/ppermute | solution.py:22
  44.2 0.5 collective-permute-done.refs_0_
  44.7 0.2 copy-done.1
  44.9 0.7 copy-done.3
  45.6 5.4 %shard_map.47.refs_1_ = bf16[64,2048]{1,0:T(8,128)(2,1)} custom-call(bf16[64,2048]{1,0:T(8,128)(2,1)} %copy-done.3, bf16[64,2048]{1,0:T(8,128)(2,1)} %shard_map.46.refs_1_, bf16[64,2048]{1,0:T(8,128)(2,1)} %copy-done.1, bf16[42,64,64]{2,1,0:T(8,128)(2,1)} %bitcast.25), custom_call_target="tpu_custom_call" | custom-call | tf_op jit(solution)/shard_map/pallas_call | solution.py:95
  51.0 3.6 %collective-permute-start.3 = (bf16[64,2048]{1,0:T(8,128)(2,1)}, bf16[64,2048]{1,0:T(8,128)(2,1)S(1)}, u32[]{:S(2)}, u32[]{:S(2)}) collective-permute-start(bf16[64,2048]{1,0:T(8,128)(2,1)} %shard_map.47.refs_1_), channel_id=1, source_target_pairs={{20,0},{21,1},{22,2},{23,3},{16,4},{17,5},{18,6},{19,7},{28,8},{29... | collective-permute-start | bytes 786440 | tf_op jit(solution)/shard_map/ppermute | solution.py:22
  54.7 3.6 %collective-permute-start.2 = (bf16[64,2048]{1,0:T(8,128)(2,1)}, bf16[64,2048]{1,0:T(8,128)(2,1)S(1)}, u32[]{:S(2)}, u32[]{:S(2)}) collective-permute-start(bf16[64,2048]{1,0:T(8,128)(2,1)} %shard_map.47.refs_1_), channel_id=1, source_target_pairs={{4,16},{5,17},{6,18},{7,19},{0,20},{1,21},{2,22},{3,23},{12,24},{1... | collective-permute-start | bytes 786440 | tf_op jit(solution)/shard_map/ppermute | solution.py:22
  58.3 10.4 %collective-permute-done.3.refs_2_ = bf16[64,2048]{1,0:T(8,128)(2,1)S(1)} collective-permute-done((bf16[64,2048]{1,0:T(8,128)(2,1)}, bf16[64,2048]{1,0:T(8,128)(2,1)S(1)}, u32[]{:S(2)}, u32[]{:S(2)}) %collective-permute-start.3) | collective-permute-done | bytes 262176 | tf_op jit(solution)/shard_map/ppermute | solution.py:22
  68.6 1.3 %collective-permute-done.2.refs_0_ = bf16[64,2048]{1,0:T(8,128)(2,1)S(1)} collective-permute-done((bf16[64,2048]{1,0:T(8,128)(2,1)}, bf16[64,2048]{1,0:T(8,128)(2,1)S(1)}, u32[]{:S(2)}, u32[]{:S(2)}) %collective-permute-start.2) | collective-permute-done | bytes 262176 | tf_op jit(solution)/shard_map/ppermute | solution.py:22
  69.9 0.0 copy-done
  69.9 0.7 copy-done.2
  70.6 2.4 %shard_map.48 = bf16[64,2048]{1,0:T(8,128)(2,1)} custom-call(bf16[64,2048]{1,0:T(8,128)(2,1)} %copy-done.2, bf16[64,2048]{1,0:T(8,128)(2,1)} %shard_map.47.refs_1_, bf16[64,2048]{1,0:T(8,128)(2,1)} %copy-done, bf16[42,64,64]{2,1,0:T(8,128)(2,1)} %bitcast.26), custom_call_target="tpu_custom_call" | custom-call | tf_op jit(solution)/shard_map/pallas_call | solution.py:95
  73.0 1.1 %reshape.34 = bf16[64,4,512]{2,1,0:T(4,128)(2,1)S(1)} reshape(bf16[64,2048]{1,0:T(8,128)(2,1)} %shard_map.48) | data formatting | bytes 524288 | tf_op jit(solution)/shard_map/reshape | solution.py:135
  74.2 10.0 %all_to_all.21 = bf16[64,4,512]{2,1,0:T(4,128)(2,1)S(1)} all-to-all(bf16[64,4,512]{2,1,0:T(4,128)(2,1)S(1)} %reshape.34), channel_id=1, replica_groups=mesh['gz'=32,'ch'=8] {'ch'}, dimensions={0} | all-to-all | bytes 524288 | tf_op jit(solution)/shard_map/all_to_all | solution.py:136
  84.1 0.1 copy.7
  84.2 0.1 reverse_select_fusion
  84.4 0.8 reshape_reshape.11
  (8 shorter events, 0.1 us)
Async XLA Ops:
  28.1 16.1 %collective-permute-start.1 = (bf16[64,2048]{1,0:T(8,128)(2,1)}, bf16[64,2048]{1,0:T(8,128)(2,1)S(1)}, u32[]{:S(2)}, u32[]{:S(2)}) collective-permute-start(bf16[64,2048]{1,0:T(8,128)(2,1)} %shard_map.46.refs_1_), channel_id=1, source_target_pairs={{20,0},{21,1},{22,2},{23,3},{16,4},{17,5},{18,6},{19,7},{28,8},{29... | collective-permute-start | bytes 786440 | tf_op jit(solution)/shard_map/ppermute | solution.py:22
  31.5 13.2 %collective-permute-start = (bf16[64,2048]{1,0:T(8,128)(2,1)}, bf16[64,2048]{1,0:T(8,128)(2,1)S(1)}, u32[]{:S(2)}, u32[]{:S(2)}) collective-permute-start(bf16[64,2048]{1,0:T(8,128)(2,1)} %shard_map.46.refs_1_), channel_id=1, source_target_pairs={{4,16},{5,17},{6,18},{7,19},{0,20},{1,21},{2,22},{3,23},{12,24},{1... | collective-permute-start | bytes 786440 | tf_op jit(solution)/shard_map/ppermute | solution.py:22
  44.2 0.7 copy-start.1
  44.9 0.7 copy-start.3
  51.0 17.6 %collective-permute-start.3 = (bf16[64,2048]{1,0:T(8,128)(2,1)}, bf16[64,2048]{1,0:T(8,128)(2,1)S(1)}, u32[]{:S(2)}, u32[]{:S(2)}) collective-permute-start(bf16[64,2048]{1,0:T(8,128)(2,1)} %shard_map.47.refs_1_), channel_id=1, source_target_pairs={{20,0},{21,1},{22,2},{23,3},{16,4},{17,5},{18,6},{19,7},{28,8},{29... | collective-permute-start | bytes 786440 | tf_op jit(solution)/shard_map/ppermute | solution.py:22
  54.7 15.3 %collective-permute-start.2 = (bf16[64,2048]{1,0:T(8,128)(2,1)}, bf16[64,2048]{1,0:T(8,128)(2,1)S(1)}, u32[]{:S(2)}, u32[]{:S(2)}) collective-permute-start(bf16[64,2048]{1,0:T(8,128)(2,1)} %shard_map.47.refs_1_), channel_id=1, source_target_pairs={{4,16},{5,17},{6,18},{7,19},{0,20},{1,21},{2,22},{3,23},{12,24},{1... | collective-permute-start | bytes 786440 | tf_op jit(solution)/shard_map/ppermute | solution.py:22
  68.6 1.3 %copy-start = (bf16[64,2048]{1,0:T(8,128)(2,1)}, bf16[64,2048]{1,0:T(8,128)(2,1)S(1)}, u32[]{:S(2)}) copy-start(bf16[64,2048]{1,0:T(8,128)(2,1)S(1)} %collective-permute-done.3.refs_2_) | copy-start | bytes 786436
  69.9 0.7 copy-start.2

commit v6 on v5

--- a/solution.py
+++ b/solution.py
@@ -37,22 +37,6 @@
     return jnp.concatenate([taps_a, taps_b, taps_d], axis=0)
 
 
-def _plane(x, w_ref, base, ok):
-    total = None
-    width = x.shape[1]
-    for a in range(3):
-        for b in range(3):
-            term = jnp.dot(w_ref[base + a * 3 + b], x, preferred_element_type=jnp.float32)
-            d = (a - 1) * Y + (b - 1)
-            if d != 0:
-                term = pltpu.roll(term, (-d) % width, 1)
-            mask = ok[a][b]
-            if mask is not None:
-                term = jnp.where(mask, term, 0.0)
-            total = term if total is None else total + term
-    return total
-
-
 def _masks(width):
     p = lax.broadcasted_iota(jnp.int32, (1, width), 1)
     yy = p % Y
@@ -73,29 +57,43 @@
     return ok
 
 
-def _kernel(*refs, depth_base, plane_bases):
-    if depth_base is None:
-        x_ref, w_ref, o_ref = refs
+def _plane(x, w, ok):
+    width = x.shape[1]
+    pieces = []
+    for a in range(3):
+        for b in range(3):
+            d = (a - 1) * Y + (b - 1)
+            moved = x if d == 0 else pltpu.roll(x, (-d) % width, 1)
+            mask = ok[a][b]
+            if mask is not None:
+                moved = jnp.where(mask, moved, jnp.zeros_like(moved))
+            pieces.append(moved)
+    stacked = jnp.concatenate(pieces, axis=0)
+    return jnp.dot(w, stacked, preferred_element_type=jnp.float32)
+
+
+def _kernel(*refs, depth_index, plane_indices):
+    if depth_index is None:
+        x_ref, wp_ref, wd_ref, o_ref = refs
         h = x_ref[...]
     else:
-        lo_ref, mid_ref, up_ref, w_ref, o_ref = refs
-        total = jnp.dot(w_ref[depth_base + 1], mid_ref[...], preferred_element_type=jnp.float32)
-        total = total + jnp.dot(w_ref[depth_base], lo_ref[...], preferred_element_type=jnp.float32)
-        total = total + jnp.dot(w_ref[depth_base + 2], up_ref[...], preferred_element_type=jnp.float32)
+        lo_ref, mid_ref, up_ref, wp_ref, wd_ref, o_ref = refs
+        stacked = jnp.concatenate([lo_ref[...], mid_ref[...], up_ref[...]], axis=0)
+        total = jnp.dot(wd_ref[depth_index], stacked, preferred_element_type=jnp.float32)
         h = jnp.maximum(total, 0.0).astype(jnp.bfloat16)
-    if plane_bases:
+    if plane_indices:
         ok = _masks(h.shape[1])
-        for base in plane_bases:
-            h = jnp.maximum(_plane(h, w_ref, base, ok), 0.0).astype(jnp.bfloat16)
+        for index in plane_indices:
+            h = jnp.maximum(_plane(h, wp_ref[index], ok), 0.0).astype(jnp.bfloat16)
     o_ref[...] = h
 
 
-def layer_kernel(inputs, w, depth_base=None, plane_bases=()):
+def layer_kernel(inputs, wp, wd, depth_index=None, plane_indices=()):
     shape = inputs[0].shape
     return pl.pallas_call(
-        functools.partial(_kernel, depth_base=depth_base, plane_bases=tuple(plane_bases)),
+        functools.partial(_kernel, depth_index=depth_index, plane_indices=tuple(plane_indices)),
         out_shape=jax.ShapeDtypeStruct(shape, jnp.bfloat16),
-    )(*inputs, w)
+    )(*inputs, wp, wd)
 
 
 def local(volume, plane_a, plane_b, depth):
@@ -118,20 +116,21 @@
     got = got.reshape(parts, -1, flat)
     h = got[:, : part * slices].reshape(parts * part, slices * flat)
     w = got[:, part * slices :].reshape(parts, taps, out_part, chans)
-    w = jnp.transpose(w, (1, 0, 2, 3)).reshape(taps, parts * out_part, chans)
     nine = 9 * layers
+    wp = w[:, : 2 * nine].reshape(parts, 2, layers, 9, out_part, chans)
+    wp = jnp.transpose(wp, (2, 1, 0, 4, 3, 5)).reshape(2 * layers, parts * out_part, 9 * chans)
+    wd = w[:, 2 * nine :].reshape(parts, layers, 3, out_part, chans)
+    wd = jnp.transpose(wd, (1, 0, 3, 2, 4)).reshape(layers, parts * out_part, 3 * chans)
 
-    def bases(layer_index):
-        return (layer_index * 9, nine + layer_index * 9)
+    def convs(layer_index):
+        return (2 * layer_index, 2 * layer_index + 1)
 
-    second = layer_kernel([h], w, None, bases(0))
+    second = layer_kernel([h], wp, wd, None, convs(0))
     for layer_index in range(layers):
         lower = from_behind(second, 2, half)
         upper = from_behind(second, -2, half)
-        following = bases(layer_index + 1) if layer_index + 1 < layers else ()
-        second = layer_kernel(
-            [lower, second, upper], w, 2 * nine + layer_index * 3, following
-        )
+        following = convs(layer_index + 1) if layer_index + 1 < layers else ()
+        second = layer_kernel([lower, second, upper], wp, wd, layer_index, following)
     h = second.reshape(parts * part, slices, flat)
     h = lax.all_to_all(h, "ch", split_axis=0, concat_axis=1, tiled=True)
     h = swap_halves(h.reshape(part, parts, slices, flat), 1, flipped)

time: 86.6 us -> 84.8 us (0.979)
  Pallas kernels: 13 us -> 9.15 us
  local copies, waits for them, and re-layouts: 9.64 us -> 11.6 us
    pallas_call x3, Pallas kernels: 13 us -> 9.15 us  [layer_kernel(): pl.pallas_call(functools.partial(_kernel, depth_index=depth_index, plane_...]
    reshape x1 -> x2, local copies, waits for them, and re-layouts: 0.09 us -> 2 us  [the longest x1 1.25 us: local(): jnp.transpose(wp, (2, 1, 0, 4, 3, 5))]
where the time goes in v6:
time: 84.8 us; the launch traced here: 83.4 us
  blocking collectives  26.6 us (31%)
  waiting for transfers between devices  21.3 us (25%)
  starting transfers between devices  14.3 us (17%)
  local copies, waits for them, and re-layouts  11.6 us (14%)
  Pallas kernels  9.15 us (11%)
    ppermute x4, waiting for transfers between devices, from_behind(): return lax.ppermute(block, ('gz', 'ch'), route)  21.3 us
    all_to_all x1, blocking collectives, local(): got = lax.all_to_all(sent, 'ch', split_axis=0, concat_axis=0, tiled=True)  16.6 us
    ppermute x4, starting transfers between devices, from_behind(): return lax.ppermute(block, ('gz', 'ch'), route)  14.3 us
    all_to_all x1, blocking collectives, local(): h = lax.all_to_all(h, 'ch', split_axis=0, concat_axis=1, tiled=True)  9.96 us
    pallas_call x3, Pallas kernels, layer_kernel(): pl.pallas_call(functools.partial(_kernel, depth_index=depth_index, plane_...  9.15 us
    concatenate x3, local copies, waits for them, and re-layouts, pack_weights(): return jnp.concatenate([taps_a, taps_b, taps_d], axis=0)  2.52 us
  transfers between devices with their start and end apart: 4, of which 4 were waited for; matrix products, arithmetic and copies ran while one was open for 0% of the time, Pallas kernels for 0%

profile of v6, /device:TPU:96, one launch (start us, length us, event | category | flops | bytes accessed | tf_op | source)
XLA Modules:
  0.0 83.4 jit_solution(9380558900916720601)
XLA Ops:
  0.0 0.8 concatenate.15
  0.8 0.9 %concatenate.13 = bf16[1,18,512]{2,1,0:T(8,128)(2,1)S(1)} reshape(bf16[2,3,3,8,64]{4,3,2,1,0:T(8,128)(2,1)} %bitcast.31) | data formatting | bytes 36864 | tf_op jit(solution)/shard_map/concatenate | solution.py:37
  1.7 0.9 %concatenate.14 = bf16[1,18,512]{2,1,0:T(8,128)(2,1)S(1)} reshape(bf16[2,3,3,8,64]{4,3,2,1,0:T(8,128)(2,1)} %bitcast.32) | data formatting | bytes 36864 | tf_op jit(solution)/shard_map/concatenate | solution.py:37
  2.5 1.0 %reshape_reshape.9 = bf16[8,2,4,4,512]{4,3,2,1,0:T(4,128)(2,1)S(1)} reshape(bf16[8,32,512]{2,1,0:T(8,128)(2,1)} %param.4) | data formatting | bytes 524288 | tf_op jit(solution)/shard_map/reshape;reshape | solution.py:27
  3.5 0.1 reverse_select_fusion.1
  3.7 0.1 copy.14
  4.0 16.6 %all_to_all.20 = bf16[8,74,512]{2,1,0:T(8,128)(2,1)S(1)} all-to-all(bf16[8,74,512]{2,1,0:T(8,128)(2,1)S(1)} %pad_maximum_fusion), channel_id=1, replica_groups=mesh['gz'=32,'ch'=8] {'ch'}, dimensions={0} | all-to-all | bytes 1212416 | tf_op jit(solution)/shard_map/all_to_all | solution.py:115
  20.6 0.2 copy.15
  20.8 0.3 reshape.41
  21.3 0.9 %reshape.40.refs_0_ = bf16[64,2048]{1,0:T(8,128)(2,1)} reshape(bf16[8,32,512]{2,1,0:T(8,128)(2,1)S(1)} %slice.16) | data formatting | bytes 524288 | tf_op jit(solution)/shard_map/reshape | solution.py:117
  22.2 0.8 reshape.45.refs_2_.refs_4_
  23.0 0.7 copy.17
  23.7 1.2 %reshape.43.refs_1_.refs_3_ = bf16[4,64,576]{2,1,0:T(8,128)(2,1)} reshape(bf16[2,2,8,8,9,64]{5,4,3,2,1,0:T(8,128)(2,1)S(1)} %copy.17) | data formatting | bytes 589824 | tf_op jit(solution)/shard_map/reshape | solution.py:121
  25.0 3.4 %shard_map.46.refs_1_ = bf16[64,2048]{1,0:T(8,128)(2,1)} custom-call(bf16[64,2048]{1,0:T(8,128)(2,1)} %reshape.40.refs_0_, bf16[4,64,576]{2,1,0:T(8,128)(2,1)} %reshape.43.refs_1_.refs_3_, bf16[2,64,192]{2,1,0:T(8,128)(2,1)} %reshape.45.refs_2_.refs_4_), custom_call_target="tpu_custom_call" | custom-call | tf_op jit(solution)/shard_map/pallas_call | solution.py:93
  28.3 3.4 %collective-permute-start.1 = (bf16[64,2048]{1,0:T(8,128)(2,1)}, bf16[64,2048]{1,0:T(8,128)(2,1)S(1)}, u32[]{:S(2)}, u32[]{:S(2)}) collective-permute-start(bf16[64,2048]{1,0:T(8,128)(2,1)} %shard_map.46.refs_1_), channel_id=1, source_target_pairs={{20,0},{21,1},{22,2},{23,3},{16,4},{17,5},{18,6},{19,7},{28,8},{29... | collective-permute-start | bytes 786440 | tf_op jit(solution)/shard_map/ppermute | solution.py:22
  31.8 3.6 %collective-permute-start = (bf16[64,2048]{1,0:T(8,128)(2,1)}, bf16[64,2048]{1,0:T(8,128)(2,1)S(1)}, u32[]{:S(2)}, u32[]{:S(2)}) collective-permute-start(bf16[64,2048]{1,0:T(8,128)(2,1)} %shard_map.46.refs_1_), channel_id=1, source_target_pairs={{4,16},{5,17},{6,18},{7,19},{0,20},{1,21},{2,22},{3,23},{12,24},{1... | collective-permute-start | bytes 786440 | tf_op jit(solution)/shard_map/ppermute | solution.py:22
  35.4 9.1 %collective-permute-done.1.refs_2_ = bf16[64,2048]{1,0:T(8,128)(2,1)S(1)} collective-permute-done((bf16[64,2048]{1,0:T(8,128)(2,1)}, bf16[64,2048]{1,0:T(8,128)(2,1)S(1)}, u32[]{:S(2)}, u32[]{:S(2)}) %collective-permute-start.1) | collective-permute-done | bytes 262176 | tf_op jit(solution)/shard_map/ppermute | solution.py:22
  44.5 0.5 collective-permute-done.refs_0_
  45.0 0.2 copy-done.1
  45.2 0.7 copy-done.3
  45.9 3.6 %shard_map.47.refs_1_ = bf16[64,2048]{1,0:T(8,128)(2,1)} custom-call(bf16[64,2048]{1,0:T(8,128)(2,1)} %copy-done.3, bf16[64,2048]{1,0:T(8,128)(2,1)} %shard_map.46.refs_1_, bf16[64,2048]{1,0:T(8,128)(2,1)} %copy-done.1, bf16[4,64,576]{2,1,0:T(8,128)(2,1)} %reshape.43.refs_1_.refs_3_, bf16[2,64,192]{2,1,0:T(8,128)(2,1)} %reshape.45.refs_2_.refs_4_), custom_call_target="tpu_custom_call" | custom-call | tf_op jit(solution)/shard_map/pallas_call | solution.py:93
  49.5 3.6 %collective-permute-start.3 = (bf16[64,2048]{1,0:T(8,128)(2,1)}, bf16[64,2048]{1,0:T(8,128)(2,1)S(1)}, u32[]{:S(2)}, u32[]{:S(2)}) collective-permute-start(bf16[64,2048]{1,0:T(8,128)(2,1)} %shard_map.47.refs_1_), channel_id=1, source_target_pairs={{20,0},{21,1},{22,2},{23,3},{16,4},{17,5},{18,6},{19,7},{28,8},{29... | collective-permute-start | bytes 786440 | tf_op jit(solution)/shard_map/ppermute | solution.py:22
  53.1 3.6 %collective-permute-start.2 = (bf16[64,2048]{1,0:T(8,128)(2,1)}, bf16[64,2048]{1,0:T(8,128)(2,1)S(1)}, u32[]{:S(2)}, u32[]{:S(2)}) collective-permute-start(bf16[64,2048]{1,0:T(8,128)(2,1)} %shard_map.47.refs_1_), channel_id=1, source_target_pairs={{4,16},{5,17},{6,18},{7,19},{0,20},{1,21},{2,22},{3,23},{12,24},{1... | collective-permute-start | bytes 786440 | tf_op jit(solution)/shard_map/ppermute | solution.py:22
  56.7 10.4 %collective-permute-done.3.refs_2_ = bf16[64,2048]{1,0:T(8,128)(2,1)S(1)} collective-permute-done((bf16[64,2048]{1,0:T(8,128)(2,1)}, bf16[64,2048]{1,0:T(8,128)(2,1)S(1)}, u32[]{:S(2)}, u32[]{:S(2)}) %collective-permute-start.3) | collective-permute-done | bytes 262176 | tf_op jit(solution)/shard_map/ppermute | solution.py:22
  67.1 1.3 %collective-permute-done.2.refs_0_ = bf16[64,2048]{1,0:T(8,128)(2,1)S(1)} collective-permute-done((bf16[64,2048]{1,0:T(8,128)(2,1)}, bf16[64,2048]{1,0:T(8,128)(2,1)S(1)}, u32[]{:S(2)}, u32[]{:S(2)}) %collective-permute-start.2) | collective-permute-done | bytes 262176 | tf_op jit(solution)/shard_map/ppermute | solution.py:22
  68.4 0.7 copy-done.2
  69.1 2.2 %shard_map.48 = bf16[64,2048]{1,0:T(8,128)(2,1)} custom-call(bf16[64,2048]{1,0:T(8,128)(2,1)} %copy-done.2, bf16[64,2048]{1,0:T(8,128)(2,1)} %shard_map.47.refs_1_, bf16[64,2048]{1,0:T(8,128)(2,1)} %copy-done, bf16[4,64,576]{2,1,0:T(8,128)(2,1)} %reshape.43.refs_1_.refs_3_, bf16[2,64,192]{2,1,0:T(8,128)(2,1)} %reshape.45.refs_2_.refs_4_), custom_call_target="tpu_custom_call" | custom-call | tf_op jit(solution)/shard_map/pallas_call | solution.py:93
  71.3 1.1 %reshape.46 = bf16[64,4,512]{2,1,0:T(4,128)(2,1)S(1)} reshape(bf16[64,2048]{1,0:T(8,128)(2,1)} %shard_map.48) | data formatting | bytes 524288 | tf_op jit(solution)/shard_map/reshape | solution.py:134
  72.4 10.0 %all_to_all.21 = bf16[64,4,512]{2,1,0:T(4,128)(2,1)S(1)} all-to-all(bf16[64,4,512]{2,1,0:T(4,128)(2,1)S(1)} %reshape.46), channel_id=1, replica_groups=mesh['gz'=32,'ch'=8] {'ch'}, dimensions={0} | all-to-all | bytes 524288 | tf_op jit(solution)/shard_map/all_to_all | solution.py:135
  82.4 0.1 copy.20
  82.5 0.1 reverse_select_fusion
  82.6 0.8 reshape_reshape.11
  (14 shorter events, 0.4 us)
Async XLA Ops:
  28.3 16.1 %collective-permute-start.1 = (bf16[64,2048]{1,0:T(8,128)(2,1)}, bf16[64,2048]{1,0:T(8,128)(2,1)S(1)}, u32[]{:S(2)}, u32[]{:S(2)}) collective-permute-start(bf16[64,2048]{1,0:T(8,128)(2,1)} %shard_map.46.refs_1_), channel_id=1, source_target_pairs={{20,0},{21,1},{22,2},{23,3},{16,4},{17,5},{18,6},{19,7},{28,8},{29... | collective-permute-start | bytes 786440 | tf_op jit(solution)/shard_map/ppermute | solution.py:22
  31.8 13.2 %collective-permute-start = (bf16[64,2048]{1,0:T(8,128)(2,1)}, bf16[64,2048]{1,0:T(8,128)(2,1)S(1)}, u32[]{:S(2)}, u32[]{:S(2)}) collective-permute-start(bf16[64,2048]{1,0:T(8,128)(2,1)} %shard_map.46.refs_1_), channel_id=1, source_target_pairs={{4,16},{5,17},{6,18},{7,19},{0,20},{1,21},{2,22},{3,23},{12,24},{1... | collective-permute-start | bytes 786440 | tf_op jit(solution)/shard_map/ppermute | solution.py:22
  44.5 0.7 copy-start.1
  45.2 0.7 copy-start.3
  49.5 17.6 %collective-permute-start.3 = (bf16[64,2048]{1,0:T(8,128)(2,1)}, bf16[64,2048]{1,0:T(8,128)(2,1)S(1)}, u32[]{:S(2)}, u32[]{:S(2)}) collective-permute-start(bf16[64,2048]{1,0:T(8,128)(2,1)} %shard_map.47.refs_1_), channel_id=1, source_target_pairs={{20,0},{21,1},{22,2},{23,3},{16,4},{17,5},{18,6},{19,7},{28,8},{29... | collective-permute-start | bytes 786440 | tf_op jit(solution)/shard_map/ppermute | solution.py:22
  53.1 15.2 %collective-permute-start.2 = (bf16[64,2048]{1,0:T(8,128)(2,1)}, bf16[64,2048]{1,0:T(8,128)(2,1)S(1)}, u32[]{:S(2)}, u32[]{:S(2)}) collective-permute-start(bf16[64,2048]{1,0:T(8,128)(2,1)} %shard_map.47.refs_1_), channel_id=1, source_target_pairs={{4,16},{5,17},{6,18},{7,19},{0,20},{1,21},{2,22},{3,23},{12,24},{1... | collective-permute-start | bytes 786440 | tf_op jit(solution)/shard_map/ppermute | solution.py:22
  67.1 1.3 %copy-start = (bf16[64,2048]{1,0:T(8,128)(2,1)}, bf16[64,2048]{1,0:T(8,128)(2,1)S(1)}, u32[]{:S(2)}) copy-start(bf16[64,2048]{1,0:T(8,128)(2,1)S(1)} %collective-permute-done.3.refs_2_) | copy-start | bytes 786436
  68.4 0.7 copy-start.2

commit v7 on v6

v7 whole, which is shorter than its diff:
```python
import functools

import jax
import jax.numpy as jnp
from jax import lax
from jax.experimental import pallas as pl
from jax.experimental.pallas import tpu as pltpu
from jax.sharding import PartitionSpec as P

X = 64
Y = 8


def from_behind(block, distance, swap):
    slabs, parts = lax.axis_size("gz"), lax.axis_size("ch")
    route = [
        ((g - distance) * parts + (c ^ swap), g * parts + c)
        for g in range(slabs)
        if 0 <= g - distance < slabs
        for c in range(parts)
    ]
    return lax.ppermute(block, ("gz", "ch"), route)


def swap_halves(block, axis, flag):
    shape = block.shape
    halves = block.reshape(shape[:axis] + (2, shape[axis] // 2) + shape[axis + 1 :])
    swapped = jnp.flip(halves, axis)
    return jnp.where(flag, swapped, halves).reshape(shape)


PLANE_COLS = 640
DEPTH_COLS = 256


def pack_weights(plane_a, plane_b, depth):
    layers, out_part, chans = plane_a.shape[:3]
    planes = jnp.stack(
        [
            jnp.transpose(plane_a, (1, 0, 3, 4, 2)).reshape(out_part, layers, 9 * chans),
            jnp.transpose(plane_b, (1, 0, 3, 4, 2)).reshape(out_part, layers, 9 * chans),
        ],
        axis=2,
    )
    planes = jnp.pad(planes, ((0, 0), (0, 0), (0, 0), (0, PLANE_COLS - 9 * chans)))
    depths = jnp.transpose(depth, (1, 0, 3, 2)).reshape(out_part, layers, 3 * chans)
    depths = jnp.pad(depths, ((0, 0), (0, 0), (0, DEPTH_COLS - 3 * chans)))
    return jnp.concatenate(
        [planes.reshape(out_part, -1), depths.reshape(out_part, -1)], axis=1
    )


def _masks(width):
    p = lax.broadcasted_iota(jnp.int32, (1, width), 1)
    yy = p % Y
    xx = (p // Y) % X
    xm = [xx >= 1, None, xx <= X - 2]
    ym = [yy >= 1, None, yy <= Y - 2]
    ok = []
    for a in range(3):
        row = []
        for b in range(3):
            if xm[a] is None:
                row.append(ym[b])
            elif ym[b] is None:
                row.append(xm[a])
            else:
                row.append(jnp.logical_and(xm[a], ym[b]))
        ok.append(row)
    return ok


def _plane(x, w, ok):
    width = x.shape[1]
    pieces = []
    for a in range(3):
        for b in range(3):
            d = (a - 1) * Y + (b - 1)
            moved = x if d == 0 else pltpu.roll(x, (-d) % width, 1)
            mask = ok[a][b]
            if mask is not None:
                moved = jnp.where(mask, moved, jnp.zeros_like(moved))
            pieces.append(moved)
    stacked = jnp.concatenate(pieces, axis=0)
    return jnp.dot(w, stacked, preferred_element_type=jnp.float32)


def _kernel(*refs, width, layers, depth_index, plane_indices):
    if depth_index is None:
        src_ref, o_ref = refs
        h = src_ref[:, :width]
    else:
        lo_ref, mid_ref, up_ref, src_ref, o_ref = refs
        chans = mid_ref.shape[0]
        at = width + 2 * layers * PLANE_COLS + depth_index * DEPTH_COLS
        stacked = jnp.concatenate([lo_ref[...], mid_ref[...], up_ref[...]], axis=0)
        w = src_ref[:, at : at + 3 * chans]
        total = jnp.dot(w, stacked, preferred_element_type=jnp.float32)
        h = jnp.maximum(total, 0.0).astype(jnp.bfloat16)
    if plane_indices:
        ok = _masks(h.shape[1])
        chans = h.shape[0]
        for index in plane_indices:
            at = width + index * PLANE_COLS
            w = src_ref[:, at : at + 9 * chans]
            h = jnp.maximum(_plane(h, w, ok), 0.0).astype(jnp.bfloat16)
    o_ref[...] = h


def layer_kernel(inputs, src, width, layers, depth_index=None, plane_indices=()):
    shape = (src.shape[0], width)
    return pl.pallas_call(
        functools.partial(
            _kernel, width=width, layers=layers, depth_index=depth_index, plane_indices=tuple(plane_indices)
        ),
        out_shape=jax.ShapeDtypeStruct(shape, jnp.bfloat16),
    )(*inputs, src)


def local(volume, plane_a, plane_b, depth):
    layers = plane_a.shape[0]
    part, slab, flat = volume.shape
    parts = lax.axis_size("ch")
    slices = slab // parts
    width = slices * flat
    weights = pack_weights(plane_a, plane_b, depth)
    half = parts // 2
    flipped = (lax.axis_index("gz") // 2) % 2 == 1
    chunks = swap_halves(volume.reshape(part, parts, slices, flat), 1, flipped)
    sent_volume = jnp.transpose(chunks, (1, 0, 2, 3)).reshape(parts, part, width)
    sent_weights = jnp.broadcast_to(weights[None], (parts,) + weights.shape)
    sent = jnp.concatenate([sent_volume, sent_weights], axis=2)
    got = lax.all_to_all(sent, "ch", split_axis=0, concat_axis=0, tiled=True)
    src = got.reshape(parts * part, -1)

    def convs(layer_index):
        return (2 * layer_index, 2 * layer_index + 1)

    second = layer_kernel([], src, width, layers, None, convs(0))
    for layer_index in range(layers):
        lower = from_behind(second, 2, half)
        upper = from_behind(second, -2, half)
        following = convs(layer_index + 1) if layer_index + 1 < layers else ()
        second = layer_kernel([lower, second, upper], src, width, layers, layer_index, following)
    h = lax.all_to_all(second, "ch", split_axis=0, concat_axis=0, tiled=True)
    h = swap_halves(h.reshape(parts, part, slices, flat), 0, flipped)
    return jnp.transpose(h, (1, 0, 2, 3)).reshape(part, slab, flat)


def solution(mesh):
    return jax.shard_map(
        local,
        mesh=mesh,
        in_specs=(
            P("ch", "gz", None),
            P(None, "ch", None, None, None),
            P(None, "ch", None, None, None),
            P(None, "ch", None, None),
        ),
        out_specs=P("ch", "gz", None),
        check_vma=False,
    )
```

time: 84.8 us -> 79.2 us (0.934)
  local copies, waits for them, and re-layouts: 11.6 us -> 5.51 us
  blocking collectives: 26.6 us -> 27.6 us
    reshape x6 -> x4, local copies, waits for them, and re-layouts: 4.41 us -> 1.04 us  [the longest x1 0.77 us: local(): return jnp.transpose(h, (1, 0, 2, 3)).reshape(part, slab, flat)]
    concatenate x3 -> x0, local copies, waits for them, and re-layouts: 2.52 us -> none  [pack_weights(): return jnp.concatenate([taps_a, taps_b, taps_d], axis=0)]
    transpose x2 -> x3, local copies, waits for them, and re-layouts: 0.82 us -> 2.33 us  [the longest x1 0.79 us: pack_weights(): jnp.transpose(plane_b, (1, 0, 3, 4, 2)).reshape(out_part, layers, 9 * chans)]
    another operation x1, local copies, waits for them, and re-layouts: 1.02 us -> 0.07 us  [swap_halves(): block.reshape(shape[:axis] + (2, shape[axis] // 2) + shape[axis + 1:])]
    all_to_all x1, blocking collectives: 9.96 us -> 10.9 us  [local(): h = lax.all_to_all(second, 'ch', split_axis=0, concat_axis=0, tiled=True)]
where the time goes in v7:
time: 79.2 us; the launch traced here: 78.4 us
  blocking collectives  27.6 us (35%)
  waiting for transfers between devices  21.3 us (27%)
  starting transfers between devices  14.2 us (18%)
  Pallas kernels  9.46 us (12%)
  local copies, waits for them, and re-layouts  5.51 us (7%)
    ppermute x4, waiting for transfers between devices, from_behind(): return lax.ppermute(block, ('gz', 'ch'), route)  21.3 us
    all_to_all x1, blocking collectives, local(): got = lax.all_to_all(sent, 'ch', split_axis=0, concat_axis=0, tiled=True)  16.7 us
    ppermute x4, starting transfers between devices, from_behind(): return lax.ppermute(block, ('gz', 'ch'), route)  14.2 us
    all_to_all x1, blocking collectives, local(): h = lax.all_to_all(second, 'ch', split_axis=0, concat_axis=0, tiled=True)  10.9 us
    pallas_call x3, Pallas kernels, layer_kernel(): pl.pallas_call(functools.partial(_kernel, width=width, layers=layers, dep...  9.46 us
    unnamed x11, local copies, waits for them, and re-layouts  1.65 us
  transfers between devices with their start and end apart: 4, of which 4 were waited for; matrix products, arithmetic and copies ran while one was open for 0% of the time, Pallas kernels for 0%

profile of v7, /device:TPU:96, one launch (start us, length us, event | category | flops | bytes accessed | tf_op | source)
XLA Modules:
  0.0 78.4 jit_solution(14590359470372238208)
XLA Ops:
  0.0 0.0 copy-start
  0.0 0.8 copy.16
  0.8 0.1 reshape.31
  0.9 0.8 %copy.13 = bf16[8,2,3,3,64]{4,3,2,0,1:T(4,128)(2,1)S(1)} copy(bf16[8,2,3,3,64]{4,0,3,2,1:T(8,128)(2,1)} %bitcast.28) | data formatting | bytes 36864 | tf_op jit(solution)/shard_map/transpose | solution.py:40
  1.6 0.1 stack_reshape.6
  1.7 0.8 %copy.14 = bf16[8,2,3,3,64]{4,3,2,0,1:T(4,128)(2,1)S(1)} copy(bf16[8,2,3,3,64]{4,0,3,2,1:T(8,128)(2,1)} %bitcast.29) | data formatting | bytes 36864 | tf_op jit(solution)/shard_map/transpose | solution.py:41
  2.5 0.1 stack_reshape.7
  2.8 0.0 copy-done
  2.8 0.1 reshape_reshape.6
  2.9 0.1 reverse_select_fusion.1
  3.0 0.2 copy.12
  3.3 16.7 %all_to_all.14 = bf16[8,8,5120]{2,1,0:T(8,128)(2,1)} all-to-all(bf16[8,8,5120]{2,1,0:T(8,128)(2,1)S(1)} %pad_maximum_fusion), channel_id=1, replica_groups=mesh['gz'=32,'ch'=8] {'ch'}, dimensions={0} | all-to-all | bytes 1310720 | tf_op jit(solution)/shard_map/all_to_all | solution.py:133
  20.0 3.4 %shard_map.46.refs_1_ = bf16[64,2048]{1,0:T(8,128)(2,1)} custom-call(bf16[64,5120]{1,0:T(8,128)(2,1)} %bitcast.20), custom_call_target="tpu_custom_call" | custom-call | tf_op jit(solution)/shard_map/pallas_call | solution.py:112
  23.4 3.4 %collective-permute-start.1 = (bf16[64,2048]{1,0:T(8,128)(2,1)}, bf16[64,2048]{1,0:T(8,128)(2,1)S(1)}, u32[]{:S(2)}, u32[]{:S(2)}) collective-permute-start(bf16[64,2048]{1,0:T(8,128)(2,1)} %shard_map.46.refs_1_), channel_id=1, source_target_pairs={{20,0},{21,1},{22,2},{23,3},{16,4},{17,5},{18,6},{19,7},{28,8},{29... | collective-permute-start | bytes 786440 | tf_op jit(solution)/shard_map/ppermute | solution.py:22
  26.9 3.6 %collective-permute-start = (bf16[64,2048]{1,0:T(8,128)(2,1)}, bf16[64,2048]{1,0:T(8,128)(2,1)S(1)}, u32[]{:S(2)}, u32[]{:S(2)}) collective-permute-start(bf16[64,2048]{1,0:T(8,128)(2,1)} %shard_map.46.refs_1_), channel_id=1, source_target_pairs={{4,16},{5,17},{6,18},{7,19},{0,20},{1,21},{2,22},{3,23},{12,24},{1... | collective-permute-start | bytes 786440 | tf_op jit(solution)/shard_map/ppermute | solution.py:22
  30.5 9.1 %collective-permute-done.1.refs_2_ = bf16[64,2048]{1,0:T(8,128)(2,1)S(1)} collective-permute-done((bf16[64,2048]{1,0:T(8,128)(2,1)}, bf16[64,2048]{1,0:T(8,128)(2,1)S(1)}, u32[]{:S(2)}, u32[]{:S(2)}) %collective-permute-start.1) | collective-permute-done | bytes 262176 | tf_op jit(solution)/shard_map/ppermute | solution.py:22
  39.5 0.0 copy-start.2
  39.5 0.5 collective-permute-done.refs_0_
  40.1 0.2 copy-done.2
  40.3 0.0 copy-start.4
  40.3 0.7 copy-done.4
  41.0 3.7 %shard_map.47.refs_1_ = bf16[64,2048]{1,0:T(8,128)(2,1)} custom-call(bf16[64,2048]{1,0:T(8,128)(2,1)} %copy-done.4, bf16[64,2048]{1,0:T(8,128)(2,1)} %shard_map.46.refs_1_, bf16[64,2048]{1,0:T(8,128)(2,1)} %copy-done.2, bf16[64,5120]{1,0:T(8,128)(2,1)} %bitcast.21), custom_call_target="tpu_custom_call" | custom-call | tf_op jit(solution)/shard_map/pallas_call | solution.py:112
  44.7 3.6 %collective-permute-start.3 = (bf16[64,2048]{1,0:T(8,128)(2,1)}, bf16[64,2048]{1,0:T(8,128)(2,1)S(1)}, u32[]{:S(2)}, u32[]{:S(2)}) collective-permute-start(bf16[64,2048]{1,0:T(8,128)(2,1)} %shard_map.47.refs_1_), channel_id=1, source_target_pairs={{20,0},{21,1},{22,2},{23,3},{16,4},{17,5},{18,6},{19,7},{28,8},{29... | collective-permute-start | bytes 786440 | tf_op jit(solution)/shard_map/ppermute | solution.py:22
  48.3 3.6 %collective-permute-start.2 = (bf16[64,2048]{1,0:T(8,128)(2,1)}, bf16[64,2048]{1,0:T(8,128)(2,1)S(1)}, u32[]{:S(2)}, u32[]{:S(2)}) collective-permute-start(bf16[64,2048]{1,0:T(8,128)(2,1)} %shard_map.47.refs_1_), channel_id=1, source_target_pairs={{4,16},{5,17},{6,18},{7,19},{0,20},{1,21},{2,22},{3,23},{12,24},{1... | collective-permute-start | bytes 786440 | tf_op jit(solution)/shard_map/ppermute | solution.py:22
  51.9 10.4 %collective-permute-done.3.refs_2_ = bf16[64,2048]{1,0:T(8,128)(2,1)S(1)} collective-permute-done((bf16[64,2048]{1,0:T(8,128)(2,1)}, bf16[64,2048]{1,0:T(8,128)(2,1)S(1)}, u32[]{:S(2)}, u32[]{:S(2)}) %collective-permute-start.3) | collective-permute-done | bytes 262176 | tf_op jit(solution)/shard_map/ppermute | solution.py:22
  62.3 1.3 %collective-permute-done.2.refs_0_ = bf16[64,2048]{1,0:T(8,128)(2,1)S(1)} collective-permute-done((bf16[64,2048]{1,0:T(8,128)(2,1)}, bf16[64,2048]{1,0:T(8,128)(2,1)S(1)}, u32[]{:S(2)}, u32[]{:S(2)}) %collective-permute-start.2) | collective-permute-done | bytes 262176 | tf_op jit(solution)/shard_map/ppermute | solution.py:22
  63.6 0.0 copy-done.1
  63.6 0.7 copy-done.3
  64.3 2.3 %shard_map.48 = bf16[64,2048]{1,0:T(8,128)(2,1)} custom-call(bf16[64,2048]{1,0:T(8,128)(2,1)} %copy-done.3, bf16[64,2048]{1,0:T(8,128)(2,1)} %shard_map.47.refs_1_, bf16[64,2048]{1,0:T(8,128)(2,1)} %copy-done.1, bf16[64,5120]{1,0:T(8,128)(2,1)} %bitcast.22), custom_call_target="tpu_custom_call" | custom-call | tf_op jit(solution)/shard_map/pallas_call | solution.py:112
  66.6 10.9 %all_to_all.15 = bf16[8,8,2048]{2,1,0:T(8,128)(2,1)S(1)} all-to-all(bf16[8,8,2048]{2,1,0:T(8,128)(2,1)} %bitcast.27), channel_id=1, replica_groups=mesh['gz'=32,'ch'=8] {'ch'}, dimensions={0} | all-to-all | bytes 524288 | tf_op jit(solution)/shard_map/all_to_all | solution.py:145
  77.5 0.1 copy.17
  77.7 0.8 reshape.35
  (11 shorter events, 0.3 us)
Async XLA Ops:
  0.0 2.8 %copy-start = (bf16[8,32,512]{2,1,0:T(8,128)(2,1)S(1)}, bf16[8,32,512]{2,1,0:T(8,128)(2,1)}, u32[]{:S(2)}) copy-start(bf16[8,32,512]{2,1,0:T(8,128)(2,1)} %param.4) | copy-start | bytes 786436
  23.4 16.1 %collective-permute-start.1 = (bf16[64,2048]{1,0:T(8,128)(2,1)}, bf16[64,2048]{1,0:T(8,128)(2,1)S(1)}, u32[]{:S(2)}, u32[]{:S(2)}) collective-permute-start(bf16[64,2048]{1,0:T(8,128)(2,1)} %shard_map.46.refs_1_), channel_id=1, source_target_pairs={{20,0},{21,1},{22,2},{23,3},{16,4},{17,5},{18,6},{19,7},{28,8},{29... | collective-permute-start | bytes 786440 | tf_op jit(solution)/shard_map/ppermute | solution.py:22
  26.9 13.2 %collective-permute-start = (bf16[64,2048]{1,0:T(8,128)(2,1)}, bf16[64,2048]{1,0:T(8,128)(2,1)S(1)}, u32[]{:S(2)}, u32[]{:S(2)}) collective-permute-start(bf16[64,2048]{1,0:T(8,128)(2,1)} %shard_map.46.refs_1_), channel_id=1, source_target_pairs={{4,16},{5,17},{6,18},{7,19},{0,20},{1,21},{2,22},{3,23},{12,24},{1... | collective-permute-start | bytes 786440 | tf_op jit(solution)/shard_map/ppermute | solution.py:22
  39.5 0.7 copy-start.2
  40.3 0.7 copy-start.4
  44.7 17.6 %collective-permute-start.3 = (bf16[64,2048]{1,0:T(8,128)(2,1)}, bf16[64,2048]{1,0:T(8,128)(2,1)S(1)}, u32[]{:S(2)}, u32[]{:S(2)}) collective-permute-start(bf16[64,2048]{1,0:T(8,128)(2,1)} %shard_map.47.refs_1_), channel_id=1, source_target_pairs={{20,0},{21,1},{22,2},{23,3},{16,4},{17,5},{18,6},{19,7},{28,8},{29... | collective-permute-start | bytes 786440 | tf_op jit(solution)/shard_map/ppermute | solution.py:22
  48.3 15.3 %collective-permute-start.2 = (bf16[64,2048]{1,0:T(8,128)(2,1)}, bf16[64,2048]{1,0:T(8,128)(2,1)S(1)}, u32[]{:S(2)}, u32[]{:S(2)}) collective-permute-start(bf16[64,2048]{1,0:T(8,128)(2,1)} %shard_map.47.refs_1_), channel_id=1, source_target_pairs={{4,16},{5,17},{6,18},{7,19},{0,20},{1,21},{2,22},{3,23},{12,24},{1... | collective-permute-start | bytes 786440 | tf_op jit(solution)/shard_map/ppermute | solution.py:22
  62.3 1.3 %copy-start.1 = (bf16[64,2048]{1,0:T(8,128)(2,1)}, bf16[64,2048]{1,0:T(8,128)(2,1)S(1)}, u32[]{:S(2)}) copy-start(bf16[64,2048]{1,0:T(8,128)(2,1)S(1)} %collective-permute-done.3.refs_2_) | copy-start | bytes 786436
  63.6 0.7 copy-start.3

commit v8 on v7

--- a/solution.py
+++ b/solution.py
@@ -85,36 +85,50 @@
     return jnp.dot(w, stacked, preferred_element_type=jnp.float32)
 
 
-def _kernel(*refs, width, layers, depth_index, plane_indices):
+def _kernel(*refs, depth_index, planes):
+    refs = list(refs)
+    o_ref = refs.pop()
     if depth_index is None:
-        src_ref, o_ref = refs
-        h = src_ref[:, :width]
+        h = refs.pop(0)[...]
     else:
-        lo_ref, mid_ref, up_ref, src_ref, o_ref = refs
+        lo_ref, mid_ref, up_ref, wd_ref = refs[:4]
+        refs = refs[4:]
         chans = mid_ref.shape[0]
-        at = width + 2 * layers * PLANE_COLS + depth_index * DEPTH_COLS
         stacked = jnp.concatenate([lo_ref[...], mid_ref[...], up_ref[...]], axis=0)
-        w = src_ref[:, at : at + 3 * chans]
-        total = jnp.dot(w, stacked, preferred_element_type=jnp.float32)
+        at = depth_index * DEPTH_COLS
+        total = jnp.dot(wd_ref[:, at : at + 3 * chans], stacked, preferred_element_type=jnp.float32)
         h = jnp.maximum(total, 0.0).astype(jnp.bfloat16)
-    if plane_indices:
+    if planes:
         ok = _masks(h.shape[1])
         chans = h.shape[0]
-        for index in plane_indices:
-            at = width + index * PLANE_COLS
-            w = src_ref[:, at : at + 9 * chans]
+        for w_ref in refs:
+            w = w_ref[:, : 9 * chans]
             h = jnp.maximum(_plane(h, w, ok), 0.0).astype(jnp.bfloat16)
     o_ref[...] = h
 
 
-def layer_kernel(inputs, src, width, layers, depth_index=None, plane_indices=()):
-    shape = (src.shape[0], width)
+def layer_kernel(inputs, src, slices, flat, layers, depth_index=None, plane_indices=()):
+    chans = src.shape[0]
+    depth_block = 2 * layers * PLANE_COLS // (layers * DEPTH_COLS)
+    first_slice = (2 * layers * PLANE_COLS + layers * DEPTH_COLS) // flat
+    piece = pl.BlockSpec((chans, flat), lambda z: (0, z))
+    specs, args = [], []
+    if depth_index is None:
+        specs.append(pl.BlockSpec((chans, flat), lambda z: (0, first_slice + z)))
+        args.append(src)
+    else:
+        specs += [piece] * 3 + [pl.BlockSpec((chans, layers * DEPTH_COLS), lambda z: (0, depth_block))]
+        args += list(inputs) + [src]
+    for k in plane_indices:
+        specs.append(pl.BlockSpec((chans, PLANE_COLS), lambda z, k=k: (0, k)))
+        args.append(src)
     return pl.pallas_call(
-        functools.partial(
-            _kernel, width=width, layers=layers, depth_index=depth_index, plane_indices=tuple(plane_indices)
-        ),
-        out_shape=jax.ShapeDtypeStruct(shape, jnp.bfloat16),
-    )(*inputs, src)
+        functools.partial(_kernel, depth_index=depth_index, planes=bool(plane_indices)),
+        out_shape=jax.ShapeDtypeStruct((chans, slices * flat), jnp.bfloat16),
+        grid=(slices,),
+        in_specs=specs,
+        out_specs=piece,
+    )(*args)
 
 
 def local(volume, plane_a, plane_b, depth):
@@ -129,19 +143,21 @@
     chunks = swap_halves(volume.reshape(part, parts, slices, flat), 1, flipped)
     sent_volume = jnp.transpose(chunks, (1, 0, 2, 3)).reshape(parts, part, width)
     sent_weights = jnp.broadcast_to(weights[None], (parts,) + weights.shape)
-    sent = jnp.concatenate([sent_volume, sent_weights], axis=2)
+    sent = jnp.concatenate([sent_weights, sent_volume], axis=2)
     got = lax.all_to_all(sent, "ch", split_axis=0, concat_axis=0, tiled=True)
     src = got.reshape(parts * part, -1)
 
     def convs(layer_index):
         return (2 * layer_index, 2 * layer_index + 1)
 
-    second = layer_kernel([], src, width, layers, None, convs(0))
+    second = layer_kernel([], src, slices, flat, layers, None, convs(0))
     for layer_index in range(layers):
         lower = from_behind(second, 2, half)
         upper = from_behind(second, -2, half)
         following = convs(layer_index + 1) if layer_index + 1 < layers else ()
-        second = layer_kernel([lower, second, upper], src, width, layers, layer_index, following)
+        second = layer_kernel(
+            [lower, second, upper], src, slices, flat, layers, layer_index, following
+        )
     h = lax.all_to_all(second, "ch", split_axis=0, concat_axis=0, tiled=True)
     h = swap_halves(h.reshape(parts, part, slices, flat), 0, flipped)
     return jnp.transpose(h, (1, 0, 2, 3)).reshape(part, slab, flat)

time: 79.2 us -> 83.5 us (1.054)
  Pallas kernels: 9.46 us -> 13.4 us
    pallas_call x3, Pallas kernels: 9.46 us -> 13.4 us  [layer_kernel(): pl.pallas_call(functools.partial(_kernel, depth_index=depth_index, planes...]
where the time goes in v8:
time: 83.5 us; the launch traced here: 82.3 us
  blocking collectives  27.6 us (33%)
  waiting for transfers between devices  21.3 us (26%)
  starting transfers between devices  14.2 us (17%)
  Pallas kernels  13.4 us (16%)
  local copies, waits for them, and re-layouts  5.52 us (7%)
    ppermute x4, waiting for transfers between devices, from_behind(): return lax.ppermute(block, ('gz', 'ch'), route)  21.3 us
    all_to_all x1, blocking collectives, local(): got = lax.all_to_all(sent, 'ch', split_axis=0, concat_axis=0, tiled=True)  16.7 us
    ppermute x4, starting transfers between devices, from_behind(): return lax.ppermute(block, ('gz', 'ch'), route)  14.2 us
    pallas_call x3, Pallas kernels, layer_kernel(): pl.pallas_call(functools.partial(_kernel, depth_index=depth_index, planes...  13.4 us
    all_to_all x1, blocking collectives, local(): h = lax.all_to_all(second, 'ch', split_axis=0, concat_axis=0, tiled=True)  10.9 us
  transfers between devices with their start and end apart: 4, of which 4 were waited for; matrix products, arithmetic and copies ran while one was open for 0% of the time, Pallas kernels for 0%

profile of v8, /device:TPU:96, one launch (start us, length us, event | category | flops | bytes accessed | tf_op | source)
XLA Modules:
  0.0 82.3 jit_solution(11866860205520246314)
XLA Ops:
  0.0 0.0 copy-start.2
  0.0 0.8 copy.15
  0.8 0.1 reshape.29
  0.9 0.8 copy.12
  1.6 0.1 stack_reshape.6
  1.7 0.8 copy.13
  2.5 0.1 stack_reshape.7
  2.8 0.0 copy-done.2
  2.8 0.1 reshape_reshape.6
  2.9 0.1 reverse_select_fusion.1
  3.0 0.2 copy.16
  3.3 16.7 %all_to_all.14 = bf16[8,8,5120]{2,1,0:T(8,128)(2,1)} all-to-all(bf16[8,8,5120]{2,1,0:T(8,128)(2,1)S(1)} %pad_maximum_fusion), channel_id=1, replica_groups=mesh['gz'=32,'ch'=8] {'ch'}, dimensions={0} | all-to-all | bytes 1310720 | tf_op jit(solution)/shard_map/all_to_all | solution.py:147
  20.0 4.6 %shard_map.46.refs_1_ = bf16[64,2048]{1,0:T(8,128)(2,1)} custom-call(bf16[64,5120]{1,0:T(8,128)(2,1)} %bitcast.20, bf16[64,5120]{1,0:T(8,128)(2,1)} %bitcast.21, bf16[64,5120]{1,0:T(8,128)(2,1)} %bitcast.22), custom_call_target="tpu_custom_call" | custom-call | tf_op jit(solution)/shard_map/pallas_call | solution.py:125
  24.6 3.4 %collective-permute-start.1 = (bf16[64,2048]{1,0:T(8,128)(2,1)}, bf16[64,2048]{1,0:T(8,128)(2,1)S(1)}, u32[]{:S(2)}, u32[]{:S(2)}) collective-permute-start(bf16[64,2048]{1,0:T(8,128)(2,1)} %shard_map.46.refs_1_), channel_id=1, source_target_pairs={{20,0},{21,1},{22,2},{23,3},{16,4},{17,5},{18,6},{19,7},{28,8},{29... | collective-permute-start | bytes 786440 | tf_op jit(solution)/shard_map/ppermute | solution.py:22
  28.0 3.6 %collective-permute-start = (bf16[64,2048]{1,0:T(8,128)(2,1)}, bf16[64,2048]{1,0:T(8,128)(2,1)S(1)}, u32[]{:S(2)}, u32[]{:S(2)}) collective-permute-start(bf16[64,2048]{1,0:T(8,128)(2,1)} %shard_map.46.refs_1_), channel_id=1, source_target_pairs={{4,16},{5,17},{6,18},{7,19},{0,20},{1,21},{2,22},{3,23},{12,24},{1... | collective-permute-start | bytes 786440 | tf_op jit(solution)/shard_map/ppermute | solution.py:22
  31.7 9.1 %collective-permute-done.1.refs_2_ = bf16[64,2048]{1,0:T(8,128)(2,1)S(1)} collective-permute-done((bf16[64,2048]{1,0:T(8,128)(2,1)}, bf16[64,2048]{1,0:T(8,128)(2,1)S(1)}, u32[]{:S(2)}, u32[]{:S(2)}) %collective-permute-start.1) | collective-permute-done | bytes 262176 | tf_op jit(solution)/shard_map/ppermute | solution.py:22
  40.7 0.0 copy-start
  40.7 0.5 collective-permute-done.refs_0_
  41.2 0.2 copy-done
  41.5 0.0 copy-start.1
  41.5 0.7 copy-done.1
  42.2 5.3 %shard_map.47.refs_1_ = bf16[64,2048]{1,0:T(8,128)(2,1)} custom-call(bf16[64,2048]{1,0:T(8,128)(2,1)} %copy-done.1, bf16[64,2048]{1,0:T(8,128)(2,1)} %shard_map.46.refs_1_, bf16[64,2048]{1,0:T(8,128)(2,1)} %copy-done, bf16[64,5120]{1,0:T(8,128)(2,1)} %bitcast.23, bf16[64,5120]{1,0:T(8,128)(2,1)} %bitcast.24, bf16[64,5120]{1,0:T(8,128)(2,1)} %bitcast.25), custom_call_target="tpu_custom_call" | custom-call | tf_op jit(solution)/shard_map/pallas_call | solution.py:125
  47.4 3.6 %collective-permute-start.3 = (bf16[64,2048]{1,0:T(8,128)(2,1)}, bf16[64,2048]{1,0:T(8,128)(2,1)S(1)}, u32[]{:S(2)}, u32[]{:S(2)}) collective-permute-start(bf16[64,2048]{1,0:T(8,128)(2,1)} %shard_map.47.refs_1_), channel_id=1, source_target_pairs={{20,0},{21,1},{22,2},{23,3},{16,4},{17,5},{18,6},{19,7},{28,8},{29... | collective-permute-start | bytes 786440 | tf_op jit(solution)/shard_map/ppermute | solution.py:22
  51.1 3.6 %collective-permute-start.2 = (bf16[64,2048]{1,0:T(8,128)(2,1)}, bf16[64,2048]{1,0:T(8,128)(2,1)S(1)}, u32[]{:S(2)}, u32[]{:S(2)}) collective-permute-start(bf16[64,2048]{1,0:T(8,128)(2,1)} %shard_map.47.refs_1_), channel_id=1, source_target_pairs={{4,16},{5,17},{6,18},{7,19},{0,20},{1,21},{2,22},{3,23},{12,24},{1... | collective-permute-start | bytes 786440 | tf_op jit(solution)/shard_map/ppermute | solution.py:22
  54.6 10.4 %collective-permute-done.3.refs_2_ = bf16[64,2048]{1,0:T(8,128)(2,1)S(1)} collective-permute-done((bf16[64,2048]{1,0:T(8,128)(2,1)}, bf16[64,2048]{1,0:T(8,128)(2,1)S(1)}, u32[]{:S(2)}, u32[]{:S(2)}) %collective-permute-start.3) | collective-permute-done | bytes 262176 | tf_op jit(solution)/shard_map/ppermute | solution.py:22
  65.0 1.3 %collective-permute-done.2.refs_0_ = bf16[64,2048]{1,0:T(8,128)(2,1)S(1)} collective-permute-done((bf16[64,2048]{1,0:T(8,128)(2,1)}, bf16[64,2048]{1,0:T(8,128)(2,1)S(1)}, u32[]{:S(2)}, u32[]{:S(2)}) %collective-permute-start.2) | collective-permute-done | bytes 262176 | tf_op jit(solution)/shard_map/ppermute | solution.py:22
  66.3 0.0 copy-done.3
  66.3 0.7 copy-done.4
  67.0 3.5 %shard_map.48 = bf16[64,2048]{1,0:T(8,128)(2,1)} custom-call(bf16[64,2048]{1,0:T(8,128)(2,1)} %copy-done.4, bf16[64,2048]{1,0:T(8,128)(2,1)} %shard_map.47.refs_1_, bf16[64,2048]{1,0:T(8,128)(2,1)} %copy-done.3, bf16[64,5120]{1,0:T(8,128)(2,1)} %bitcast.26), custom_call_target="tpu_custom_call" | custom-call | tf_op jit(solution)/shard_map/pallas_call | solution.py:125
  70.5 10.9 %all_to_all.15 = bf16[8,8,2048]{2,1,0:T(8,128)(2,1)S(1)} all-to-all(bf16[8,8,2048]{2,1,0:T(8,128)(2,1)} %bitcast.31), channel_id=1, replica_groups=mesh['gz'=32,'ch'=8] {'ch'}, dimensions={0} | all-to-all | bytes 524288 | tf_op jit(solution)/shard_map/all_to_all | solution.py:161
  81.4 0.1 copy.17
  81.6 0.8 reshape.35
  (11 shorter events, 0.3 us)
Async XLA Ops:
  0.0 2.8 %copy-start.2 = (bf16[8,32,512]{2,1,0:T(8,128)(2,1)S(1)}, bf16[8,32,512]{2,1,0:T(8,128)(2,1)}, u32[]{:S(2)}) copy-start(bf16[8,32,512]{2,1,0:T(8,128)(2,1)} %param.4) | copy-start | bytes 786436
  24.6 16.1 %collective-permute-start.1 = (bf16[64,2048]{1,0:T(8,128)(2,1)}, bf16[64,2048]{1,0:T(8,128)(2,1)S(1)}, u32[]{:S(2)}, u32[]{:S(2)}) collective-permute-start(bf16[64,2048]{1,0:T(8,128)(2,1)} %shard_map.46.refs_1_), channel_id=1, source_target_pairs={{20,0},{21,1},{22,2},{23,3},{16,4},{17,5},{18,6},{19,7},{28,8},{29... | collective-permute-start | bytes 786440 | tf_op jit(solution)/shard_map/ppermute | solution.py:22
  28.0 13.2 %collective-permute-start = (bf16[64,2048]{1,0:T(8,128)(2,1)}, bf16[64,2048]{1,0:T(8,128)(2,1)S(1)}, u32[]{:S(2)}, u32[]{:S(2)}) collective-permute-start(bf16[64,2048]{1,0:T(8,128)(2,1)} %shard_map.46.refs_1_), channel_id=1, source_target_pairs={{4,16},{5,17},{6,18},{7,19},{0,20},{1,21},{2,22},{3,23},{12,24},{1... | collective-permute-start | bytes 786440 | tf_op jit(solution)/shard_map/ppermute | solution.py:22
  40.7 0.7 copy-start
  41.5 0.7 copy-start.1
  47.4 17.6 %collective-permute-start.3 = (bf16[64,2048]{1,0:T(8,128)(2,1)}, bf16[64,2048]{1,0:T(8,128)(2,1)S(1)}, u32[]{:S(2)}, u32[]{:S(2)}) collective-permute-start(bf16[64,2048]{1,0:T(8,128)(2,1)} %shard_map.47.refs_1_), channel_id=1, source_target_pairs={{20,0},{21,1},{22,2},{23,3},{16,4},{17,5},{18,6},{19,7},{28,8},{29... | collective-permute-start | bytes 786440 | tf_op jit(solution)/shard_map/ppermute | solution.py:22
  51.1 15.2 %collective-permute-start.2 = (bf16[64,2048]{1,0:T(8,128)(2,1)}, bf16[64,2048]{1,0:T(8,128)(2,1)S(1)}, u32[]{:S(2)}, u32[]{:S(2)}) collective-permute-start(bf16[64,2048]{1,0:T(8,128)(2,1)} %shard_map.47.refs_1_), channel_id=1, source_target_pairs={{4,16},{5,17},{6,18},{7,19},{0,20},{1,21},{2,22},{3,23},{12,24},{1... | collective-permute-start | bytes 786440 | tf_op jit(solution)/shard_map/ppermute | solution.py:22
  65.0 1.3 %copy-start.3 = (bf16[64,2048]{1,0:T(8,128)(2,1)}, bf16[64,2048]{1,0:T(8,128)(2,1)S(1)}, u32[]{:S(2)}) copy-start(bf16[64,2048]{1,0:T(8,128)(2,1)S(1)} %collective-permute-done.3.refs_2_) | copy-start | bytes 786436
  66.3 0.7 copy-start.4

commit v9 on v7

v9 whole, which is shorter than its diff:
```python
import functools

import jax
import jax.numpy as jnp
from jax import lax
from jax.experimental import pallas as pl
from jax.experimental.pallas import tpu as pltpu
from jax.sharding import Mesh
from jax.sharding import PartitionSpec as P

X = 64
Y = 8
PLANE_COLS = 640
DEPTH_COLS = 256
LAYER_COLS = 2 * PLANE_COLS + DEPTH_COLS
SLAB = ("z", "yh", "core")
GROUP = ("yh", "ch")


def pack_weights(plane_a, plane_b, depth):
    layers, out_part, chans = plane_a.shape[:3]
    pad = ((0, 0), (0, 0), (0, PLANE_COLS - 9 * chans))
    taps_a = jnp.pad(jnp.transpose(plane_a, (1, 0, 3, 4, 2)).reshape(out_part, layers, -1), pad)
    taps_b = jnp.pad(jnp.transpose(plane_b, (1, 0, 3, 4, 2)).reshape(out_part, layers, -1), pad)
    taps_d = jnp.transpose(depth, (1, 0, 3, 2)).reshape(out_part, layers, 3 * chans)
    taps_d = jnp.pad(taps_d, ((0, 0), (0, 0), (0, DEPTH_COLS - 3 * chans)))
    return jnp.concatenate([taps_a, taps_b, taps_d], axis=2)


def _masks(width):
    p = lax.broadcasted_iota(jnp.int32, (1, width), 1)
    yy = p % Y
    xx = (p // Y) % X
    xm = [xx >= 1, None, xx <= X - 2]
    ym = [yy >= 1, None, yy <= Y - 2]
    ok = []
    for a in range(3):
        row = []
        for b in range(3):
            if xm[a] is None:
                row.append(ym[b])
            elif ym[b] is None:
                row.append(xm[a])
            else:
                row.append(jnp.logical_and(xm[a], ym[b]))
        ok.append(row)
    return ok


def _plane(x, w, ok):
    width = x.shape[1]
    pieces = []
    for a in range(3):
        for b in range(3):
            d = (a - 1) * Y + (b - 1)
            moved = x if d == 0 else pltpu.roll(x, (-d) % width, 1)
            mask = ok[a][b]
            if mask is not None:
                moved = jnp.where(mask, moved, jnp.zeros_like(moved))
            pieces.append(moved)
    stacked = jnp.concatenate(pieces, axis=0)
    return jnp.dot(w, stacked, preferred_element_type=jnp.float32)


def _kernel(*refs, depth_layer, plane_layer, vol_cols, chans, split_out):
    if split_out:
        o_refs = refs[-2:]
        refs = refs[:-2]
    else:
        o_refs = refs[-1:]
        refs = refs[:-1]
    src_ref = refs[-1]
    if depth_layer is None:
        h = jnp.concatenate(
            [src_ref[:chans, :vol_cols], src_ref[chans:, :vol_cols]], axis=1
        )
    else:
        lo_ref, low_ref, high_ref, up_ref = refs[:4]
        low, high = low_ref[...], high_ref[...]
        stacked = jnp.concatenate(
            [
                jnp.concatenate([lo_ref[...], low], axis=1),
                jnp.concatenate([low, high], axis=1),
                jnp.concatenate([high, up_ref[...]], axis=1),
            ],
            axis=0,
        )
        rows = slice(depth_layer * chans, (depth_layer + 1) * chans)
        at = vol_cols + 2 * PLANE_COLS
        total = jnp.dot(src_ref[rows, at : at + 3 * chans], stacked, preferred_element_type=jnp.float32)
        h = jnp.maximum(total, 0.0).astype(jnp.bfloat16)
    if plane_layer is not None:
        ok = _masks(h.shape[1])
        rows = slice(plane_layer * chans, (plane_layer + 1) * chans)
        for k in range(2):
            at = vol_cols + k * PLANE_COLS
            w = src_ref[rows, at : at + 9 * chans]
            h = jnp.maximum(_plane(h, w, ok), 0.0).astype(jnp.bfloat16)
    half = h.shape[1] // 2
    if split_out:
        o_refs[0][...] = h[:, :half]
        o_refs[1][...] = h[:, half:]
    else:
        o_refs[0][...] = jnp.concatenate([h[:, :half], h[:, half:]], axis=0)


def layer_kernel(inputs, src, vol_cols, chans, depth_layer, plane_layer, split_out):
    half = jax.ShapeDtypeStruct((chans, vol_cols), jnp.bfloat16)
    out_shape = (half, half) if split_out else jax.ShapeDtypeStruct((2 * chans, vol_cols), jnp.bfloat16)
    return pl.pallas_call(
        functools.partial(
            _kernel,
            depth_layer=depth_layer,
            plane_layer=plane_layer,
            vol_cols=vol_cols,
            chans=chans,
            split_out=split_out,
        ),
        out_shape=out_shape,
    )(*inputs, src)


def shift_z(block, step):
    size = lax.axis_size("z")
    route = [(i, i + step) for i in range(size) if 0 <= i + step < size]
    return lax.ppermute(block, "z", route)


def local(volume, plane_a, plane_b, depth):
    layers, out_part, chans = plane_a.shape[:3]
    part, slab, flat = volume.shape
    members = lax.axis_size("yh") * lax.axis_size("ch")
    per = slab // members
    vol_cols = per * flat
    sent_volume = jnp.transpose(volume.reshape(part, members, per, flat), (1, 0, 2, 3))
    sent_volume = sent_volume.reshape(members, part, vol_cols)
    weights = pack_weights(plane_a, plane_b, depth)
    mine = lax.dynamic_index_in_dim(weights, lax.axis_index("yh"), 1, keepdims=False)
    sent_weights = jnp.broadcast_to(mine[None], (members,) + mine.shape)
    sent = jnp.concatenate([sent_volume, sent_weights], axis=2)
    got = lax.all_to_all(sent, GROUP, split_axis=0, concat_axis=0, tiled=True)
    src = got.reshape(2 * chans, -1)
    low, high = layer_kernel([], src, vol_cols, chans, None, 0, True)
    for layer_index in range(layers):
        below = shift_z(high, 1)
        above = shift_z(low, -1)
        last = layer_index + 1 == layers
        out = layer_kernel(
            [below, low, high, above],
            src,
            vol_cols,
            chans,
            layer_index,
            None if last else layer_index + 1,
            not last,
        )
        if not last:
            low, high = out
    h = lax.all_to_all(out.reshape(members, part, vol_cols), GROUP, split_axis=0, concat_axis=0, tiled=True)
    h = jnp.transpose(h.reshape(members, part, per, flat), (1, 0, 2, 3))
    return h.reshape(part, slab, flat)


def solution(mesh):
    slabs = mesh.shape["gz"]
    split = Mesh(
        mesh.devices.reshape(slabs // 4, 2, 2, mesh.shape["ch"]), ("z", "yh", "core", "ch")
    )
    return jax.shard_map(
        local,
        mesh=split,
        in_specs=(
            P("ch", SLAB, None),
            P(None, "ch", None, None, None),
            P(None, "ch", None, None, None),
            P(None, "ch", None, None),
        ),
        out_specs=P("ch", SLAB, None),
        check_vma=False,
    )
```

time: 79.2 us -> 72.5 us (0.915)
  waiting for transfers between devices: 21.3 us -> 10.7 us
  blocking collectives: 27.6 us -> 32.1 us
  starting transfers between devices: 14.2 us -> 12.8 us
    ppermute x4, waiting for transfers between devices: 21.3 us -> 10.7 us  [shift_z(): return lax.ppermute(block, 'z', route)]
    all_to_all x2, blocking collectives: 27.6 us -> 32.1 us  [the longest x1 19.9 us: local(): got = lax.all_to_all(sent, GROUP, split_axis=0, concat_axis=0, tiled=True)]
    ppermute x4, starting transfers between devices: 14.2 us -> 12.8 us  [shift_z(): return lax.ppermute(block, 'z', route)]
    reshape x3 -> x5, local copies, waits for them, and re-layouts: 0.95 us -> 2.27 us  [the longest x1 1.05 us: local(): volume.reshape(part, members, per, flat)]
    unnamed x11 -> x8, local copies, waits for them, and re-layouts: 1.65 us -> 1.32 us
    transpose x2 -> x3, local copies, waits for them, and re-layouts: 1.57 us -> 1.73 us  [the longest x1 0.79 us: pack_weights(): jnp.transpose(plane_b, (1, 0, 3, 4, 2)).reshape(out_part, layers, -1)]
where the time goes in v9:
time: 72.5 us; the launch traced here: 71.2 us
  blocking collectives  32.1 us (44%)
  starting transfers between devices  12.8 us (18%)
  waiting for transfers between devices  10.7 us (15%)
  Pallas kernels  9.38 us (13%)
  local copies, waits for them, and re-layouts  6.15 us (8%)
    all_to_all x1, blocking collectives, local(): got = lax.all_to_all(sent, GROUP, split_axis=0, concat_axis=0, tiled=True)  19.9 us
    ppermute x4, starting transfers between devices, shift_z(): return lax.ppermute(block, 'z', route)  12.8 us
    all_to_all x1, blocking collectives, local(): lax.all_to_all(out.reshape(members, part, vol_cols), GROUP, split_axis=0,...  12.2 us
    ppermute x4, waiting for transfers between devices, shift_z(): return lax.ppermute(block, 'z', route)  10.7 us
    pallas_call x3, Pallas kernels, layer_kernel(): pl.pallas_call(functools.partial(_kernel, depth_layer=depth_layer, plane_...  9.38 us
  transfers between devices with their start and end apart: 4, of which 4 were waited for; matrix products, arithmetic and copies ran while one was open for 0% of the time, Pallas kernels for 0%

profile of v9, /device:TPU:96, one launch (start us, length us, event | category | flops | bytes accessed | tf_op | source)
XLA Modules:
  0.0 71.2 jit_solution(10217449857121605812)
XLA Ops:
  0.0 0.7 %copy.10 = bf16[8,2,3,64]{3,2,0,1:T(4,128)(2,1)S(1)} copy(bf16[8,2,3,64]{3,0,2,1:T(8,128)(2,1)} %bitcast.29) | data formatting | bytes 12288 | tf_op jit(solution)/shard_map/transpose | solution.py:25
  0.7 0.1 reshape.33
  0.8 0.8 %copy.8 = bf16[8,2,3,3,64]{4,3,2,0,1:T(4,128)(2,1)S(1)} copy(bf16[8,2,3,3,64]{4,0,3,2,1:T(8,128)(2,1)} %bitcast.27) | data formatting | bytes 36864 | tf_op jit(solution)/shard_map/transpose | solution.py:23
  1.6 0.1 reshape.31
  1.7 0.8 %copy.9 = bf16[8,2,3,3,64]{4,3,2,0,1:T(4,128)(2,1)S(1)} copy(bf16[8,2,3,3,64]{4,0,3,2,1:T(8,128)(2,1)} %bitcast.28) | data formatting | bytes 36864 | tf_op jit(solution)/shard_map/transpose | solution.py:24
  2.5 0.1 reshape.32
  2.6 1.1 %reshape.29 = bf16[8,16,2,512]{3,2,1,0:T(2,128)(2,1)S(1)} reshape(bf16[8,32,512]{2,1,0:T(8,128)(2,1)} %param.4) | data formatting | bytes 524288 | tf_op jit(solution)/shard_map/reshape | solution.py:135
  3.7 0.2 copy.7
  3.9 19.9 %all_to_all.10 = bf16[16,8,2560]{2,1,0:T(8,128)(2,1)} all-to-all(bf16[16,8,2560]{2,1,0:T(8,128)(2,1)S(1)} %pad_maximum_fusion), channel_id=1, replica_groups=mesh['z'=8,'yh'=2,'core'=2,'ch'=8] {'yh','ch'}, dimensions={0} | all-to-all | bytes 1310720 | tf_op jit(solution)/shard_map/all_to_all | solution.py:141
  23.8 3.4 %shard_map.46 = (bf16[64,1024]{1,0:T(8,128)(2,1)}, bf16[64,1024]{1,0:T(8,128)(2,1)}) custom-call(bf16[128,2560]{1,0:T(8,128)(2,1)} %bitcast.19), custom_call_target="tpu_custom_call" | custom-call | tf_op jit(solution)/shard_map/pallas_call | solution.py:110
  27.2 5.0 %collective-permute-start = (bf16[64,1024]{1,0:T(8,128)(2,1)}, bf16[64,1024]{1,0:T(8,128)(2,1)S(1)}, u32[]{:S(2)}, u32[]{:S(2)}) collective-permute-start(bf16[64,1024]{1,0:T(8,128)(2,1)} %get-tuple-element.9.refs_2_), channel_id=1, source_target_pairs={{0,32},{32,64},{64,96},{96,128},{128,160},{160,192},{192,224},{1,3... | collective-permute-start | bytes 393224 | tf_op jit(solution)/shard_map/ppermute | solution.py:126
  32.2 1.9 %collective-permute-start.1 = (bf16[64,1024]{1,0:T(8,128)(2,1)}, bf16[64,1024]{1,0:T(8,128)(2,1)S(1)}, u32[]{:S(2)}, u32[]{:S(2)}) collective-permute-start(bf16[64,1024]{1,0:T(8,128)(2,1)} %get-tuple-element.10.refs_1_), channel_id=1, source_target_pairs={{32,0},{64,32},{96,64},{128,96},{160,128},{192,160},{224,192},{33,... | collective-permute-start | bytes 393224 | tf_op jit(solution)/shard_map/ppermute | solution.py:126
  34.1 0.9 %collective-permute-done.refs_0_ = bf16[64,1024]{1,0:T(8,128)(2,1)S(1)} collective-permute-done((bf16[64,1024]{1,0:T(8,128)(2,1)}, bf16[64,1024]{1,0:T(8,128)(2,1)S(1)}, u32[]{:S(2)}, u32[]{:S(2)}) %collective-permute-start) | collective-permute-done | bytes 131104 | tf_op jit(solution)/shard_map/ppermute | solution.py:126
  35.0 0.0 copy-start
  35.0 5.5 %collective-permute-done.1.refs_3_ = bf16[64,1024]{1,0:T(8,128)(2,1)S(1)} collective-permute-done((bf16[64,1024]{1,0:T(8,128)(2,1)}, bf16[64,1024]{1,0:T(8,128)(2,1)S(1)}, u32[]{:S(2)}, u32[]{:S(2)}) %collective-permute-start.1) | collective-permute-done | bytes 131104 | tf_op jit(solution)/shard_map/ppermute | solution.py:126
  40.5 0.0 copy-done
  40.5 0.0 copy-start.1
  40.5 0.7 copy-done.1
  41.1 3.7 %shard_map.47 = (bf16[64,1024]{1,0:T(8,128)(2,1)}, bf16[64,1024]{1,0:T(8,128)(2,1)}) custom-call(bf16[64,1024]{1,0:T(8,128)(2,1)} %copy-done, bf16[64,1024]{1,0:T(8,128)(2,1)} %get-tuple-element.10.refs_1_, bf16[64,1024]{1,0:T(8,128)(2,1)} %get-tuple-element.9.refs_2_, bf16[64,1024]{1,0:T(8,128)(2,1)} %copy-done.1, bf16[128,2560]{1,0:T(8,128)(2,1)} %bitcast.20), custom_call_target="tpu_custom_call" | custom-call | tf_op jit(solution)/shard_map/pallas_call | solution.py:110
  44.8 1.9 %collective-permute-start.2 = (bf16[64,1024]{1,0:T(8,128)(2,1)}, bf16[64,1024]{1,0:T(8,128)(2,1)S(1)}, u32[]{:S(2)}, u32[]{:S(2)}) collective-permute-start(bf16[64,1024]{1,0:T(8,128)(2,1)} %get-tuple-element.11.refs_2_), channel_id=1, source_target_pairs={{0,32},{32,64},{64,96},{96,128},{128,160},{160,192},{192,224},{1,3... | collective-permute-start | bytes 393224 | tf_op jit(solution)/shard_map/ppermute | solution.py:126
  46.8 3.9 %collective-permute-start.3 = (bf16[64,1024]{1,0:T(8,128)(2,1)}, bf16[64,1024]{1,0:T(8,128)(2,1)S(1)}, u32[]{:S(2)}, u32[]{:S(2)}) collective-permute-start(bf16[64,1024]{1,0:T(8,128)(2,1)} %get-tuple-element.12.refs_1_), channel_id=1, source_target_pairs={{32,0},{64,32},{96,64},{128,96},{160,128},{192,160},{224,192},{33,... | collective-permute-start | bytes 393224 | tf_op jit(solution)/shard_map/ppermute | solution.py:126
  50.7 1.2 %collective-permute-done.2.refs_0_ = bf16[64,1024]{1,0:T(8,128)(2,1)S(1)} collective-permute-done((bf16[64,1024]{1,0:T(8,128)(2,1)}, bf16[64,1024]{1,0:T(8,128)(2,1)S(1)}, u32[]{:S(2)}, u32[]{:S(2)}) %collective-permute-start.2) | collective-permute-done | bytes 131104 | tf_op jit(solution)/shard_map/ppermute | solution.py:126
  51.9 0.0 copy-start.2
  51.9 3.1 %collective-permute-done.3.refs_3_ = bf16[64,1024]{1,0:T(8,128)(2,1)S(1)} collective-permute-done((bf16[64,1024]{1,0:T(8,128)(2,1)}, bf16[64,1024]{1,0:T(8,128)(2,1)S(1)}, u32[]{:S(2)}, u32[]{:S(2)}) %collective-permute-start.3) | collective-permute-done | bytes 131104 | tf_op jit(solution)/shard_map/ppermute | solution.py:126
  55.0 0.0 copy-done.2
  55.0 0.0 copy-start.3
  55.0 0.7 copy-done.3
  55.7 2.3 %shard_map.48 = bf16[128,1024]{1,0:T(8,128)(2,1)} custom-call(bf16[64,1024]{1,0:T(8,128)(2,1)} %copy-done.2, bf16[64,1024]{1,0:T(8,128)(2,1)} %get-tuple-element.12.refs_1_, bf16[64,1024]{1,0:T(8,128)(2,1)} %get-tuple-element.11.refs_2_, bf16[64,1024]{1,0:T(8,128)(2,1)} %copy-done.3, bf16[128,2560]{1,0:T(8,128)(2,1)} %bitcast.21), custom_call_target="tpu_custom_call" | custom-call | tf_op jit(solution)/shard_map/pallas_call | solution.py:110
  58.0 12.2 %all_to_all.11 = bf16[16,8,1024]{2,1,0:T(8,128)(2,1)S(1)} all-to-all(bf16[16,8,1024]{2,1,0:T(8,128)(2,1)} %bitcast.26), channel_id=1, replica_groups=mesh['z'=8,'yh'=2,'core'=2,'ch'=8] {'yh','ch'}, dimensions={0} | all-to-all | bytes 524288 | tf_op jit(solution)/shard_map/all_to_all | solution.py:159
  70.2 0.2 copy.13
  70.4 0.8 %reshape.37 = bf16[8,32,512]{2,1,0:T(8,128)(2,1)} reshape(bf16[8,16,2,512]{3,2,1,0:T(2,128)(2,1)S(1)} %bitcast.24) | data formatting | bytes 524288 | tf_op jit(solution)/shard_map/reshape | solution.py:161
  (3 shorter events, 0.1 us)
Async XLA Ops:
  27.2 7.8 %collective-permute-start = (bf16[64,1024]{1,0:T(8,128)(2,1)}, bf16[64,1024]{1,0:T(8,128)(2,1)S(1)}, u32[]{:S(2)}, u32[]{:S(2)}) collective-permute-start(bf16[64,1024]{1,0:T(8,128)(2,1)} %get-tuple-element.9.refs_2_), channel_id=1, source_target_pairs={{0,32},{32,64},{64,96},{96,128},{128,160},{160,192},{192,224},{1,3... | collective-permute-start | bytes 393224 | tf_op jit(solution)/shard_map/ppermute | solution.py:126
  32.2 8.3 %collective-permute-start.1 = (bf16[64,1024]{1,0:T(8,128)(2,1)}, bf16[64,1024]{1,0:T(8,128)(2,1)S(1)}, u32[]{:S(2)}, u32[]{:S(2)}) collective-permute-start(bf16[64,1024]{1,0:T(8,128)(2,1)} %get-tuple-element.10.refs_1_), channel_id=1, source_target_pairs={{32,0},{64,32},{96,64},{128,96},{160,128},{192,160},{224,192},{33,... | collective-permute-start | bytes 393224 | tf_op jit(solution)/shard_map/ppermute | solution.py:126
  35.0 5.5 %copy-start = (bf16[64,1024]{1,0:T(8,128)(2,1)}, bf16[64,1024]{1,0:T(8,128)(2,1)S(1)}, u32[]{:S(2)}) copy-start(bf16[64,1024]{1,0:T(8,128)(2,1)S(1)} %collective-permute-done.refs_0_) | copy-start | bytes 393220
  40.5 0.7 copy-start.1
  44.8 7.1 %collective-permute-start.2 = (bf16[64,1024]{1,0:T(8,128)(2,1)}, bf16[64,1024]{1,0:T(8,128)(2,1)S(1)}, u32[]{:S(2)}, u32[]{:S(2)}) collective-permute-start(bf16[64,1024]{1,0:T(8,128)(2,1)} %get-tuple-element.11.refs_2_), channel_id=1, source_target_pairs={{0,32},{32,64},{64,96},{96,128},{128,160},{160,192},{192,224},{1,3... | collective-permute-start | bytes 393224 | tf_op jit(solution)/shard_map/ppermute | solution.py:126
  46.8 8.3 %collective-permute-start.3 = (bf16[64,1024]{1,0:T(8,128)(2,1)}, bf16[64,1024]{1,0:T(8,128)(2,1)S(1)}, u32[]{:S(2)}, u32[]{:S(2)}) collective-permute-start(bf16[64,1024]{1,0:T(8,128)(2,1)} %get-tuple-element.12.refs_1_), channel_id=1, source_target_pairs={{32,0},{64,32},{96,64},{128,96},{160,128},{192,160},{224,192},{33,... | collective-permute-start | bytes 393224 | tf_op jit(solution)/shard_map/ppermute | solution.py:126
  51.9 3.1 %copy-start.2 = (bf16[64,1024]{1,0:T(8,128)(2,1)}, bf16[64,1024]{1,0:T(8,128)(2,1)S(1)}, u32[]{:S(2)}) copy-start(bf16[64,1024]{1,0:T(8,128)(2,1)S(1)} %collective-permute-done.2.refs_0_) | copy-start | bytes 393220
  55.0 0.7 copy-start.3

commit v10 on v9

--- a/solution.py
+++ b/solution.py
@@ -120,6 +120,40 @@
     )(*inputs, src)
 
 
+def _half_kernel(*refs, depth_layer, plane_layer, vol_cols, chans, row_half):
+    src_ref, o_ref = refs[-2:]
+    if depth_layer is None:
+        h = src_ref[row_half * chans : (row_half + 1) * chans, :vol_cols]
+    else:
+        lo_ref, mid_ref, up_ref = refs[:3]
+        stacked = jnp.concatenate([lo_ref[...], mid_ref[...], up_ref[...]], axis=0)
+        rows = slice(depth_layer * chans, (depth_layer + 1) * chans)
+        at = vol_cols + 2 * PLANE_COLS
+        total = jnp.dot(src_ref[rows, at : at + 3 * chans], stacked, preferred_element_type=jnp.float32)
+        h = jnp.maximum(total, 0.0).astype(jnp.bfloat16)
+    ok = _masks(h.shape[1])
+    rows = slice(plane_layer * chans, (plane_layer + 1) * chans)
+    for k in range(2):
+        at = vol_cols + k * PLANE_COLS
+        w = src_ref[rows, at : at + 9 * chans]
+        h = jnp.maximum(_plane(h, w, ok), 0.0).astype(jnp.bfloat16)
+    o_ref[...] = h
+
+
+def half_kernel(inputs, src, vol_cols, chans, depth_layer, plane_layer, row_half=0):
+    return pl.pallas_call(
+        functools.partial(
+            _half_kernel,
+            depth_layer=depth_layer,
+            plane_layer=plane_layer,
+            vol_cols=vol_cols,
+            chans=chans,
+            row_half=row_half,
+        ),
+        out_shape=jax.ShapeDtypeStruct((chans, vol_cols), jnp.bfloat16),
+    )(*inputs, src)
+
+
 def shift_z(block, step):
     size = lax.axis_size("z")
     route = [(i, i + step) for i in range(size) if 0 <= i + step < size]
@@ -140,22 +174,19 @@
     sent = jnp.concatenate([sent_volume, sent_weights], axis=2)
     got = lax.all_to_all(sent, GROUP, split_axis=0, concat_axis=0, tiled=True)
     src = got.reshape(2 * chans, -1)
-    low, high = layer_kernel([], src, vol_cols, chans, None, 0, True)
-    for layer_index in range(layers):
+    high = half_kernel([], src, vol_cols, chans, None, 0, 1)
+    below = shift_z(high, 1)
+    low = half_kernel([], src, vol_cols, chans, None, 0, 0)
+    above = shift_z(low, -1)
+    for layer_index in range(layers - 1):
+        new_low = half_kernel([below, low, high], src, vol_cols, chans, layer_index, layer_index + 1)
+        new_high = half_kernel([low, high, above], src, vol_cols, chans, layer_index, layer_index + 1)
+        low, high = new_low, new_high
         below = shift_z(high, 1)
         above = shift_z(low, -1)
-        last = layer_index + 1 == layers
-        out = layer_kernel(
-            [below, low, high, above],
-            src,
-            vol_cols,
-            chans,
-            layer_index,
-            None if last else layer_index + 1,
-            not last,
-        )
-        if not last:
-            low, high = out
+    out = layer_kernel(
+        [below, low, high, above], src, vol_cols, chans, layers - 1, None, False
+    )
     h = lax.all_to_all(out.reshape(members, part, vol_cols), GROUP, split_axis=0, concat_axis=0, tiled=True)
     h = jnp.transpose(h.reshape(members, part, per, flat), (1, 0, 2, 3))
     return h.reshape(part, slab, flat)

time: 72.5 us -> 72.5 us (level)
  waiting for transfers between devices: 10.7 us -> 6.25 us
  Pallas kernels: 9.38 us -> 13.7 us
    pallas_call x0 -> x4, Pallas kernels: none -> 11.4 us  [half_kernel(): pl.pallas_call(functools.partial(_half_kernel, depth_layer=depth_layer, p...]
    pallas_call x3 -> x1, Pallas kernels: 9.38 us -> 2.32 us  [layer_kernel(): pl.pallas_call(functools.partial(_kernel, depth_layer=depth_layer, plane_...]
    ppermute x4, waiting for transfers between devices: 10.7 us -> 6.25 us  [shift_z(): return lax.ppermute(block, 'z', route)]
  transfers between devices with their start and end apart: 4 -> 4, of which waited for: 4 -> 1; matrix products, arithmetic and copies ran while one was open for 0% -> 0% of each run, Pallas kernels for 0% -> 12%
where the time goes in v10:
time: 72.5 us; the launch traced here: 71.9 us
  blocking collectives  32.1 us (44%)
  Pallas kernels  13.7 us (19%)
  starting transfers between devices  12.8 us (18%)
  local copies, waits for them, and re-layouts  6.79 us (9%)
  waiting for transfers between devices  6.25 us (9%)
    all_to_all x1, blocking collectives, local(): got = lax.all_to_all(sent, GROUP, split_axis=0, concat_axis=0, tiled=True)  19.9 us
    ppermute x4, starting transfers between devices, shift_z(): return lax.ppermute(block, 'z', route)  12.8 us
    all_to_all x1, blocking collectives, local(): lax.all_to_all(out.reshape(members, part, vol_cols), GROUP, split_axis=0,...  12.2 us
    pallas_call x4, Pallas kernels, half_kernel(): pl.pallas_call(functools.partial(_half_kernel, depth_layer=depth_layer, p...  11.4 us
    ppermute x4, waiting for transfers between devices, shift_z(): return lax.ppermute(block, 'z', route)  6.25 us
    pallas_call x1, Pallas kernels, layer_kernel(): pl.pallas_call(functools.partial(_kernel, depth_layer=depth_layer, plane_...  2.32 us
    unnamed x8, local copies, waits for them, and re-layouts  1.96 us
  transfers between devices with their start and end apart: 4, of which 1 were waited for; matrix products, arithmetic and copies ran while one was open for 0% of the time, Pallas kernels for 12%

profile of v10, /device:TPU:96, one launch (start us, length us, event | category | flops | bytes accessed | tf_op | source)
XLA Modules:
  0.0 71.9 jit_solution(921837802019647983)
XLA Ops:
  0.0 0.7 copy.10
  0.7 0.1 reshape.33
  0.8 0.8 %copy.8 = bf16[8,2,3,3,64]{4,3,2,0,1:T(4,128)(2,1)S(1)} copy(bf16[8,2,3,3,64]{4,0,3,2,1:T(8,128)(2,1)} %bitcast.29) | data formatting | bytes 36864 | tf_op jit(solution)/shard_map/transpose | solution.py:23
  1.6 0.1 reshape.31
  1.7 0.8 %copy.9 = bf16[8,2,3,3,64]{4,3,2,0,1:T(4,128)(2,1)S(1)} copy(bf16[8,2,3,3,64]{4,0,3,2,1:T(8,128)(2,1)} %bitcast.30) | data formatting | bytes 36864 | tf_op jit(solution)/shard_map/transpose | solution.py:24
  2.5 0.1 reshape.32
  2.6 1.1 %reshape.29 = bf16[8,16,2,512]{3,2,1,0:T(2,128)(2,1)S(1)} reshape(bf16[8,32,512]{2,1,0:T(8,128)(2,1)} %param.4) | data formatting | bytes 524288 | tf_op jit(solution)/shard_map/reshape | solution.py:169
  3.7 0.2 copy.7
  3.9 19.9 %all_to_all.10 = bf16[16,8,2560]{2,1,0:T(8,128)(2,1)} all-to-all(bf16[16,8,2560]{2,1,0:T(8,128)(2,1)S(1)} %pad_maximum_fusion), channel_id=1, replica_groups=mesh['z'=8,'yh'=2,'core'=2,'ch'=8] {'yh','ch'}, dimensions={0} | all-to-all | bytes 1310720 | tf_op jit(solution)/shard_map/all_to_all | solution.py:175
  23.8 2.7 %shard_map.46.refs_0_.refs_1_ = bf16[64,1024]{1,0:T(8,128)(2,1)} custom-call(bf16[128,2560]{1,0:T(8,128)(2,1)} %bitcast.19), custom_call_target="tpu_custom_call" | custom-call | tf_op jit(solution)/shard_map/pallas_call | solution.py:144
  26.5 2.0 %collective-permute-start = (bf16[64,1024]{1,0:T(8,128)(2,1)}, bf16[64,1024]{1,0:T(8,128)(2,1)S(1)}, u32[]{:S(2)}, u32[]{:S(2)}) collective-permute-start(bf16[64,1024]{1,0:T(8,128)(2,1)} %shard_map.46.refs_0_.refs_1_), channel_id=1, source_target_pairs={{32,0},{64,32},{96,64},{128,96},{160,128},{192,160},{224,192},{33,... | collective-permute-start | bytes 393224 | tf_op jit(solution)/shard_map/ppermute | solution.py:160
  28.5 2.7 %shard_map.47.refs_1_.refs_2_ = bf16[64,1024]{1,0:T(8,128)(2,1)} custom-call(bf16[128,2560]{1,0:T(8,128)(2,1)} %bitcast.20), custom_call_target="tpu_custom_call" | custom-call | tf_op jit(solution)/shard_map/pallas_call | solution.py:144
  31.2 5.0 %collective-permute-start.2 = (bf16[64,1024]{1,0:T(8,128)(2,1)}, bf16[64,1024]{1,0:T(8,128)(2,1)S(1)}, u32[]{:S(2)}, u32[]{:S(2)}) collective-permute-start(bf16[64,1024]{1,0:T(8,128)(2,1)} %shard_map.47.refs_1_.refs_2_), channel_id=1, source_target_pairs={{0,32},{32,64},{64,96},{96,128},{128,160},{160,192},{192,224},{1,3... | collective-permute-start | bytes 393224 | tf_op jit(solution)/shard_map/ppermute | solution.py:160
  36.3 0.0 collective-permute-done.refs_2_
  36.3 0.0 copy-start.1
  36.3 0.7 copy-done.1
  36.9 3.0 %shard_map.48.refs_2_ = bf16[64,1024]{1,0:T(8,128)(2,1)} custom-call(bf16[64,1024]{1,0:T(8,128)(2,1)} %shard_map.46.refs_0_.refs_1_, bf16[64,1024]{1,0:T(8,128)(2,1)} %shard_map.47.refs_1_.refs_2_, bf16[64,1024]{1,0:T(8,128)(2,1)} %copy-done.1, bf16[128,2560]{1,0:T(8,128)(2,1)} %bitcast.21), custom_call_target="tpu_custom_call" | custom-call | tf_op jit(solution)/shard_map/pallas_call | solution.py:144
  39.9 3.8 %collective-permute-start.1 = (bf16[64,1024]{1,0:T(8,128)(2,1)}, bf16[64,1024]{1,0:T(8,128)(2,1)S(1)}, u32[]{:S(2)}, u32[]{:S(2)}) collective-permute-start(bf16[64,1024]{1,0:T(8,128)(2,1)} %shard_map.48.refs_2_), channel_id=1, source_target_pairs={{0,32},{32,64},{64,96},{96,128},{128,160},{160,192},{192,224},{1,3... | collective-permute-start | bytes 393224 | tf_op jit(solution)/shard_map/ppermute | solution.py:160
  43.8 0.0 collective-permute-done.2.refs_0_
  43.8 0.0 copy-start
  43.8 0.6 copy-done
  44.4 3.0 %shard_map.49.refs_1_ = bf16[64,1024]{1,0:T(8,128)(2,1)} custom-call(bf16[64,1024]{1,0:T(8,128)(2,1)} %copy-done, bf16[64,1024]{1,0:T(8,128)(2,1)} %shard_map.46.refs_0_.refs_1_, bf16[64,1024]{1,0:T(8,128)(2,1)} %shard_map.47.refs_1_.refs_2_, bf16[128,2560]{1,0:T(8,128)(2,1)} %bitcast.22), custom_call_target="tpu_custom_call" | custom-call | tf_op jit(solution)/shard_map/pallas_call | solution.py:144
  47.4 2.0 %collective-permute-start.3 = (bf16[64,1024]{1,0:T(8,128)(2,1)}, bf16[64,1024]{1,0:T(8,128)(2,1)S(1)}, u32[]{:S(2)}, u32[]{:S(2)}) collective-permute-start(bf16[64,1024]{1,0:T(8,128)(2,1)} %shard_map.49.refs_1_), channel_id=1, source_target_pairs={{32,0},{64,32},{96,64},{128,96},{160,128},{192,160},{224,192},{33,... | collective-permute-start | bytes 393224 | tf_op jit(solution)/shard_map/ppermute | solution.py:160
  49.4 0.0 collective-permute-done.1.refs_0_
  49.4 0.0 copy-start.2
  49.5 6.2 %collective-permute-done.3.refs_3_ = bf16[64,1024]{1,0:T(8,128)(2,1)S(1)} collective-permute-done((bf16[64,1024]{1,0:T(8,128)(2,1)}, bf16[64,1024]{1,0:T(8,128)(2,1)S(1)}, u32[]{:S(2)}, u32[]{:S(2)}) %collective-permute-start.3) | collective-permute-done | bytes 131104 | tf_op jit(solution)/shard_map/ppermute | solution.py:160
  55.7 0.0 copy-done.2
  55.7 0.7 copy-done.3
  56.4 2.3 %shard_map.50 = bf16[128,1024]{1,0:T(8,128)(2,1)} custom-call(bf16[64,1024]{1,0:T(8,128)(2,1)} %copy-done.2, bf16[64,1024]{1,0:T(8,128)(2,1)} %shard_map.49.refs_1_, bf16[64,1024]{1,0:T(8,128)(2,1)} %shard_map.48.refs_2_, bf16[64,1024]{1,0:T(8,128)(2,1)} %copy-done.3, bf16[128,2560]{1,0:T(8,128)(2,1)} %bitcast.23), custom_call_target="tpu_custom_call" | custom-call | tf_op jit(solution)/shard_map/pallas_call | solution.py:110
  58.7 12.2 %all_to_all.11 = bf16[16,8,1024]{2,1,0:T(8,128)(2,1)S(1)} all-to-all(bf16[16,8,1024]{2,1,0:T(8,128)(2,1)} %bitcast.28), channel_id=1, replica_groups=mesh['z'=8,'yh'=2,'core'=2,'ch'=8] {'yh','ch'}, dimensions={0} | all-to-all | bytes 524288 | tf_op jit(solution)/shard_map/all_to_all | solution.py:190
  70.8 0.2 copy.13
  71.1 0.8 %reshape.37 = bf16[8,32,512]{2,1,0:T(8,128)(2,1)} reshape(bf16[8,16,2,512]{3,2,1,0:T(2,128)(2,1)S(1)} %bitcast.26) | data formatting | bytes 524288 | tf_op jit(solution)/shard_map/reshape | solution.py:192
  (4 shorter events, 0.1 us)
Async XLA Ops:
  26.5 9.7 %collective-permute-start = (bf16[64,1024]{1,0:T(8,128)(2,1)}, bf16[64,1024]{1,0:T(8,128)(2,1)S(1)}, u32[]{:S(2)}, u32[]{:S(2)}) collective-permute-start(bf16[64,1024]{1,0:T(8,128)(2,1)} %shard_map.46.refs_0_.refs_1_), channel_id=1, source_target_pairs={{32,0},{64,32},{96,64},{128,96},{160,128},{192,160},{224,192},{33,... | collective-permute-start | bytes 393224 | tf_op jit(solution)/shard_map/ppermute | solution.py:160
  31.2 12.5 %collective-permute-start.2 = (bf16[64,1024]{1,0:T(8,128)(2,1)}, bf16[64,1024]{1,0:T(8,128)(2,1)S(1)}, u32[]{:S(2)}, u32[]{:S(2)}) collective-permute-start(bf16[64,1024]{1,0:T(8,128)(2,1)} %shard_map.47.refs_1_.refs_2_), channel_id=1, source_target_pairs={{0,32},{32,64},{64,96},{96,128},{128,160},{160,192},{192,224},{1,3... | collective-permute-start | bytes 393224 | tf_op jit(solution)/shard_map/ppermute | solution.py:160
  36.3 0.7 copy-start.1
  39.9 9.5 %collective-permute-start.1 = (bf16[64,1024]{1,0:T(8,128)(2,1)}, bf16[64,1024]{1,0:T(8,128)(2,1)S(1)}, u32[]{:S(2)}, u32[]{:S(2)}) collective-permute-start(bf16[64,1024]{1,0:T(8,128)(2,1)} %shard_map.48.refs_2_), channel_id=1, source_target_pairs={{0,32},{32,64},{64,96},{96,128},{128,160},{160,192},{192,224},{1,3... | collective-permute-start | bytes 393224 | tf_op jit(solution)/shard_map/ppermute | solution.py:160
  43.8 0.7 copy-start
  47.4 8.3 %collective-permute-start.3 = (bf16[64,1024]{1,0:T(8,128)(2,1)}, bf16[64,1024]{1,0:T(8,128)(2,1)S(1)}, u32[]{:S(2)}, u32[]{:S(2)}) collective-permute-start(bf16[64,1024]{1,0:T(8,128)(2,1)} %shard_map.49.refs_1_), channel_id=1, source_target_pairs={{32,0},{64,32},{96,64},{128,96},{160,128},{192,160},{224,192},{33,... | collective-permute-start | bytes 393224 | tf_op jit(solution)/shard_map/ppermute | solution.py:160
  49.4 6.3 %copy-start.2 = (bf16[64,1024]{1,0:T(8,128)(2,1)}, bf16[64,1024]{1,0:T(8,128)(2,1)S(1)}, u32[]{:S(2)}) copy-start(bf16[64,1024]{1,0:T(8,128)(2,1)S(1)} %collective-permute-done.1.refs_0_) | copy-start | bytes 393220
  55.7 0.7 copy-start.3

commit v11 on v9

--- a/solution.py
+++ b/solution.py
@@ -62,62 +62,80 @@
     return jnp.dot(w, stacked, preferred_element_type=jnp.float32)
 
 
-def _kernel(*refs, depth_layer, plane_layer, vol_cols, chans, split_out):
-    if split_out:
-        o_refs = refs[-2:]
-        refs = refs[:-2]
-    else:
-        o_refs = refs[-1:]
-        refs = refs[:-1]
-    src_ref = refs[-1]
-    if depth_layer is None:
-        h = jnp.concatenate(
-            [src_ref[:chans, :vol_cols], src_ref[chans:, :vol_cols]], axis=1
-        )
-    else:
-        lo_ref, low_ref, high_ref, up_ref = refs[:4]
-        low, high = low_ref[...], high_ref[...]
-        stacked = jnp.concatenate(
-            [
+W_COLS = 2 * PLANE_COLS + DEPTH_COLS
+PIECE = 512
+
+
+def _kernel(*refs, depth, planes, stack_out):
+    refs = list(refs)
+    o_ref = refs.pop()
+    if planes:
+        wp_ref = refs.pop()
+    if depth:
+        wd_ref = refs.pop()
+        if len(refs) == 4:
+            lo_ref, low_ref, high_ref, up_ref = refs
+            low, high = low_ref[...], high_ref[...]
+            parts = [
                 jnp.concatenate([lo_ref[...], low], axis=1),
                 jnp.concatenate([low, high], axis=1),
                 jnp.concatenate([high, up_ref[...]], axis=1),
-            ],
-            axis=0,
-        )
-        rows = slice(depth_layer * chans, (depth_layer + 1) * chans)
-        at = vol_cols + 2 * PLANE_COLS
-        total = jnp.dot(src_ref[rows, at : at + 3 * chans], stacked, preferred_element_type=jnp.float32)
+            ]
+        else:
+            parts = [r[...] for r in refs]
+        chans = parts[0].shape[0]
+        stacked = jnp.concatenate(parts, axis=0)
+        total = jnp.dot(wd_ref[:, : 3 * chans], stacked, preferred_element_type=jnp.float32)
         h = jnp.maximum(total, 0.0).astype(jnp.bfloat16)
-    if plane_layer is not None:
+    else:
+        h = jnp.concatenate([r[...] for r in refs], axis=1)
+    if planes:
         ok = _masks(h.shape[1])
-        rows = slice(plane_layer * chans, (plane_layer + 1) * chans)
+        chans = h.shape[0]
         for k in range(2):
-            at = vol_cols + k * PLANE_COLS
-            w = src_ref[rows, at : at + 9 * chans]
+            w = wp_ref[:, k * PLANE_COLS : k * PLANE_COLS + 9 * chans]
             h = jnp.maximum(_plane(h, w, ok), 0.0).astype(jnp.bfloat16)
-    half = h.shape[1] // 2
-    if split_out:
-        o_refs[0][...] = h[:, :half]
-        o_refs[1][...] = h[:, half:]
+    if stack_out:
+        half = h.shape[1] // 2
+        o_ref[...] = jnp.concatenate([h[:, :half], h[:, half:]], axis=0)
     else:
-        o_refs[0][...] = jnp.concatenate([h[:, :half], h[:, half:]], axis=0)
+        o_ref[...] = h
 
 
-def layer_kernel(inputs, src, vol_cols, chans, depth_layer, plane_layer, split_out):
-    half = jax.ShapeDtypeStruct((chans, vol_cols), jnp.bfloat16)
-    out_shape = (half, half) if split_out else jax.ShapeDtypeStruct((2 * chans, vol_cols), jnp.bfloat16)
+def layer_kernel(inputs, src, vol_cols, chans, depth_layer=None, plane_layer=None, row_half=0, stack_out=False):
+    specs, args = [], []
+    if depth_layer is None:
+        for j in range(vol_cols // PIECE):
+            specs.append(pl.BlockSpec((chans, PIECE), lambda i, j=j: (row_half, W_COLS // PIECE + j)))
+            args.append(src)
+        width = vol_cols
+    else:
+        specs += [pl.BlockSpec(inp.shape, lambda i: (0, 0)) for inp in inputs]
+        args += list(inputs)
+        width = inputs[1].shape[1] * (2 if len(inputs) == 4 else 1)
+        specs.append(
+            pl.BlockSpec((chans, DEPTH_COLS), lambda i: (depth_layer, 2 * PLANE_COLS // DEPTH_COLS))
+        )
+        args.append(src)
+    if plane_layer is not None:
+        specs.append(pl.BlockSpec((chans, 2 * PLANE_COLS), lambda i: (plane_layer, 0)))
+        args.append(src)
+    if stack_out:
+        out_shape = jax.ShapeDtypeStruct((2 * chans, width // 2), jnp.bfloat16)
+    else:
+        out_shape = jax.ShapeDtypeStruct((chans, width), jnp.bfloat16)
     return pl.pallas_call(
         functools.partial(
             _kernel,
-            depth_layer=depth_layer,
-            plane_layer=plane_layer,
-            vol_cols=vol_cols,
-            chans=chans,
-            split_out=split_out,
+            depth=depth_layer is not None,
+            planes=plane_layer is not None,
+            stack_out=stack_out,
         ),
         out_shape=out_shape,
-    )(*inputs, src)
+        in_specs=specs,
+        out_specs=pl.BlockSpec(out_shape.shape, lambda i: (0, 0)),
+        grid=(1,),
+    )(*args)
 
 
 def shift_z(block, step):
@@ -137,25 +155,22 @@
     weights = pack_weights(plane_a, plane_b, depth)
     mine = lax.dynamic_index_in_dim(weights, lax.axis_index("yh"), 1, keepdims=False)
     sent_weights = jnp.broadcast_to(mine[None], (members,) + mine.shape)
-    sent = jnp.concatenate([sent_volume, sent_weights], axis=2)
+    sent = jnp.concatenate([sent_weights, sent_volume], axis=2)
     got = lax.all_to_all(sent, GROUP, split_axis=0, concat_axis=0, tiled=True)
     src = got.reshape(2 * chans, -1)
-    low, high = layer_kernel([], src, vol_cols, chans, None, 0, True)
-    for layer_index in range(layers):
+    high = layer_kernel([], src, vol_cols, chans, None, 0, 1)
+    below = shift_z(high, 1)
+    low = layer_kernel([], src, vol_cols, chans, None, 0, 0)
+    above = shift_z(low, -1)
+    for layer_index in range(layers - 1):
+        new_low = layer_kernel([below, low, high], src, vol_cols, chans, layer_index, layer_index + 1)
+        new_high = layer_kernel([low, high, above], src, vol_cols, chans, layer_index, layer_index + 1)
+        low, high = new_low, new_high
         below = shift_z(high, 1)
         above = shift_z(low, -1)
-        last = layer_index + 1 == layers
-        out = layer_kernel(
-            [below, low, high, above],
-            src,
-            vol_cols,
-            chans,
-            layer_index,
-            None if last else layer_index + 1,
-            not last,
-        )
-        if not last:
-            low, high = out
+    out = layer_kernel(
+        [below, low, high, above], src, vol_cols, chans, layers - 1, None, stack_out=True
+    )
     h = lax.all_to_all(out.reshape(members, part, vol_cols), GROUP, split_axis=0, concat_axis=0, tiled=True)
     h = jnp.transpose(h.reshape(members, part, per, flat), (1, 0, 2, 3))
     return h.reshape(part, slab, flat)

time: 72.5 us -> 71.7 us (0.989)
  waiting for transfers between devices: 10.7 us -> 6.25 us
  Pallas kernels: 9.38 us -> 12.9 us
    ppermute x4, waiting for transfers between devices: 10.7 us -> 6.25 us  [shift_z(): return lax.ppermute(block, 'z', route)]
    pallas_call x3 -> x5, Pallas kernels: 9.38 us -> 12.9 us  [layer_kernel(): pl.pallas_call(functools.partial(_kernel, depth=depth_layer is not None,...]
  transfers between devices with their start and end apart: 4 -> 4, of which waited for: 4 -> 1; matrix products, arithmetic and copies ran while one was open for 0% -> 0% of each run, Pallas kernels for 0% -> 12%
where the time goes in v11:
time: 71.7 us; the launch traced here: 71.1 us
  blocking collectives  32.1 us (45%)
  Pallas kernels  12.9 us (18%)
  starting transfers between devices  12.8 us (18%)
  local copies, waits for them, and re-layouts  6.79 us (9%)
  waiting for transfers between devices  6.25 us (9%)
    all_to_all x1, blocking collectives, local(): got = lax.all_to_all(sent, GROUP, split_axis=0, concat_axis=0, tiled=True)  19.9 us
    pallas_call x5, Pallas kernels, layer_kernel(): pl.pallas_call(functools.partial(_kernel, depth=depth_layer is not None,...  12.9 us
    ppermute x4, starting transfers between devices, shift_z(): return lax.ppermute(block, 'z', route)  12.8 us
    all_to_all x1, blocking collectives, local(): lax.all_to_all(out.reshape(members, part, vol_cols), GROUP, split_axis=0,...  12.2 us
    ppermute x4, waiting for transfers between devices, shift_z(): return lax.ppermute(block, 'z', route)  6.25 us
    unnamed x8, local copies, waits for them, and re-layouts  1.96 us
  transfers between devices with their start and end apart: 4, of which 1 were waited for; matrix products, arithmetic and copies ran while one was open for 0% of the time, Pallas kernels for 12%

profile of v11, /device:TPU:96, one launch (start us, length us, event | category | flops | bytes accessed | tf_op | source)
XLA Modules:
  0.0 71.1 jit_solution(15093859628729504638)
XLA Ops:
  0.0 0.7 %copy.9 = bf16[8,2,3,64]{3,2,0,1:T(4,128)(2,1)S(1)} copy(bf16[8,2,3,64]{3,0,2,1:T(8,128)(2,1)} %bitcast.37) | data formatting | bytes 12288 | tf_op jit(solution)/shard_map/transpose | solution.py:25
  0.7 0.1 reshape.31
  0.8 0.8 %copy.7 = bf16[8,2,3,3,64]{4,3,2,0,1:T(4,128)(2,1)S(1)} copy(bf16[8,2,3,3,64]{4,0,3,2,1:T(8,128)(2,1)} %bitcast.35) | data formatting | bytes 36864 | tf_op jit(solution)/shard_map/transpose | solution.py:23
  1.6 0.1 reshape.29
  1.7 0.8 %copy.8 = bf16[8,2,3,3,64]{4,3,2,0,1:T(4,128)(2,1)S(1)} copy(bf16[8,2,3,3,64]{4,0,3,2,1:T(8,128)(2,1)} %bitcast.36) | data formatting | bytes 36864 | tf_op jit(solution)/shard_map/transpose | solution.py:24
  2.5 0.1 reshape.30
  2.6 1.1 %reshape.32 = bf16[8,16,2,512]{3,2,1,0:T(2,128)(2,1)S(1)} reshape(bf16[8,32,512]{2,1,0:T(8,128)(2,1)} %param.4) | data formatting | bytes 524288 | tf_op jit(solution)/shard_map/reshape | solution.py:153
  3.7 0.2 copy.10
  3.9 19.9 %all_to_all.10 = bf16[16,8,2560]{2,1,0:T(8,128)(2,1)} all-to-all(bf16[16,8,2560]{2,1,0:T(8,128)(2,1)S(1)} %pad_maximum_fusion), channel_id=1, replica_groups=mesh['z'=8,'yh'=2,'core'=2,'ch'=8] {'yh','ch'}, dimensions={0} | all-to-all | bytes 1310720 | tf_op jit(solution)/shard_map/all_to_all | solution.py:159
  23.8 2.6 %shard_map.46.refs_0_.refs_1_ = bf16[64,1024]{1,0:T(8,128)(2,1)} custom-call(bf16[128,2560]{1,0:T(8,128)(2,1)} %bitcast.19, bf16[128,2560]{1,0:T(8,128)(2,1)} %bitcast.20, bf16[128,2560]{1,0:T(8,128)(2,1)} %bitcast.21), custom_call_target="tpu_custom_call" | custom-call | tf_op jit(solution)/shard_map/pallas_call | solution.py:127
  26.4 2.0 %collective-permute-start = (bf16[64,1024]{1,0:T(8,128)(2,1)}, bf16[64,1024]{1,0:T(8,128)(2,1)S(1)}, u32[]{:S(2)}, u32[]{:S(2)}) collective-permute-start(bf16[64,1024]{1,0:T(8,128)(2,1)} %shard_map.46.refs_0_.refs_1_), channel_id=1, source_target_pairs={{32,0},{64,32},{96,64},{128,96},{160,128},{192,160},{224,192},{33,... | collective-permute-start | bytes 393224 | tf_op jit(solution)/shard_map/ppermute | solution.py:144
  28.4 2.6 %shard_map.47.refs_1_.refs_2_ = bf16[64,1024]{1,0:T(8,128)(2,1)} custom-call(bf16[128,2560]{1,0:T(8,128)(2,1)} %bitcast.22, bf16[128,2560]{1,0:T(8,128)(2,1)} %bitcast.23, bf16[128,2560]{1,0:T(8,128)(2,1)} %bitcast.24), custom_call_target="tpu_custom_call" | custom-call | tf_op jit(solution)/shard_map/pallas_call | solution.py:127
  31.0 5.0 %collective-permute-start.2 = (bf16[64,1024]{1,0:T(8,128)(2,1)}, bf16[64,1024]{1,0:T(8,128)(2,1)S(1)}, u32[]{:S(2)}, u32[]{:S(2)}) collective-permute-start(bf16[64,1024]{1,0:T(8,128)(2,1)} %shard_map.47.refs_1_.refs_2_), channel_id=1, source_target_pairs={{0,32},{32,64},{64,96},{96,128},{128,160},{160,192},{192,224},{1,3... | collective-permute-start | bytes 393224 | tf_op jit(solution)/shard_map/ppermute | solution.py:144
  36.1 0.0 collective-permute-done.refs_2_
  36.1 0.0 copy-start.1
  36.1 0.7 copy-done.1
  36.7 2.8 %shard_map.48.refs_2_ = bf16[64,1024]{1,0:T(8,128)(2,1)} custom-call(bf16[64,1024]{1,0:T(8,128)(2,1)} %shard_map.46.refs_0_.refs_1_, bf16[64,1024]{1,0:T(8,128)(2,1)} %shard_map.47.refs_1_.refs_2_, bf16[64,1024]{1,0:T(8,128)(2,1)} %copy-done.1, bf16[128,2560]{1,0:T(8,128)(2,1)} %bitcast.25, bf16[128,2560]{1,0:T(8,128)(2,1)} %bitcast.26), custom_call_target="tpu_custom_call" | custom-call | tf_op jit(solution)/shard_map/pallas_call | solution.py:127
  39.6 3.8 %collective-permute-start.1 = (bf16[64,1024]{1,0:T(8,128)(2,1)}, bf16[64,1024]{1,0:T(8,128)(2,1)S(1)}, u32[]{:S(2)}, u32[]{:S(2)}) collective-permute-start(bf16[64,1024]{1,0:T(8,128)(2,1)} %shard_map.48.refs_2_), channel_id=1, source_target_pairs={{0,32},{32,64},{64,96},{96,128},{128,160},{160,192},{192,224},{1,3... | collective-permute-start | bytes 393224 | tf_op jit(solution)/shard_map/ppermute | solution.py:144
  43.4 0.0 collective-permute-done.2.refs_0_
  43.4 0.0 copy-start
  43.4 0.6 copy-done
  44.1 2.8 %shard_map.49.refs_1_ = bf16[64,1024]{1,0:T(8,128)(2,1)} custom-call(bf16[64,1024]{1,0:T(8,128)(2,1)} %copy-done, bf16[64,1024]{1,0:T(8,128)(2,1)} %shard_map.46.refs_0_.refs_1_, bf16[64,1024]{1,0:T(8,128)(2,1)} %shard_map.47.refs_1_.refs_2_, bf16[128,2560]{1,0:T(8,128)(2,1)} %bitcast.27, bf16[128,2560]{1,0:T(8,128)(2,1)} %bitcast.28), custom_call_target="tpu_custom_call" | custom-call | tf_op jit(solution)/shard_map/pallas_call | solution.py:127
  46.9 2.0 %collective-permute-start.3 = (bf16[64,1024]{1,0:T(8,128)(2,1)}, bf16[64,1024]{1,0:T(8,128)(2,1)S(1)}, u32[]{:S(2)}, u32[]{:S(2)}) collective-permute-start(bf16[64,1024]{1,0:T(8,128)(2,1)} %shard_map.49.refs_1_), channel_id=1, source_target_pairs={{32,0},{64,32},{96,64},{128,96},{160,128},{192,160},{224,192},{33,... | collective-permute-start | bytes 393224 | tf_op jit(solution)/shard_map/ppermute | solution.py:144
  48.9 0.0 collective-permute-done.1.refs_0_
  48.9 0.0 copy-start.2
  48.9 6.2 %collective-permute-done.3.refs_3_ = bf16[64,1024]{1,0:T(8,128)(2,1)S(1)} collective-permute-done((bf16[64,1024]{1,0:T(8,128)(2,1)}, bf16[64,1024]{1,0:T(8,128)(2,1)S(1)}, u32[]{:S(2)}, u32[]{:S(2)}) %collective-permute-start.3) | collective-permute-done | bytes 131104 | tf_op jit(solution)/shard_map/ppermute | solution.py:144
  55.2 0.0 copy-done.2
  55.2 0.7 copy-done.3
  55.8 2.1 %shard_map.50 = bf16[128,1024]{1,0:T(8,128)(2,1)} custom-call(bf16[64,1024]{1,0:T(8,128)(2,1)} %copy-done.2, bf16[64,1024]{1,0:T(8,128)(2,1)} %shard_map.49.refs_1_, bf16[64,1024]{1,0:T(8,128)(2,1)} %shard_map.48.refs_2_, bf16[64,1024]{1,0:T(8,128)(2,1)} %copy-done.3, bf16[128,2560]{1,0:T(8,128)(2,1)} %bitcast.29), custom_call_target="tpu_custom_call" | custom-call | tf_op jit(solution)/shard_map/pallas_call | solution.py:127
  57.9 12.2 %all_to_all.11 = bf16[16,8,1024]{2,1,0:T(8,128)(2,1)S(1)} all-to-all(bf16[16,8,1024]{2,1,0:T(8,128)(2,1)} %bitcast.34), channel_id=1, replica_groups=mesh['z'=8,'yh'=2,'core'=2,'ch'=8] {'yh','ch'}, dimensions={0} | all-to-all | bytes 524288 | tf_op jit(solution)/shard_map/all_to_all | solution.py:174
  70.1 0.2 copy.13
  70.3 0.8 %reshape.37 = bf16[8,32,512]{2,1,0:T(8,128)(2,1)} reshape(bf16[8,16,2,512]{3,2,1,0:T(2,128)(2,1)S(1)} %bitcast.32) | data formatting | bytes 524288 | tf_op jit(solution)/shard_map/reshape | solution.py:176
  (4 shorter events, 0.1 us)
Async XLA Ops:
  26.4 9.7 %collective-permute-start = (bf16[64,1024]{1,0:T(8,128)(2,1)}, bf16[64,1024]{1,0:T(8,128)(2,1)S(1)}, u32[]{:S(2)}, u32[]{:S(2)}) collective-permute-start(bf16[64,1024]{1,0:T(8,128)(2,1)} %shard_map.46.refs_0_.refs_1_), channel_id=1, source_target_pairs={{32,0},{64,32},{96,64},{128,96},{160,128},{192,160},{224,192},{33,... | collective-permute-start | bytes 393224 | tf_op jit(solution)/shard_map/ppermute | solution.py:144
  31.0 12.4 %collective-permute-start.2 = (bf16[64,1024]{1,0:T(8,128)(2,1)}, bf16[64,1024]{1,0:T(8,128)(2,1)S(1)}, u32[]{:S(2)}, u32[]{:S(2)}) collective-permute-start(bf16[64,1024]{1,0:T(8,128)(2,1)} %shard_map.47.refs_1_.refs_2_), channel_id=1, source_target_pairs={{0,32},{32,64},{64,96},{96,128},{128,160},{160,192},{192,224},{1,3... | collective-permute-start | bytes 393224 | tf_op jit(solution)/shard_map/ppermute | solution.py:144
  36.1 0.7 copy-start.1
  39.6 9.3 %collective-permute-start.1 = (bf16[64,1024]{1,0:T(8,128)(2,1)}, bf16[64,1024]{1,0:T(8,128)(2,1)S(1)}, u32[]{:S(2)}, u32[]{:S(2)}) collective-permute-start(bf16[64,1024]{1,0:T(8,128)(2,1)} %shard_map.48.refs_2_), channel_id=1, source_target_pairs={{0,32},{32,64},{64,96},{96,128},{128,160},{160,192},{192,224},{1,3... | collective-permute-start | bytes 393224 | tf_op jit(solution)/shard_map/ppermute | solution.py:144
  43.4 0.7 copy-start
  46.9 8.3 %collective-permute-start.3 = (bf16[64,1024]{1,0:T(8,128)(2,1)}, bf16[64,1024]{1,0:T(8,128)(2,1)S(1)}, u32[]{:S(2)}, u32[]{:S(2)}) collective-permute-start(bf16[64,1024]{1,0:T(8,128)(2,1)} %shard_map.49.refs_1_), channel_id=1, source_target_pairs={{32,0},{64,32},{96,64},{128,96},{160,128},{192,160},{224,192},{33,... | collective-permute-start | bytes 393224 | tf_op jit(solution)/shard_map/ppermute | solution.py:144
  48.9 6.2 %copy-start.2 = (bf16[64,1024]{1,0:T(8,128)(2,1)}, bf16[64,1024]{1,0:T(8,128)(2,1)S(1)}, u32[]{:S(2)}) copy-start(bf16[64,1024]{1,0:T(8,128)(2,1)S(1)} %collective-permute-done.1.refs_0_) | copy-start | bytes 393220
  55.2 0.7 copy-start.3

commit v12 on v10

--- a/solution.py
+++ b/solution.py
@@ -15,6 +15,13 @@
 LAYER_COLS = 2 * PLANE_COLS + DEPTH_COLS
 SLAB = ("z", "yh", "core")
 GROUP = ("yh", "ch")
+
+
+ANYWHERE_VMEM = pl.BlockSpec(memory_space=pltpu.VMEM)
+
+
+def in_vmem(arrays):
+    return [pltpu.with_memory_space_constraint(a, pltpu.VMEM) for a in arrays]
 
 
 def pack_weights(plane_a, plane_b, depth):
@@ -117,7 +124,9 @@
             split_out=split_out,
         ),
         out_shape=out_shape,
-    )(*inputs, src)
+        in_specs=[ANYWHERE_VMEM] * (len(inputs) + 1),
+        out_specs=(ANYWHERE_VMEM, ANYWHERE_VMEM) if split_out else ANYWHERE_VMEM,
+    )(*in_vmem(list(inputs) + [src]))
 
 
 def _half_kernel(*refs, depth_layer, plane_layer, vol_cols, chans, row_half):
@@ -151,7 +160,9 @@
             row_half=row_half,
         ),
         out_shape=jax.ShapeDtypeStruct((chans, vol_cols), jnp.bfloat16),
-    )(*inputs, src)
+        in_specs=[ANYWHERE_VMEM] * (len(inputs) + 1),
+        out_specs=ANYWHERE_VMEM,
+    )(*in_vmem(list(inputs) + [src]))
 
 
 def shift_z(block, step):

time: 72.5 us -> 66.4 us (0.916)
  Pallas kernels: 13.7 us -> 7.63 us
    pallas_call x4, Pallas kernels: 11.4 us -> 6.66 us  [half_kernel(): pl.pallas_call(functools.partial(_half_kernel, depth_layer=depth_layer, p...]
    pallas_call x1, Pallas kernels: 2.32 us -> 0.96 us  [layer_kernel(): pl.pallas_call(functools.partial(_kernel, depth_layer=depth_layer, plane_...]
  transfers between devices with their start and end apart: 4 -> 4, of which waited for: 1 -> 1; matrix products, arithmetic and copies ran while one was open for 0% -> 0% of each run, Pallas kernels for 12% -> 8%
where the time goes in v12:
time: 66.4 us; the launch traced here: 65.8 us
  blocking collectives  31.9 us (48%)
  starting transfers between devices  13.1 us (20%)
  Pallas kernels  7.63 us (11%)
  local copies, waits for them, and re-layouts  6.67 us (10%)
  waiting for transfers between devices  6.26 us (9%)
    all_to_all x1, blocking collectives, local(): got = lax.all_to_all(sent, GROUP, split_axis=0, concat_axis=0, tiled=True)  19.8 us
    ppermute x4, starting transfers between devices, shift_z(): return lax.ppermute(block, 'z', route)  13.1 us
    all_to_all x1, blocking collectives, local(): lax.all_to_all(out.reshape(members, part, vol_cols), GROUP, split_axis=0,...  12.2 us
    pallas_call x4, Pallas kernels, half_kernel(): pl.pallas_call(functools.partial(_half_kernel, depth_layer=depth_layer, p...  6.66 us
    ppermute x4, waiting for transfers between devices, shift_z(): return lax.ppermute(block, 'z', route)  6.26 us
    unnamed x8, local copies, waits for them, and re-layouts  1.84 us
  transfers between devices with their start and end apart: 4, of which 1 were waited for; matrix products, arithmetic and copies ran while one was open for 0% of the time, Pallas kernels for 8%

profile of v12, /device:TPU:96, one launch (start us, length us, event | category | flops | bytes accessed | tf_op | source)
XLA Modules:
  0.0 65.8 jit_solution(14301201261164491406)
XLA Ops:
  0.0 0.7 %copy.10 = bf16[8,2,3,64]{3,2,0,1:T(4,128)(2,1)S(1)} copy(bf16[8,2,3,64]{3,0,2,1:T(8,128)(2,1)} %bitcast.31) | data formatting | bytes 12288 | tf_op jit(solution)/shard_map/transpose | solution.py:32
  0.7 0.1 reshape.33
  0.8 0.8 %copy.8 = bf16[8,2,3,3,64]{4,3,2,0,1:T(4,128)(2,1)S(1)} copy(bf16[8,2,3,3,64]{4,0,3,2,1:T(8,128)(2,1)} %bitcast.29) | data formatting | bytes 36864 | tf_op jit(solution)/shard_map/transpose | solution.py:30
  1.6 0.1 reshape.31
  1.7 0.8 %copy.9 = bf16[8,2,3,3,64]{4,3,2,0,1:T(4,128)(2,1)S(1)} copy(bf16[8,2,3,3,64]{4,0,3,2,1:T(8,128)(2,1)} %bitcast.30) | data formatting | bytes 36864 | tf_op jit(solution)/shard_map/transpose | solution.py:31
  2.5 0.1 reshape.32
  2.6 1.1 %reshape.29 = bf16[8,16,2,512]{3,2,1,0:T(2,128)(2,1)S(1)} reshape(bf16[8,32,512]{2,1,0:T(8,128)(2,1)} %param.4) | data formatting | bytes 524288 | tf_op jit(solution)/shard_map/reshape | solution.py:180
  3.7 0.2 copy.7
  3.9 19.8 %all_to_all.10 = bf16[16,8,2560]{2,1,0:T(8,128)(2,1)S(1)} all-to-all(bf16[16,8,2560]{2,1,0:T(8,128)(2,1)S(1)} %pad_maximum_fusion), channel_id=1, replica_groups=mesh['z'=8,'yh'=2,'core'=2,'ch'=8] {'yh','ch'}, dimensions={0} | all-to-all | bytes 1310720 | tf_op jit(solution)/shard_map/all_to_all | solution.py:186
  23.7 1.6 %shard_map.46.refs_0_.refs_1_ = bf16[64,1024]{1,0:T(8,128)(2,1)} custom-call(bf16[128,2560]{1,0:T(8,128)(2,1)S(1)} %bitcast.19), custom_call_target="tpu_custom_call" | custom-call | tf_op jit(solution)/shard_map/pallas_call | solution.py:153
  25.3 0.0 copy-start
  25.3 2.1 %collective-permute-start = (bf16[64,1024]{1,0:T(8,128)(2,1)}, bf16[64,1024]{1,0:T(8,128)(2,1)S(1)}, u32[]{:S(2)}, u32[]{:S(2)}) collective-permute-start(bf16[64,1024]{1,0:T(8,128)(2,1)} %shard_map.46.refs_0_.refs_1_), channel_id=1, source_target_pairs={{32,0},{64,32},{96,64},{128,96},{160,128},{192,160},{224,192},{33,... | collective-permute-start | bytes 393224 | tf_op jit(solution)/shard_map/ppermute | solution.py:171
  27.5 1.6 %shard_map.47.refs_1_.refs_2_ = bf16[64,1024]{1,0:T(8,128)(2,1)} custom-call(bf16[128,2560]{1,0:T(8,128)(2,1)S(1)} %bitcast.20), custom_call_target="tpu_custom_call" | custom-call | tf_op jit(solution)/shard_map/pallas_call | solution.py:153
  29.1 5.0 %collective-permute-start.2 = (bf16[64,1024]{1,0:T(8,128)(2,1)}, bf16[64,1024]{1,0:T(8,128)(2,1)S(1)}, u32[]{:S(2)}, u32[]{:S(2)}) collective-permute-start(bf16[64,1024]{1,0:T(8,128)(2,1)} %shard_map.47.refs_1_.refs_2_), channel_id=1, source_target_pairs={{0,32},{32,64},{64,96},{96,128},{128,160},{160,192},{192,224},{1,3... | collective-permute-start | bytes 393224 | tf_op jit(solution)/shard_map/ppermute | solution.py:171
  34.1 0.0 collective-permute-done.refs_2_
  34.1 0.0 copy-done
  34.1 0.0 copy-start.1
  34.2 0.9 %copy-done.1 = bf16[64,1024]{1,0:T(8,128)(2,1)S(1)} copy-done((bf16[64,1024]{1,0:T(8,128)(2,1)S(1)}, bf16[64,1024]{1,0:T(8,128)(2,1)}, u32[]{:S(2)}) %copy-start.1) | copy-done | bytes 131096
  35.1 1.7 %shard_map.48.refs_2_ = bf16[64,1024]{1,0:T(8,128)(2,1)} custom-call(bf16[64,1024]{1,0:T(8,128)(2,1)S(1)} %copy-done, bf16[64,1024]{1,0:T(8,128)(2,1)S(1)} %copy-done.1, bf16[64,1024]{1,0:T(8,128)(2,1)S(1)} %collective-permute-done.refs_2_, bf16[128,2560]{1,0:T(8,128)(2,1)S(1)} %bitcast.21), custom_call_target="tpu_custom_call" | custom-call | tf_op jit(solution)/shard_map/pallas_call | solution.py:153
  36.8 0.0 copy-start.2
  36.8 4.0 %collective-permute-start.1 = (bf16[64,1024]{1,0:T(8,128)(2,1)}, bf16[64,1024]{1,0:T(8,128)(2,1)S(1)}, u32[]{:S(2)}, u32[]{:S(2)}) collective-permute-start(bf16[64,1024]{1,0:T(8,128)(2,1)} %shard_map.48.refs_2_), channel_id=1, source_target_pairs={{0,32},{32,64},{64,96},{96,128},{128,160},{160,192},{192,224},{1,3... | collective-permute-start | bytes 393224 | tf_op jit(solution)/shard_map/ppermute | solution.py:171
  40.8 0.0 collective-permute-done.2.refs_0_
  40.8 1.7 %shard_map.49.refs_1_ = bf16[64,1024]{1,0:T(8,128)(2,1)} custom-call(bf16[64,1024]{1,0:T(8,128)(2,1)S(1)} %collective-permute-done.2.refs_0_, bf16[64,1024]{1,0:T(8,128)(2,1)S(1)} %copy-done, bf16[64,1024]{1,0:T(8,128)(2,1)S(1)} %copy-done.1, bf16[128,2560]{1,0:T(8,128)(2,1)S(1)} %bitcast.22), custom_call_target="tpu_custom_call" | custom-call | tf_op jit(solution)/shard_map/pallas_call | solution.py:153
  42.5 2.0 %collective-permute-start.3 = (bf16[64,1024]{1,0:T(8,128)(2,1)}, bf16[64,1024]{1,0:T(8,128)(2,1)S(1)}, u32[]{:S(2)}, u32[]{:S(2)}) collective-permute-start(bf16[64,1024]{1,0:T(8,128)(2,1)} %shard_map.49.refs_1_), channel_id=1, source_target_pairs={{32,0},{64,32},{96,64},{128,96},{160,128},{192,160},{224,192},{33,... | collective-permute-start | bytes 393224 | tf_op jit(solution)/shard_map/ppermute | solution.py:171
  44.5 0.0 collective-permute-done.1.refs_0_
  44.5 6.3 %collective-permute-done.3.refs_3_ = bf16[64,1024]{1,0:T(8,128)(2,1)S(1)} collective-permute-done((bf16[64,1024]{1,0:T(8,128)(2,1)}, bf16[64,1024]{1,0:T(8,128)(2,1)S(1)}, u32[]{:S(2)}, u32[]{:S(2)}) %collective-permute-start.3) | collective-permute-done | bytes 131104 | tf_op jit(solution)/shard_map/ppermute | solution.py:171
  50.7 0.0 copy-done.2
  50.7 0.9 %copy-done.3 = bf16[64,1024]{1,0:T(8,128)(2,1)S(1)} copy-done((bf16[64,1024]{1,0:T(8,128)(2,1)S(1)}, bf16[64,1024]{1,0:T(8,128)(2,1)}, u32[]{:S(2)}) %copy-start.3) | copy-done | bytes 131096
  51.6 1.0 %shard_map.50 = bf16[128,1024]{1,0:T(8,128)(2,1)} custom-call(bf16[64,1024]{1,0:T(8,128)(2,1)S(1)} %collective-permute-done.1.refs_0_, bf16[64,1024]{1,0:T(8,128)(2,1)S(1)} %copy-done.3, bf16[64,1024]{1,0:T(8,128)(2,1)S(1)} %copy-done.2, bf16[64,1024]{1,0:T(8,128)(2,1)S(1)} %collective-permute-done.3.refs_3_, bf16[128,2560]{1,0:T(8,128)(2,1)S(1)} %bitcast.23), custom_call_target="tpu_custom_call" | custom-call | tf_op jit(solution)/shard_map/pallas_call | solution.py:117
  52.6 12.2 %all_to_all.11 = bf16[16,8,1024]{2,1,0:T(8,128)(2,1)S(1)} all-to-all(bf16[16,8,1024]{2,1,0:T(8,128)(2,1)} %bitcast.28), channel_id=1, replica_groups=mesh['z'=8,'yh'=2,'core'=2,'ch'=8] {'yh','ch'}, dimensions={0} | all-to-all | bytes 524288 | tf_op jit(solution)/shard_map/all_to_all | solution.py:201
  64.8 0.2 copy.13
  65.0 0.8 %reshape.37 = bf16[8,32,512]{2,1,0:T(8,128)(2,1)} reshape(bf16[8,16,2,512]{3,2,1,0:T(2,128)(2,1)S(1)} %bitcast.26) | data formatting | bytes 524288 | tf_op jit(solution)/shard_map/reshape | solution.py:203
  (4 shorter events, 0.1 us)
Async XLA Ops:
  25.3 8.8 %copy-start = (bf16[64,1024]{1,0:T(8,128)(2,1)S(1)}, bf16[64,1024]{1,0:T(8,128)(2,1)}, u32[]{:S(2)}) copy-start(bf16[64,1024]{1,0:T(8,128)(2,1)} %shard_map.46.refs_0_.refs_1_) | copy-start | bytes 393220
  25.3 8.8 %collective-permute-start = (bf16[64,1024]{1,0:T(8,128)(2,1)}, bf16[64,1024]{1,0:T(8,128)(2,1)S(1)}, u32[]{:S(2)}, u32[]{:S(2)}) collective-permute-start(bf16[64,1024]{1,0:T(8,128)(2,1)} %shard_map.46.refs_0_.refs_1_), channel_id=1, source_target_pairs={{32,0},{64,32},{96,64},{128,96},{160,128},{192,160},{224,192},{33,... | collective-permute-start | bytes 393224 | tf_op jit(solution)/shard_map/ppermute | solution.py:171
  29.1 11.7 %collective-permute-start.2 = (bf16[64,1024]{1,0:T(8,128)(2,1)}, bf16[64,1024]{1,0:T(8,128)(2,1)S(1)}, u32[]{:S(2)}, u32[]{:S(2)}) collective-permute-start(bf16[64,1024]{1,0:T(8,128)(2,1)} %shard_map.47.refs_1_.refs_2_), channel_id=1, source_target_pairs={{0,32},{32,64},{64,96},{96,128},{128,160},{160,192},{192,224},{1,3... | collective-permute-start | bytes 393224 | tf_op jit(solution)/shard_map/ppermute | solution.py:171
  34.1 0.9 %copy-start.1 = (bf16[64,1024]{1,0:T(8,128)(2,1)S(1)}, bf16[64,1024]{1,0:T(8,128)(2,1)}, u32[]{:S(2)}) copy-start(bf16[64,1024]{1,0:T(8,128)(2,1)} %shard_map.47.refs_1_.refs_2_) | copy-start | bytes 393220
  36.8 14.0 %copy-start.2 = (bf16[64,1024]{1,0:T(8,128)(2,1)S(1)}, bf16[64,1024]{1,0:T(8,128)(2,1)}, u32[]{:S(2)}) copy-start(bf16[64,1024]{1,0:T(8,128)(2,1)} %shard_map.48.refs_2_) | copy-start | bytes 393220
  36.8 7.7 %collective-permute-start.1 = (bf16[64,1024]{1,0:T(8,128)(2,1)}, bf16[64,1024]{1,0:T(8,128)(2,1)S(1)}, u32[]{:S(2)}, u32[]{:S(2)}) collective-permute-start(bf16[64,1024]{1,0:T(8,128)(2,1)} %shard_map.48.refs_2_), channel_id=1, source_target_pairs={{0,32},{32,64},{64,96},{96,128},{128,160},{160,192},{192,224},{1,3... | collective-permute-start | bytes 393224 | tf_op jit(solution)/shard_map/ppermute | solution.py:171
  42.5 8.3 %collective-permute-start.3 = (bf16[64,1024]{1,0:T(8,128)(2,1)}, bf16[64,1024]{1,0:T(8,128)(2,1)S(1)}, u32[]{:S(2)}, u32[]{:S(2)}) collective-permute-start(bf16[64,1024]{1,0:T(8,128)(2,1)} %shard_map.49.refs_1_), channel_id=1, source_target_pairs={{32,0},{64,32},{96,64},{128,96},{160,128},{192,160},{224,192},{33,... | collective-permute-start | bytes 393224 | tf_op jit(solution)/shard_map/ppermute | solution.py:171
  50.7 0.9 %copy-start.3 = (bf16[64,1024]{1,0:T(8,128)(2,1)S(1)}, bf16[64,1024]{1,0:T(8,128)(2,1)}, u32[]{:S(2)}) copy-start(bf16[64,1024]{1,0:T(8,128)(2,1)} %shard_map.49.refs_1_) | copy-start | bytes 393220

commit v13 on v12

--- a/solution.py
+++ b/solution.py
@@ -112,8 +112,8 @@
 
 
 def layer_kernel(inputs, src, vol_cols, chans, depth_layer, plane_layer, split_out):
-    half = jax.ShapeDtypeStruct((chans, vol_cols), jnp.bfloat16)
-    out_shape = (half, half) if split_out else jax.ShapeDtypeStruct((2 * chans, vol_cols), jnp.bfloat16)
+    half = pltpu.VMEM((chans, vol_cols), jnp.bfloat16)
+    out_shape = (half, half) if split_out else pltpu.VMEM((2 * chans, vol_cols), jnp.bfloat16)
     return pl.pallas_call(
         functools.partial(
             _kernel,
@@ -159,7 +159,7 @@
             chans=chans,
             row_half=row_half,
         ),
-        out_shape=jax.ShapeDtypeStruct((chans, vol_cols), jnp.bfloat16),
+        out_shape=pltpu.VMEM((chans, vol_cols), jnp.bfloat16),
         in_specs=[ANYWHERE_VMEM] * (len(inputs) + 1),
         out_specs=ANYWHERE_VMEM,
     )(*in_vmem(list(inputs) + [src]))

time: 66.4 us -> 60.3 us (0.908)
  Pallas kernels: 7.63 us -> 4.3 us
  local copies, waits for them, and re-layouts: 6.67 us -> 4.83 us
    pallas_call x4, Pallas kernels: 6.66 us -> 4.04 us  [half_kernel(): pl.pallas_call(functools.partial(_half_kernel, depth_layer=depth_layer, p...]
    unnamed x8 -> x0, local copies, waits for them, and re-layouts: 1.84 us -> none
    pallas_call x1, Pallas kernels: 0.96 us -> 0.25 us  [layer_kernel(): pl.pallas_call(functools.partial(_kernel, depth_layer=depth_layer, plane_...]
  transfers between devices with their start and end apart: 4 -> 4, of which waited for: 1 -> 1; matrix products, arithmetic and copies ran while one was open for 0% -> 0% of each run, Pallas kernels for 8% -> 5%
where the time goes in v13:
time: 60.3 us; the launch traced here: 59.8 us
  blocking collectives  31.5 us (52%)
  starting transfers between devices  12.9 us (21%)
  waiting for transfers between devices  6.07 us (10%)
  local copies, waits for them, and re-layouts  4.83 us (8%)
  Pallas kernels  4.3 us (7%)
    all_to_all x1, blocking collectives, local(): got = lax.all_to_all(sent, GROUP, split_axis=0, concat_axis=0, tiled=True)  19.8 us
    ppermute x4, starting transfers between devices, shift_z(): return lax.ppermute(block, 'z', route)  12.9 us
    all_to_all x1, blocking collectives, local(): lax.all_to_all(out.reshape(members, part, vol_cols), GROUP, split_axis=0,...  11.8 us
    ppermute x4, waiting for transfers between devices, shift_z(): return lax.ppermute(block, 'z', route)  6.07 us
    pallas_call x4, Pallas kernels, half_kernel(): pl.pallas_call(functools.partial(_half_kernel, depth_layer=depth_layer, p...  4.04 us
  transfers between devices with their start and end apart: 4, of which 1 were waited for; matrix products, arithmetic and copies ran while one was open for 0% of the time, Pallas kernels for 5%

profile of v13, /device:TPU:96, one launch (start us, length us, event | category | flops | bytes accessed | tf_op | source)
XLA Modules:
  0.0 59.8 jit_solution(8959180098548857713)
XLA Ops:
  0.0 0.7 %copy.10 = bf16[8,2,3,64]{3,2,0,1:T(4,128)(2,1)S(1)} copy(bf16[8,2,3,64]{3,0,2,1:T(8,128)(2,1)} %bitcast.31) | data formatting | bytes 12288 | tf_op jit(solution)/shard_map/transpose | solution.py:32
  0.7 0.1 reshape.33
  0.8 0.8 %copy.8 = bf16[8,2,3,3,64]{4,3,2,0,1:T(4,128)(2,1)S(1)} copy(bf16[8,2,3,3,64]{4,0,3,2,1:T(8,128)(2,1)} %bitcast.29) | data formatting | bytes 36864 | tf_op jit(solution)/shard_map/transpose | solution.py:30
  1.6 0.1 reshape.31
  1.7 0.8 %copy.9 = bf16[8,2,3,3,64]{4,3,2,0,1:T(4,128)(2,1)S(1)} copy(bf16[8,2,3,3,64]{4,0,3,2,1:T(8,128)(2,1)} %bitcast.30) | data formatting | bytes 36864 | tf_op jit(solution)/shard_map/transpose | solution.py:31
  2.5 0.1 reshape.32
  2.6 1.1 %reshape.29 = bf16[8,16,2,512]{3,2,1,0:T(2,128)(2,1)S(1)} reshape(bf16[8,32,512]{2,1,0:T(8,128)(2,1)} %param.4) | data formatting | bytes 524288 | tf_op jit(solution)/shard_map/reshape | solution.py:180
  3.7 0.2 copy.7
  3.9 19.8 %all_to_all.10 = bf16[16,8,2560]{2,1,0:T(8,128)(2,1)S(1)} all-to-all(bf16[16,8,2560]{2,1,0:T(8,128)(2,1)S(1)} %pad_maximum_fusion), channel_id=1, replica_groups=mesh['z'=8,'yh'=2,'core'=2,'ch'=8] {'yh','ch'}, dimensions={0} | all-to-all | bytes 1310720 | tf_op jit(solution)/shard_map/all_to_all | solution.py:186
  23.7 1.0 %shard_map.46.refs_0_.refs_1_ = bf16[64,1024]{1,0:T(8,128)(2,1)S(1)} custom-call(bf16[128,2560]{1,0:T(8,128)(2,1)S(1)} %bitcast.19), custom_call_target="tpu_custom_call" | custom-call | tf_op jit(solution)/shard_map/pallas_call | solution.py:153
  24.7 2.0 %collective-permute-start = (bf16[64,1024]{1,0:T(8,128)(2,1)S(1)}, bf16[64,1024]{1,0:T(8,128)(2,1)S(1)}, u32[]{:S(2)}, u32[]{:S(2)}) collective-permute-start(bf16[64,1024]{1,0:T(8,128)(2,1)S(1)} %shard_map.46.refs_0_.refs_1_), channel_id=1, source_target_pairs={{32,0},{64,32},{96,64},{128,96},{160,128},{192,160},{224,192},{33,... | collective-permute-start | bytes 393224 | tf_op jit(solution)/shard_map/ppermute | solution.py:171
  26.7 1.0 %shard_map.47.refs_1_.refs_2_ = bf16[64,1024]{1,0:T(8,128)(2,1)S(1)} custom-call(bf16[128,2560]{1,0:T(8,128)(2,1)S(1)} %bitcast.20), custom_call_target="tpu_custom_call" | custom-call | tf_op jit(solution)/shard_map/pallas_call | solution.py:153
  27.7 5.0 %collective-permute-start.2 = (bf16[64,1024]{1,0:T(8,128)(2,1)S(1)}, bf16[64,1024]{1,0:T(8,128)(2,1)S(1)}, u32[]{:S(2)}, u32[]{:S(2)}) collective-permute-start(bf16[64,1024]{1,0:T(8,128)(2,1)S(1)} %shard_map.47.refs_1_.refs_2_), channel_id=1, source_target_pairs={{0,32},{32,64},{64,96},{96,128},{128,160},{160,192},{192,224},{1,3... | collective-permute-start | bytes 393224 | tf_op jit(solution)/shard_map/ppermute | solution.py:171
  32.7 0.0 collective-permute-done.refs_2_
  32.7 1.1 %shard_map.48.refs_2_ = bf16[64,1024]{1,0:T(8,128)(2,1)S(1)} custom-call(bf16[64,1024]{1,0:T(8,128)(2,1)S(1)} %shard_map.46.refs_0_.refs_1_, bf16[64,1024]{1,0:T(8,128)(2,1)S(1)} %shard_map.47.refs_1_.refs_2_, bf16[64,1024]{1,0:T(8,128)(2,1)S(1)} %collective-permute-done.refs_2_, bf16[128,2560]{1,0:T(8,128)(2,1)S(1)} %bitcast.21), custom_call_target="tpu_custom_call" | custom-call | tf_op jit(solution)/shard_map/pallas_call | solution.py:153
  33.8 3.8 %collective-permute-start.1 = (bf16[64,1024]{1,0:T(8,128)(2,1)S(1)}, bf16[64,1024]{1,0:T(8,128)(2,1)S(1)}, u32[]{:S(2)}, u32[]{:S(2)}) collective-permute-start(bf16[64,1024]{1,0:T(8,128)(2,1)S(1)} %shard_map.48.refs_2_), channel_id=1, source_target_pairs={{0,32},{32,64},{64,96},{96,128},{128,160},{160,192},{192,224},{1,3... | collective-permute-start | bytes 393224 | tf_op jit(solution)/shard_map/ppermute | solution.py:171
  37.6 0.0 collective-permute-done.2.refs_0_
  37.7 1.1 %shard_map.49.refs_1_ = bf16[64,1024]{1,0:T(8,128)(2,1)S(1)} custom-call(bf16[64,1024]{1,0:T(8,128)(2,1)S(1)} %collective-permute-done.2.refs_0_, bf16[64,1024]{1,0:T(8,128)(2,1)S(1)} %shard_map.46.refs_0_.refs_1_, bf16[64,1024]{1,0:T(8,128)(2,1)S(1)} %shard_map.47.refs_1_.refs_2_, bf16[128,2560]{1,0:T(8,128)(2,1)S(1)} %bitcast.22), custom_call_target="tpu_custom_call" | custom-call | tf_op jit(solution)/shard_map/pallas_call | solution.py:153
  38.7 2.0 %collective-permute-start.3 = (bf16[64,1024]{1,0:T(8,128)(2,1)S(1)}, bf16[64,1024]{1,0:T(8,128)(2,1)S(1)}, u32[]{:S(2)}, u32[]{:S(2)}) collective-permute-start(bf16[64,1024]{1,0:T(8,128)(2,1)S(1)} %shard_map.49.refs_1_), channel_id=1, source_target_pairs={{32,0},{64,32},{96,64},{128,96},{160,128},{192,160},{224,192},{33,... | collective-permute-start | bytes 393224 | tf_op jit(solution)/shard_map/ppermute | solution.py:171
  40.7 0.0 collective-permute-done.1.refs_0_
  40.7 6.0 %collective-permute-done.3.refs_3_ = bf16[64,1024]{1,0:T(8,128)(2,1)S(1)} collective-permute-done((bf16[64,1024]{1,0:T(8,128)(2,1)S(1)}, bf16[64,1024]{1,0:T(8,128)(2,1)S(1)}, u32[]{:S(2)}, u32[]{:S(2)}) %collective-permute-start.3) | collective-permute-done | bytes 131104 | tf_op jit(solution)/shard_map/ppermute | solution.py:171
  46.8 0.3 shard_map.50
  47.1 11.8 %all_to_all.11 = bf16[16,8,1024]{2,1,0:T(8,128)(2,1)S(1)} all-to-all(bf16[16,8,1024]{2,1,0:T(8,128)(2,1)S(1)} %bitcast.24), channel_id=1, replica_groups=mesh['z'=8,'yh'=2,'core'=2,'ch'=8] {'yh','ch'}, dimensions={0} | all-to-all | bytes 524288 | tf_op jit(solution)/shard_map/all_to_all | solution.py:201
  58.8 0.2 copy.13
  59.0 0.8 %reshape.37 = bf16[8,32,512]{2,1,0:T(8,128)(2,1)} reshape(bf16[8,16,2,512]{3,2,1,0:T(2,128)(2,1)S(1)} %bitcast.27) | data formatting | bytes 524288 | tf_op jit(solution)/shard_map/reshape | solution.py:203
  (3 shorter events, 0.1 us)
Async XLA Ops:
  24.7 8.1 %collective-permute-start = (bf16[64,1024]{1,0:T(8,128)(2,1)S(1)}, bf16[64,1024]{1,0:T(8,128)(2,1)S(1)}, u32[]{:S(2)}, u32[]{:S(2)}) collective-permute-start(bf16[64,1024]{1,0:T(8,128)(2,1)S(1)} %shard_map.46.refs_0_.refs_1_), channel_id=1, source_target_pairs={{32,0},{64,32},{96,64},{128,96},{160,128},{192,160},{224,192},{33,... | collective-permute-start | bytes 393224 | tf_op jit(solution)/shard_map/ppermute | solution.py:171
  27.7 10.0 %collective-permute-start.2 = (bf16[64,1024]{1,0:T(8,128)(2,1)S(1)}, bf16[64,1024]{1,0:T(8,128)(2,1)S(1)}, u32[]{:S(2)}, u32[]{:S(2)}) collective-permute-start(bf16[64,1024]{1,0:T(8,128)(2,1)S(1)} %shard_map.47.refs_1_.refs_2_), channel_id=1, source_target_pairs={{0,32},{32,64},{64,96},{96,128},{128,160},{160,192},{192,224},{1,3... | collective-permute-start | bytes 393224 | tf_op jit(solution)/shard_map/ppermute | solution.py:171
  33.8 6.9 %collective-permute-start.1 = (bf16[64,1024]{1,0:T(8,128)(2,1)S(1)}, bf16[64,1024]{1,0:T(8,128)(2,1)S(1)}, u32[]{:S(2)}, u32[]{:S(2)}) collective-permute-start(bf16[64,1024]{1,0:T(8,128)(2,1)S(1)} %shard_map.48.refs_2_), channel_id=1, source_target_pairs={{0,32},{32,64},{64,96},{96,128},{128,160},{160,192},{192,224},{1,3... | collective-permute-start | bytes 393224 | tf_op jit(solution)/shard_map/ppermute | solution.py:171
  38.7 8.1 %collective-permute-start.3 = (bf16[64,1024]{1,0:T(8,128)(2,1)S(1)}, bf16[64,1024]{1,0:T(8,128)(2,1)S(1)}, u32[]{:S(2)}, u32[]{:S(2)}) collective-permute-start(bf16[64,1024]{1,0:T(8,128)(2,1)S(1)} %shard_map.49.refs_1_), channel_id=1, source_target_pairs={{32,0},{64,32},{96,64},{128,96},{160,128},{192,160},{224,192},{33,... | collective-permute-start | bytes 393224 | tf_op jit(solution)/shard_map/ppermute | solution.py:171

commit v14 on v13

--- a/solution.py
+++ b/solution.py
@@ -10,9 +10,6 @@
 
 X = 64
 Y = 8
-PLANE_COLS = 640
-DEPTH_COLS = 256
-LAYER_COLS = 2 * PLANE_COLS + DEPTH_COLS
 SLAB = ("z", "yh", "core")
 GROUP = ("yh", "ch")
 
@@ -26,12 +23,10 @@
 
 def pack_weights(plane_a, plane_b, depth):
     layers, out_part, chans = plane_a.shape[:3]
-    pad = ((0, 0), (0, 0), (0, PLANE_COLS - 9 * chans))
-    taps_a = jnp.pad(jnp.transpose(plane_a, (1, 0, 3, 4, 2)).reshape(out_part, layers, -1), pad)
-    taps_b = jnp.pad(jnp.transpose(plane_b, (1, 0, 3, 4, 2)).reshape(out_part, layers, -1), pad)
+    planes = jnp.transpose(jnp.stack([plane_a, plane_b]), (2, 1, 0, 4, 5, 3))
+    planes = planes.reshape(out_part, layers, 18 * chans)
     taps_d = jnp.transpose(depth, (1, 0, 3, 2)).reshape(out_part, layers, 3 * chans)
-    taps_d = jnp.pad(taps_d, ((0, 0), (0, 0), (0, DEPTH_COLS - 3 * chans)))
-    return jnp.concatenate([taps_a, taps_b, taps_d], axis=2)
+    return jnp.concatenate([planes, taps_d], axis=2)
 
 
 def _masks(width):
@@ -93,14 +88,14 @@
             axis=0,
         )
         rows = slice(depth_layer * chans, (depth_layer + 1) * chans)
-        at = vol_cols + 2 * PLANE_COLS
+        at = vol_cols + 18 * chans
         total = jnp.dot(src_ref[rows, at : at + 3 * chans], stacked, preferred_element_type=jnp.float32)
         h = jnp.maximum(total, 0.0).astype(jnp.bfloat16)
     if plane_layer is not None:
         ok = _masks(h.shape[1])
         rows = slice(plane_layer * chans, (plane_layer + 1) * chans)
         for k in range(2):
-            at = vol_cols + k * PLANE_COLS
+            at = vol_cols + k * 9 * chans
             w = src_ref[rows, at : at + 9 * chans]
             h = jnp.maximum(_plane(h, w, ok), 0.0).astype(jnp.bfloat16)
     half = h.shape[1] // 2
@@ -137,13 +132,13 @@
         lo_ref, mid_ref, up_ref = refs[:3]
         stacked = jnp.concatenate([lo_ref[...], mid_ref[...], up_ref[...]], axis=0)
         rows = slice(depth_layer * chans, (depth_layer + 1) * chans)
-        at = vol_cols + 2 * PLANE_COLS
+        at = vol_cols + 18 * chans
         total = jnp.dot(src_ref[rows, at : at + 3 * chans], stacked, preferred_element_type=jnp.float32)
         h = jnp.maximum(total, 0.0).astype(jnp.bfloat16)
     ok = _masks(h.shape[1])
     rows = slice(plane_layer * chans, (plane_layer + 1) * chans)
     for k in range(2):
-        at = vol_cols + k * PLANE_COLS
+        at = vol_cols + k * 9 * chans
         w = src_ref[rows, at : at + 9 * chans]
         h = jnp.maximum(_plane(h, w, ok), 0.0).astype(jnp.bfloat16)
     o_ref[...] = h

time: 60.3 us -> 58.2 us (0.965)
  local copies, waits for them, and re-layouts: 4.83 us -> 2.31 us
  other arithmetic: 0.06 us -> 0.86 us
    transpose x2 -> x1, local copies, waits for them, and re-layouts: 1.57 us -> 0.04 us  [pack_weights(): planes = jnp.transpose(jnp.stack([plane_a, plane_b]), (2, 1, 0, 4, 5, 3))]
    reshape x1, local copies, waits for them, and re-layouts: 1.05 us -> 0.1 us  [local(): volume.reshape(part, members, per, flat)]
    transpose x0 -> x1, other arithmetic: none -> 0.8 us  [pack_weights(): planes = jnp.transpose(jnp.stack([plane_a, plane_b]), (2, 1, 0, 4, 5, 3))]
where the time goes in v14:
time: 58.2 us; the launch traced here: 57.9 us
  blocking collectives  31.2 us (54%)
  starting transfers between devices  12.9 us (22%)
  waiting for transfers between devices  6.06 us (10%)
  Pallas kernels  4.35 us (7%)
  local copies, waits for them, and re-layouts  2.31 us (4%)
  other arithmetic  0.86 us (1%)
    all_to_all x1, blocking collectives, local(): got = lax.all_to_all(sent, GROUP, split_axis=0, concat_axis=0, tiled=True)  19.4 us
    ppermute x4, starting transfers between devices, shift_z(): return lax.ppermute(block, 'z', route)  12.9 us
    all_to_all x1, blocking collectives, local(): lax.all_to_all(out.reshape(members, part, vol_cols), GROUP, split_axis=0,...  11.8 us
    ppermute x4, waiting for transfers between devices, shift_z(): return lax.ppermute(block, 'z', route)  6.06 us
    pallas_call x4, Pallas kernels, half_kernel(): pl.pallas_call(functools.partial(_half_kernel, depth_layer=depth_layer, p...  4.1 us
  transfers between devices with their start and end apart: 4, of which 1 were waited for; matrix products, arithmetic and copies ran while one was open for 0% of the time, Pallas kernels for 5%

profile of v14, /device:TPU:96, one launch (start us, length us, event | category | flops | bytes accessed | tf_op | source)
XLA Modules:
  0.0 57.9 jit_solution(17340062979234231769)
XLA Ops:
  0.0 0.0 copy-start
  0.0 0.8 %copy.9 = bf16[8,2,3,64]{3,2,0,1:T(4,128)(2,1)S(1)} copy(bf16[8,2,3,64]{3,0,2,1:T(8,128)(2,1)} %bitcast.31) | data formatting | bytes 12288 | tf_op jit(solution)/shard_map/transpose | solution.py:28
  0.8 0.1 reshape.29
  0.9 0.8 %maximum_bitcast_fusion = bf16[8,2,2,3,3,64]{5,0,4,3,1,2:T(8,128)(2,1)S(1)} fusion(bf16[1,2,8,64,3,3]{3,2,5,4,1,0:T(8,128)(2,1)} %bitcast.29, bf16[1,2,8,64,3,3]{3,2,5,4,1,0:T(8,128)(2,1)} %bitcast.30), kind=kLoop, calls=%fused_computation.2 | loop fusion | flops 18432 | bytes 73728 | tf_op jit(solution)/shard_map/transpose | solution.py:26
  1.7 0.1 reshape.28
  1.8 0.0 copy-done
  1.8 0.1 reshape.26
  2.0 0.2 copy.7
  2.2 19.4 %all_to_all.10 = bf16[16,8,2368]{2,1,0:T(8,128)(2,1)S(1)} all-to-all(bf16[16,8,2368]{2,1,0:T(8,128)(2,1)S(1)} %pad_maximum_fusion), channel_id=1, replica_groups=mesh['z'=8,'yh'=2,'core'=2,'ch'=8] {'yh','ch'}, dimensions={0} | all-to-all | bytes 1212416 | tf_op jit(solution)/shard_map/all_to_all | solution.py:181
  21.6 1.0 %shard_map.46.refs_0_.refs_1_ = bf16[64,1024]{1,0:T(8,128)(2,1)S(1)} custom-call(bf16[128,2368]{1,0:T(8,128)(2,1)S(1)} %bitcast.19), custom_call_target="tpu_custom_call" | custom-call | tf_op jit(solution)/shard_map/pallas_call | solution.py:148
  22.6 2.0 %collective-permute-start = (bf16[64,1024]{1,0:T(8,128)(2,1)S(1)}, bf16[64,1024]{1,0:T(8,128)(2,1)S(1)}, u32[]{:S(2)}, u32[]{:S(2)}) collective-permute-start(bf16[64,1024]{1,0:T(8,128)(2,1)S(1)} %shard_map.46.refs_0_.refs_1_), channel_id=1, source_target_pairs={{32,0},{64,32},{96,64},{128,96},{160,128},{192,160},{224,192},{33,... | collective-permute-start | bytes 393224 | tf_op jit(solution)/shard_map/ppermute | solution.py:166
  24.7 1.0 %shard_map.47.refs_1_.refs_2_ = bf16[64,1024]{1,0:T(8,128)(2,1)S(1)} custom-call(bf16[128,2368]{1,0:T(8,128)(2,1)S(1)} %bitcast.20), custom_call_target="tpu_custom_call" | custom-call | tf_op jit(solution)/shard_map/pallas_call | solution.py:148
  25.6 5.0 %collective-permute-start.2 = (bf16[64,1024]{1,0:T(8,128)(2,1)S(1)}, bf16[64,1024]{1,0:T(8,128)(2,1)S(1)}, u32[]{:S(2)}, u32[]{:S(2)}) collective-permute-start(bf16[64,1024]{1,0:T(8,128)(2,1)S(1)} %shard_map.47.refs_1_.refs_2_), channel_id=1, source_target_pairs={{0,32},{32,64},{64,96},{96,128},{128,160},{160,192},{192,224},{1,3... | collective-permute-start | bytes 393224 | tf_op jit(solution)/shard_map/ppermute | solution.py:166
  30.7 0.0 collective-permute-done.refs_2_
  30.7 1.1 %shard_map.48.refs_2_ = bf16[64,1024]{1,0:T(8,128)(2,1)S(1)} custom-call(bf16[64,1024]{1,0:T(8,128)(2,1)S(1)} %shard_map.46.refs_0_.refs_1_, bf16[64,1024]{1,0:T(8,128)(2,1)S(1)} %shard_map.47.refs_1_.refs_2_, bf16[64,1024]{1,0:T(8,128)(2,1)S(1)} %collective-permute-done.refs_2_, bf16[128,2368]{1,0:T(8,128)(2,1)S(1)} %bitcast.21), custom_call_target="tpu_custom_call" | custom-call | tf_op jit(solution)/shard_map/pallas_call | solution.py:148
  31.8 3.8 %collective-permute-start.1 = (bf16[64,1024]{1,0:T(8,128)(2,1)S(1)}, bf16[64,1024]{1,0:T(8,128)(2,1)S(1)}, u32[]{:S(2)}, u32[]{:S(2)}) collective-permute-start(bf16[64,1024]{1,0:T(8,128)(2,1)S(1)} %shard_map.48.refs_2_), channel_id=1, source_target_pairs={{0,32},{32,64},{64,96},{96,128},{128,160},{160,192},{192,224},{1,3... | collective-permute-start | bytes 393224 | tf_op jit(solution)/shard_map/ppermute | solution.py:166
  35.6 0.0 collective-permute-done.2.refs_0_
  35.6 1.1 %shard_map.49.refs_1_ = bf16[64,1024]{1,0:T(8,128)(2,1)S(1)} custom-call(bf16[64,1024]{1,0:T(8,128)(2,1)S(1)} %collective-permute-done.2.refs_0_, bf16[64,1024]{1,0:T(8,128)(2,1)S(1)} %shard_map.46.refs_0_.refs_1_, bf16[64,1024]{1,0:T(8,128)(2,1)S(1)} %shard_map.47.refs_1_.refs_2_, bf16[128,2368]{1,0:T(8,128)(2,1)S(1)} %bitcast.22), custom_call_target="tpu_custom_call" | custom-call | tf_op jit(solution)/shard_map/pallas_call | solution.py:148
  36.7 2.0 %collective-permute-start.3 = (bf16[64,1024]{1,0:T(8,128)(2,1)S(1)}, bf16[64,1024]{1,0:T(8,128)(2,1)S(1)}, u32[]{:S(2)}, u32[]{:S(2)}) collective-permute-start(bf16[64,1024]{1,0:T(8,128)(2,1)S(1)} %shard_map.49.refs_1_), channel_id=1, source_target_pairs={{32,0},{64,32},{96,64},{128,96},{160,128},{192,160},{224,192},{33,... | collective-permute-start | bytes 393224 | tf_op jit(solution)/shard_map/ppermute | solution.py:166
  38.7 0.0 collective-permute-done.1.refs_0_
  38.7 6.0 %collective-permute-done.3.refs_3_ = bf16[64,1024]{1,0:T(8,128)(2,1)S(1)} collective-permute-done((bf16[64,1024]{1,0:T(8,128)(2,1)S(1)}, bf16[64,1024]{1,0:T(8,128)(2,1)S(1)}, u32[]{:S(2)}, u32[]{:S(2)}) %collective-permute-start.3) | collective-permute-done | bytes 131104 | tf_op jit(solution)/shard_map/ppermute | solution.py:166
  44.8 0.3 shard_map.50
  45.0 11.8 %all_to_all.11 = bf16[16,8,1024]{2,1,0:T(8,128)(2,1)S(1)} all-to-all(bf16[16,8,1024]{2,1,0:T(8,128)(2,1)S(1)} %bitcast.24), channel_id=1, replica_groups=mesh['z'=8,'yh'=2,'core'=2,'ch'=8] {'yh','ch'}, dimensions={0} | all-to-all | bytes 524288 | tf_op jit(solution)/shard_map/all_to_all | solution.py:196
  56.9 0.2 copy.12
  57.1 0.8 %reshape.33 = bf16[8,32,512]{2,1,0:T(8,128)(2,1)} reshape(bf16[8,16,2,512]{3,2,1,0:T(2,128)(2,1)S(1)} %bitcast.27) | data formatting | bytes 524288 | tf_op jit(solution)/shard_map/reshape | solution.py:198
  (4 shorter events, 0.1 us)
Async XLA Ops:
  0.0 1.8 %copy-start = (bf16[8,32,512]{2,1,0:T(8,128)(2,1)S(1)}, bf16[8,32,512]{2,1,0:T(8,128)(2,1)}, u32[]{:S(2)}) copy-start(bf16[8,32,512]{2,1,0:T(8,128)(2,1)} %param.4) | copy-start | bytes 786436
  22.6 8.1 %collective-permute-start = (bf16[64,1024]{1,0:T(8,128)(2,1)S(1)}, bf16[64,1024]{1,0:T(8,128)(2,1)S(1)}, u32[]{:S(2)}, u32[]{:S(2)}) collective-permute-start(bf16[64,1024]{1,0:T(8,128)(2,1)S(1)} %shard_map.46.refs_0_.refs_1_), channel_id=1, source_target_pairs={{32,0},{64,32},{96,64},{128,96},{160,128},{192,160},{224,192},{33,... | collective-permute-start | bytes 393224 | tf_op jit(solution)/shard_map/ppermute | solution.py:166
  25.6 10.0 %collective-permute-start.2 = (bf16[64,1024]{1,0:T(8,128)(2,1)S(1)}, bf16[64,1024]{1,0:T(8,128)(2,1)S(1)}, u32[]{:S(2)}, u32[]{:S(2)}) collective-permute-start(bf16[64,1024]{1,0:T(8,128)(2,1)S(1)} %shard_map.47.refs_1_.refs_2_), channel_id=1, source_target_pairs={{0,32},{32,64},{64,96},{96,128},{128,160},{160,192},{192,224},{1,3... | collective-permute-start | bytes 393224 | tf_op jit(solution)/shard_map/ppermute | solution.py:166
  31.8 6.9 %collective-permute-start.1 = (bf16[64,1024]{1,0:T(8,128)(2,1)S(1)}, bf16[64,1024]{1,0:T(8,128)(2,1)S(1)}, u32[]{:S(2)}, u32[]{:S(2)}) collective-permute-start(bf16[64,1024]{1,0:T(8,128)(2,1)S(1)} %shard_map.48.refs_2_), channel_id=1, source_target_pairs={{0,32},{32,64},{64,96},{96,128},{128,160},{160,192},{192,224},{1,3... | collective-permute-start | bytes 393224 | tf_op jit(solution)/shard_map/ppermute | solution.py:166
  36.7 8.1 %collective-permute-start.3 = (bf16[64,1024]{1,0:T(8,128)(2,1)S(1)}, bf16[64,1024]{1,0:T(8,128)(2,1)S(1)}, u32[]{:S(2)}, u32[]{:S(2)}) collective-permute-start(bf16[64,1024]{1,0:T(8,128)(2,1)S(1)} %shard_map.49.refs_1_), channel_id=1, source_target_pairs={{32,0},{64,32},{96,64},{128,96},{160,128},{192,160},{224,192},{33,... | collective-permute-start | bytes 393224 | tf_op jit(solution)/shard_map/ppermute | solution.py:166

commit v15 on v9

v15 whole, which is shorter than its diff:
```python
import functools

import jax
import jax.numpy as jnp
from jax import lax
from jax.experimental import pallas as pl
from jax.experimental.pallas import tpu as pltpu
from jax.sharding import Mesh
from jax.sharding import PartitionSpec as P

X = 64
Y = 8
SLAB = ("z", "yh", "core")
GROUP = ("yh", "ch")


ANYWHERE_VMEM = pl.BlockSpec(memory_space=pltpu.VMEM)


def in_vmem(arrays):
    return [pltpu.with_memory_space_constraint(a, pltpu.VMEM) for a in arrays]


def pack_weights(plane_a, plane_b, depth):
    layers, out_part, chans = plane_a.shape[:3]
    planes = jnp.transpose(jnp.stack([plane_a, plane_b]), (2, 1, 0, 4, 5, 3))
    planes = planes.reshape(out_part, layers, 18 * chans)
    taps_d = jnp.transpose(depth, (1, 0, 3, 2)).reshape(out_part, layers, 3 * chans)
    return jnp.concatenate([planes, taps_d], axis=2)


def _masks(width):
    p = lax.broadcasted_iota(jnp.int32, (1, width), 1)
    yy = p % Y
    xx = (p // Y) % X
    xm = [xx >= 1, None, xx <= X - 2]
    ym = [yy >= 1, None, yy <= Y - 2]
    ok = []
    for a in range(3):
        row = []
        for b in range(3):
            if xm[a] is None:
                row.append(ym[b])
            elif ym[b] is None:
                row.append(xm[a])
            else:
                row.append(jnp.logical_and(xm[a], ym[b]))
        ok.append(row)
    return ok


def _plane(x, w, ok):
    width = x.shape[1]
    pieces = []
    for a in range(3):
        for b in range(3):
            d = (a - 1) * Y + (b - 1)
            moved = x if d == 0 else pltpu.roll(x, (-d) % width, 1)
            mask = ok[a][b]
            if mask is not None:
                moved = jnp.where(mask, moved, jnp.zeros_like(moved))
            pieces.append(moved)
    stacked = jnp.concatenate(pieces, axis=0)
    return jnp.dot(w, stacked, preferred_element_type=jnp.float32)


def shift_z(block, step):
    size = lax.axis_size("z")
    route = [(i, i + step) for i in range(size) if 0 <= i + step < size]
    return lax.ppermute(block, "z", route)


def _own_kernel(src_ref, o_ref, *, vol_cols, chans):
    h = jnp.concatenate([src_ref[:chans, :vol_cols], src_ref[chans:, :vol_cols]], axis=1)
    o_ref[...] = _planes(h, src_ref, 0, vol_cols, chans)


def _side_kernel(left_ref, right_ref, src_ref, o_ref, *, vol_cols, chans):
    h = jnp.concatenate(
        [left_ref[:chans], left_ref[chans:], right_ref[:chans], right_ref[chans:]], axis=1
    )
    o_ref[...] = _planes(h, src_ref, 0, vol_cols, chans)


def _planes(h, src_ref, layer, vol_cols, chans):
    ok = _masks(h.shape[1])
    rows = slice(layer * chans, (layer + 1) * chans)
    for k in range(2):
        at = vol_cols + k * 9 * chans
        w = src_ref[rows, at : at + 9 * chans]
        h = jnp.maximum(_plane(h, w, ok), 0.0).astype(jnp.bfloat16)
    return h


def _depth(parts, src_ref, layer, vol_cols, chans):
    rows = slice(layer * chans, (layer + 1) * chans)
    at = vol_cols + 18 * chans
    stacked = jnp.concatenate(parts, axis=0)
    return jnp.dot(src_ref[rows, at : at + 3 * chans], stacked, preferred_element_type=jnp.float32)


def _rest_kernel(side_ref, own_ref, keep_ref, src_ref, o_ref, *, vol_cols, chans):
    w = vol_cols
    q = [side_ref[:, :w], side_ref[:, w : 2 * w], own_ref[:, :w], own_ref[:, w:],
         side_ref[:, 2 * w : 3 * w], side_ref[:, 3 * w :]]
    total = _depth(
        [jnp.concatenate(q[0:4], axis=1), jnp.concatenate(q[1:5], axis=1), jnp.concatenate(q[2:6], axis=1)],
        src_ref, 0, vol_cols, chans,
    )
    total = jnp.where(keep_ref[...] > 0, total, 0.0)
    h = jnp.maximum(total, 0.0).astype(jnp.bfloat16)
    s = _planes(h, src_ref, 1, vol_cols, chans)
    total = _depth([s[:, : 2 * w], s[:, w : 3 * w], s[:, 2 * w :]], src_ref, 1, vol_cols, chans)
    h = jnp.maximum(total, 0.0).astype(jnp.bfloat16)
    o_ref[...] = jnp.concatenate([h[:, :w], h[:, w:]], axis=0)


def run(kernel, inputs, out_shape, **params):
    return pl.pallas_call(
        functools.partial(kernel, **params),
        out_shape=out_shape,
        in_specs=[ANYWHERE_VMEM] * len(inputs),
        out_specs=ANYWHERE_VMEM,
    )(*in_vmem(inputs))


def local(volume, plane_a, plane_b, depth):
    layers, out_part, chans = plane_a.shape[:3]
    part, slab, flat = volume.shape
    members = lax.axis_size("yh") * lax.axis_size("ch")
    per = slab // members
    vol_cols = per * flat
    sent_volume = jnp.transpose(volume.reshape(part, members, per, flat), (1, 0, 2, 3))
    sent_volume = sent_volume.reshape(members, part, vol_cols)
    weights = pack_weights(plane_a, plane_b, depth)
    mine = lax.dynamic_index_in_dim(weights, lax.axis_index("yh"), 1, keepdims=False)
    sent_weights = jnp.broadcast_to(mine[None], (members,) + mine.shape)
    sent = jnp.concatenate([sent_volume, sent_weights], axis=2)
    got = lax.all_to_all(sent, GROUP, split_axis=0, concat_axis=0, tiled=True)
    src = got.reshape(2 * chans, -1)
    raw = src[:, :vol_cols]
    left = shift_z(raw, 1)
    right = shift_z(raw, -1)
    z, last = lax.axis_index("z"), lax.axis_size("z") - 1
    lane = lax.broadcasted_iota(jnp.int32, (1, 4 * vol_cols), 1)
    outside = ((lane < vol_cols) & (z == 0)) | ((lane >= 3 * vol_cols) & (z == last))
    keep = jnp.where(outside, 0.0, 1.0).astype(jnp.float32)
    shape = functools.partial(pltpu.VMEM, dtype=jnp.bfloat16)
    own = run(_own_kernel, [src], shape((chans, 2 * vol_cols)), vol_cols=vol_cols, chans=chans)
    side = run(_side_kernel, [left, right, src], shape((chans, 4 * vol_cols)), vol_cols=vol_cols, chans=chans)
    out = run(_rest_kernel, [side, own, keep, src], shape((2 * chans, vol_cols)), vol_cols=vol_cols, chans=chans)
    h = lax.all_to_all(out.reshape(members, part, vol_cols), GROUP, split_axis=0, concat_axis=0, tiled=True)
    h = jnp.transpose(h.reshape(members, part, per, flat), (1, 0, 2, 3))
    return h.reshape(part, slab, flat)


def solution(mesh):
    slabs = mesh.shape["gz"]
    split = Mesh(
        mesh.devices.reshape(slabs // 4, 2, 2, mesh.shape["ch"]), ("z", "yh", "core", "ch")
    )
    return jax.shard_map(
        local,
        mesh=split,
        in_specs=(
            P("ch", SLAB, None),
            P(None, "ch", None, None, None),
            P(None, "ch", None, None, None),
            P(None, "ch", None, None),
        ),
        out_specs=P("ch", SLAB, None),
        check_vma=False,
    )
```

time: 72.5 us -> 57.5 us (0.79); the launches traced: 71.2 us -> 57.1 us
  blocking collectives: 32.1 us -> 12.5 us
  waiting for transfers between devices: 10.7 us -> 18.4 us
  local copies, waits for them, and re-layouts: 6.15 us -> 2.29 us
  other arithmetic: 0.06 us -> 1.75 us
  Pallas kernels: 9.38 us -> 8.08 us
  starting transfers between devices: 12.8 us -> 14 us
    all_to_all x1 -> x0, blocking collectives: 19.9 us -> none  [local(): got = lax.all_to_all(sent, GROUP, split_axis=0, concat_axis=0, tiled=True)]
    all_to_all x0 -> x1, waiting for transfers between devices: none -> 12.6 us  [local(): got = lax.all_to_all(sent, GROUP, split_axis=0, concat_axis=0, tiled=True)]
    all_to_all x0 -> x1, starting transfers between devices: none -> 7.03 us  [local(): got = lax.all_to_all(sent, GROUP, split_axis=0, concat_axis=0, tiled=True)]
    ppermute x4 -> x2, starting transfers between devices: 12.8 us -> 6.96 us  [shift_z(): return lax.ppermute(block, 'z', route)]
    ppermute x4 -> x2, waiting for transfers between devices: 10.7 us -> 5.82 us  [shift_z(): return lax.ppermute(block, 'z', route)]
    transpose x2 -> x1, local copies, waits for them, and re-layouts: 1.57 us -> 0.04 us  [pack_weights(): planes = jnp.transpose(jnp.stack([plane_a, plane_b]), (2, 1, 0, 4, 5, 3))]
    unnamed x8 -> x2, local copies, waits for them, and re-layouts: 1.32 us -> 0.01 us
    pallas_call x3, Pallas kernels: 9.38 us -> 8.08 us  [run(): pl.pallas_call(functools.partial(kernel, **params), out_shape=out_shape,...]
  transfers between devices with their start and end apart: 4 -> 3, of which waited for: 4 -> 3; matrix products, arithmetic and copies ran while one was open for 0% -> 0% of each run, Pallas kernels for 0% -> 3%
where the time goes in v15:
time: 57.5 us; the launch traced here: 57.1 us
  waiting for transfers between devices  18.4 us (32%)
  starting transfers between devices  14 us (24%)
  blocking collectives  12.5 us (22%)
  Pallas kernels  8.08 us (14%)
  local copies, waits for them, and re-layouts  2.29 us (4%)
  other arithmetic  1.75 us (3%)
    all_to_all x1, waiting for transfers between devices, local(): got = lax.all_to_all(sent, GROUP, split_axis=0, concat_axis=0, tiled=True)  12.6 us
    all_to_all x1, blocking collectives, local(): lax.all_to_all(out.reshape(members, part, vol_cols), GROUP, split_axis=0,...  12.5 us
    pallas_call x3, Pallas kernels, run(): pl.pallas_call(functools.partial(kernel, **params), out_shape=out_shape,...  8.08 us
    all_to_all x1, starting transfers between devices, local(): got = lax.all_to_all(sent, GROUP, split_axis=0, concat_axis=0, tiled=True)  7.03 us
    ppermute x2, starting transfers between devices, shift_z(): return lax.ppermute(block, 'z', route)  6.96 us
    ppermute x2, waiting for transfers between devices, shift_z(): return lax.ppermute(block, 'z', route)  5.82 us
  transfers between devices with their start and end apart: 3, of which 3 were waited for; matrix products, arithmetic and copies ran while one was open for 0% of the time, Pallas kernels for 3%

profile of v15, /device:TPU:96, one launch (start us, length us, event | category | flops | bytes accessed | tf_op | source)
XLA Modules:
  0.0 57.1 jit_solution(6583925497580840223)
XLA Ops:
  0.0 0.0 copy-start
  0.0 0.8 %maximum_bitcast_fusion = bf16[8,2,2,3,3,64]{5,0,4,3,1,2:T(8,128)(2,1)S(1)} fusion(bf16[1,2,8,64,3,3]{3,2,5,4,1,0:T(8,128)(2,1)} %bitcast.28, bf16[1,2,8,64,3,3]{3,2,5,4,1,0:T(8,128)(2,1)} %bitcast.29), kind=kLoop, calls=%fused_computation.2 | loop fusion | flops 18432 | bytes 73728 | tf_op jit(solution)/shard_map/transpose | solution.py:26
  0.9 0.1 reshape.60
  1.0 0.7 %copy.9 = bf16[8,2,3,64]{3,2,0,1:T(4,128)(2,1)S(1)} copy(bf16[8,2,3,64]{3,0,2,1:T(8,128)(2,1)} %bitcast.30) | data formatting | bytes 12288 | tf_op jit(solution)/shard_map/transpose | solution.py:28
  1.8 0.1 reshape.61
  1.8 0.0 copy-done
  1.8 0.1 reshape.58
  2.0 0.2 copy.7
  2.2 0.9 %pad_maximum_fusion = bf16[16,8,2368]{2,1,0:T(8,128)(2,1)} fusion(bf16[16,8,1344]{2,1,0:T(8,128)(2,1)S(1)} %broadcast_in_dim.17, bf16[16,8,1024]{2,1,0:T(8,128)(2,1)S(1)} %bitcast.24), kind=kLoop, calls=%fused_computation | loop fusion | flops 1212416 | bytes 1212416 | tf_op jit(solution)/shard_map/concatenate | solution.py:138
  3.0 7.0 %all-to-all-start = ((bf16[16,8,2368]{2,1,0:T(8,128)(2,1)}), bf16[16,8,2368]{2,1,0:T(8,128)(2,1)S(1)}, u32[]{:S(2)}, u32[]{:S(2)}) async-start(bf16[16,8,2368]{2,1,0:T(8,128)(2,1)} %pad_maximum_fusion), calls=%async_computation | async-start | bytes 1245184 | tf_op jit(solution)/shard_map/all_to_all | solution.py:139
  10.1 12.6 %all-to-all-done = bf16[16,8,2368]{2,1,0:T(8,128)(2,1)S(1)} async-done(((bf16[16,8,2368]{2,1,0:T(8,128)(2,1)}), bf16[16,8,2368]{2,1,0:T(8,128)(2,1)S(1)}, u32[]{:S(2)}, u32[]{:S(2)}) %all-to-all-start) | async-done | bytes 606240 | tf_op jit(solution)/shard_map/all_to_all | solution.py:139
  22.7 5.0 %collective-permute-start = (bf16[128,1024]{1,0:T(8,128)(2,1)S(1)}, bf16[128,1024]{1,0:T(8,128)(2,1)S(1)}, u32[]{:S(2)}, u32[]{:S(2)}) collective-permute-start(bf16[128,1024]{1,0:T(8,128)(2,1)S(1)} %slice.4), channel_id=1, source_target_pairs={{0,32},{32,64},{64,96},{96,128},{128,160},{160,192},{192,224},{1,3... | collective-permute-start | bytes 786440 | tf_op jit(solution)/shard_map/ppermute | solution.py:70
  27.7 1.9 %collective-permute-start.1 = (bf16[128,1024]{1,0:T(8,128)(2,1)S(1)}, bf16[128,1024]{1,0:T(8,128)(2,1)S(1)}, u32[]{:S(2)}, u32[]{:S(2)}) collective-permute-start(bf16[128,1024]{1,0:T(8,128)(2,1)S(1)} %slice.4), channel_id=1, source_target_pairs={{32,0},{64,32},{96,64},{128,96},{160,128},{192,160},{224,192},{33,... | collective-permute-start | bytes 786440 | tf_op jit(solution)/shard_map/ppermute | solution.py:70
  29.7 1.7 %shard_map.47.own_ref = bf16[64,2048]{1,0:T(8,128)(2,1)S(1)} custom-call(bf16[128,2368]{1,0:T(8,128)(2,1)S(1)} %bitcast.20), custom_call_target="tpu_custom_call" | custom-call | tf_op jit(solution)/shard_map/pallas_call | solution.py:119
  31.4 0.5 collective-permute-done.left_ref
  31.9 5.3 %collective-permute-done.1.right_ref = bf16[128,1024]{1,0:T(8,128)(2,1)S(1)} collective-permute-done((bf16[128,1024]{1,0:T(8,128)(2,1)S(1)}, bf16[128,1024]{1,0:T(8,128)(2,1)S(1)}, u32[]{:S(2)}, u32[]{:S(2)}) %collective-permute-start.1) | collective-permute-done | bytes 262176 | tf_op jit(solution)/shard_map/ppermute | solution.py:70
  37.2 3.1 %shard_map.46.side_ref = bf16[64,4096]{1,0:T(8,128)(2,1)S(1)} custom-call(bf16[128,1024]{1,0:T(8,128)(2,1)S(1)} %collective-permute-done.left_ref, bf16[128,1024]{1,0:T(8,128)(2,1)S(1)} %collective-permute-done.1.right_ref, bf16[128,2368]{1,0:T(8,128)(2,1)S(1)} %bitcast.21), custom_call_target="tpu_custom_call" | custom-call | tf_op jit(solution)/shard_map/pallas_call | solution.py:119
  40.3 3.3 %shard_map.48 = bf16[128,1024]{1,0:T(8,128)(2,1)S(1)} custom-call(bf16[64,4096]{1,0:T(8,128)(2,1)S(1)} %shard_map.46.side_ref, bf16[64,2048]{1,0:T(8,128)(2,1)S(1)} %shard_map.47.own_ref, f32[1,4096]{1,0:T(1,128)S(1)} %or_select_fusion.keep_ref, bf16[128,2368]{1,0:T(8,128)(2,1)S(1)} %bitcast.22), custom_call_target="tpu_custom_call" | custom-call | tf_op jit(solution)/shard_map/pallas_call | solution.py:119
  43.6 12.5 %all_to_all.10 = bf16[16,8,1024]{2,1,0:T(8,128)(2,1)S(1)} all-to-all(bf16[16,8,1024]{2,1,0:T(8,128)(2,1)S(1)} %bitcast.23), channel_id=1, replica_groups=mesh['z'=8,'yh'=2,'core'=2,'ch'=8] {'yh','ch'}, dimensions={0} | all-to-all | bytes 524288 | tf_op jit(solution)/shard_map/all_to_all | solution.py:152
  56.1 0.2 copy.12
  56.3 0.8 %reshape.65 = bf16[8,32,512]{2,1,0:T(8,128)(2,1)} reshape(bf16[8,16,2,512]{3,2,1,0:T(2,128)(2,1)S(1)} %bitcast.26) | data formatting | bytes 524288 | tf_op jit(solution)/shard_map/reshape | solution.py:154
  (5 shorter events, 0.1 us)
Async XLA Ops:
  0.0 1.8 %copy-start = (bf16[8,32,512]{2,1,0:T(8,128)(2,1)S(1)}, bf16[8,32,512]{2,1,0:T(8,128)(2,1)}, u32[]{:S(2)}) copy-start(bf16[8,32,512]{2,1,0:T(8,128)(2,1)} %param.4) | copy-start | bytes 786436
  3.0 19.6 %all-to-all-start = ((bf16[16,8,2368]{2,1,0:T(8,128)(2,1)}), bf16[16,8,2368]{2,1,0:T(8,128)(2,1)S(1)}, u32[]{:S(2)}, u32[]{:S(2)}) async-start(bf16[16,8,2368]{2,1,0:T(8,128)(2,1)} %pad_maximum_fusion), calls=%async_computation | async-start | bytes 1245184 | tf_op jit(solution)/shard_map/all_to_all | solution.py:139
  22.7 9.2 %collective-permute-start = (bf16[128,1024]{1,0:T(8,128)(2,1)S(1)}, bf16[128,1024]{1,0:T(8,128)(2,1)S(1)}, u32[]{:S(2)}, u32[]{:S(2)}) collective-permute-start(bf16[128,1024]{1,0:T(8,128)(2,1)S(1)} %slice.4), channel_id=1, source_target_pairs={{0,32},{32,64},{64,96},{96,128},{128,160},{160,192},{192,224},{1,3... | collective-permute-start | bytes 786440 | tf_op jit(solution)/shard_map/ppermute | solution.py:70
  27.7 9.5 %collective-permute-start.1 = (bf16[128,1024]{1,0:T(8,128)(2,1)S(1)}, bf16[128,1024]{1,0:T(8,128)(2,1)S(1)}, u32[]{:S(2)}, u32[]{:S(2)}) collective-permute-start(bf16[128,1024]{1,0:T(8,128)(2,1)S(1)} %slice.4), channel_id=1, source_target_pairs={{32,0},{64,32},{96,64},{128,96},{160,128},{192,160},{224,192},{33,... | collective-permute-start | bytes 786440 | tf_op jit(solution)/shard_map/ppermute | solution.py:70

commit v16 on v15

--- a/solution.py
+++ b/solution.py
@@ -75,10 +75,8 @@
     o_ref[...] = _planes(h, src_ref, 0, vol_cols, chans)
 
 
-def _side_kernel(left_ref, right_ref, src_ref, o_ref, *, vol_cols, chans):
-    h = jnp.concatenate(
-        [left_ref[:chans], left_ref[chans:], right_ref[:chans], right_ref[chans:]], axis=1
-    )
+def _side_kernel(side_ref, src_ref, o_ref, *, vol_cols, chans):
+    h = jnp.concatenate([side_ref[:chans], side_ref[chans:]], axis=1)
     o_ref[...] = _planes(h, src_ref, 0, vol_cols, chans)
 
 
@@ -99,10 +97,10 @@
     return jnp.dot(src_ref[rows, at : at + 3 * chans], stacked, preferred_element_type=jnp.float32)
 
 
-def _rest_kernel(side_ref, own_ref, keep_ref, src_ref, o_ref, *, vol_cols, chans):
+def _rest_kernel(left_ref, own_ref, right_ref, keep_ref, src_ref, o_ref, *, vol_cols, chans):
     w = vol_cols
-    q = [side_ref[:, :w], side_ref[:, w : 2 * w], own_ref[:, :w], own_ref[:, w:],
-         side_ref[:, 2 * w : 3 * w], side_ref[:, 3 * w :]]
+    q = [left_ref[:, :w], left_ref[:, w:], own_ref[:, :w], own_ref[:, w:],
+         right_ref[:, :w], right_ref[:, w:]]
     total = _depth(
         [jnp.concatenate(q[0:4], axis=1), jnp.concatenate(q[1:5], axis=1), jnp.concatenate(q[2:6], axis=1)],
         src_ref, 0, vol_cols, chans,
@@ -147,8 +145,13 @@
     keep = jnp.where(outside, 0.0, 1.0).astype(jnp.float32)
     shape = functools.partial(pltpu.VMEM, dtype=jnp.bfloat16)
     own = run(_own_kernel, [src], shape((chans, 2 * vol_cols)), vol_cols=vol_cols, chans=chans)
-    side = run(_side_kernel, [left, right, src], shape((chans, 4 * vol_cols)), vol_cols=vol_cols, chans=chans)
-    out = run(_rest_kernel, [side, own, keep, src], shape((2 * chans, vol_cols)), vol_cols=vol_cols, chans=chans)
+    pair = shape((chans, 2 * vol_cols))
+    left = run(_side_kernel, [left, src], pair, vol_cols=vol_cols, chans=chans)
+    right = run(_side_kernel, [right, src], pair, vol_cols=vol_cols, chans=chans)
+    out = run(
+        _rest_kernel, [left, own, right, keep, src], shape((2 * chans, vol_cols)),
+        vol_cols=vol_cols, chans=chans,
+    )
     h = lax.all_to_all(out.reshape(members, part, vol_cols), GROUP, split_axis=0, concat_axis=0, tiled=True)
     h = jnp.transpose(h.reshape(members, part, per, flat), (1, 0, 2, 3))
     return h.reshape(part, slab, flat)

time: 57.5 us -> 53.3 us (0.927)
  waiting for transfers between devices: 18.4 us -> 13.7 us
    ppermute x2, waiting for transfers between devices: 5.82 us -> 1.15 us  [shift_z(): return lax.ppermute(block, 'z', route)]
    pallas_call x3 -> x4, Pallas kernels: 8.08 us -> 8.44 us  [run(): pl.pallas_call(functools.partial(kernel, **params), out_shape=out_shape,...]
  transfers between devices with their start and end apart: 3 -> 3, of which waited for: 3 -> 2; matrix products, arithmetic and copies ran while one was open for 0% -> 0% of each run, Pallas kernels for 3% -> 6%
where the time goes in v16:
time: 53.3 us; the launch traced here: 52.9 us
  starting transfers between devices  14.1 us (26%)
  waiting for transfers between devices  13.7 us (26%)
  blocking collectives  12.5 us (23%)
  Pallas kernels  8.44 us (16%)
  local copies, waits for them, and re-layouts  2.29 us (4%)
  other arithmetic  1.75 us (3%)
    all_to_all x1, waiting for transfers between devices, local(): got = lax.all_to_all(sent, GROUP, split_axis=0, concat_axis=0, tiled=True)  12.6 us
    all_to_all x1, blocking collectives, local(): lax.all_to_all(out.reshape(members, part, vol_cols), GROUP, split_axis=0,...  12.5 us
    pallas_call x4, Pallas kernels, run(): pl.pallas_call(functools.partial(kernel, **params), out_shape=out_shape,...  8.44 us
    ppermute x2, starting transfers between devices, shift_z(): return lax.ppermute(block, 'z', route)  7.05 us
    all_to_all x1, starting transfers between devices, local(): got = lax.all_to_all(sent, GROUP, split_axis=0, concat_axis=0, tiled=True)  7.03 us
    ppermute x2, waiting for transfers between devices, shift_z(): return lax.ppermute(block, 'z', route)  1.15 us
  transfers between devices with their start and end apart: 3, of which 2 were waited for; matrix products, arithmetic and copies ran while one was open for 0% of the time, Pallas kernels for 6%

profile of v16, /device:TPU:96, one launch (start us, length us, event | category | flops | bytes accessed | tf_op | source)
XLA Modules:
  0.0 52.9 jit_solution(11518847936264698903)
XLA Ops:
  0.0 0.0 copy-start
  0.0 0.8 %maximum_bitcast_fusion = bf16[8,2,2,3,3,64]{5,0,4,3,1,2:T(8,128)(2,1)S(1)} fusion(bf16[1,2,8,64,3,3]{3,2,5,4,1,0:T(8,128)(2,1)} %bitcast.29, bf16[1,2,8,64,3,3]{3,2,5,4,1,0:T(8,128)(2,1)} %bitcast.30), kind=kLoop, calls=%fused_computation.2 | loop fusion | flops 18432 | bytes 73728 | tf_op jit(solution)/shard_map/transpose | solution.py:26
  0.9 0.1 reshape.60
  1.0 0.7 %copy.9 = bf16[8,2,3,64]{3,2,0,1:T(4,128)(2,1)S(1)} copy(bf16[8,2,3,64]{3,0,2,1:T(8,128)(2,1)} %bitcast.31) | data formatting | bytes 12288 | tf_op jit(solution)/shard_map/transpose | solution.py:28
  1.8 0.1 reshape.61
  1.8 0.0 copy-done
  1.8 0.1 reshape.58
  2.0 0.2 copy.7
  2.2 0.9 %pad_maximum_fusion = bf16[16,8,2368]{2,1,0:T(8,128)(2,1)} fusion(bf16[16,8,1344]{2,1,0:T(8,128)(2,1)S(1)} %broadcast_in_dim.17, bf16[16,8,1024]{2,1,0:T(8,128)(2,1)S(1)} %bitcast.25), kind=kLoop, calls=%fused_computation | loop fusion | flops 1212416 | bytes 1212416 | tf_op jit(solution)/shard_map/concatenate | solution.py:136
  3.0 7.0 %all-to-all-start = ((bf16[16,8,2368]{2,1,0:T(8,128)(2,1)}), bf16[16,8,2368]{2,1,0:T(8,128)(2,1)S(1)}, u32[]{:S(2)}, u32[]{:S(2)}) async-start(bf16[16,8,2368]{2,1,0:T(8,128)(2,1)} %pad_maximum_fusion), calls=%async_computation | async-start | bytes 1245184 | tf_op jit(solution)/shard_map/all_to_all | solution.py:137
  10.1 12.6 %all-to-all-done = bf16[16,8,2368]{2,1,0:T(8,128)(2,1)S(1)} async-done(((bf16[16,8,2368]{2,1,0:T(8,128)(2,1)}), bf16[16,8,2368]{2,1,0:T(8,128)(2,1)S(1)}, u32[]{:S(2)}, u32[]{:S(2)}) %all-to-all-start) | async-done | bytes 606240 | tf_op jit(solution)/shard_map/all_to_all | solution.py:137
  22.7 2.0 %collective-permute-start.1 = (bf16[128,1024]{1,0:T(8,128)(2,1)S(1)}, bf16[128,1024]{1,0:T(8,128)(2,1)S(1)}, u32[]{:S(2)}, u32[]{:S(2)}) collective-permute-start(bf16[128,1024]{1,0:T(8,128)(2,1)S(1)} %slice.4), channel_id=1, source_target_pairs={{32,0},{64,32},{96,64},{128,96},{160,128},{192,160},{224,192},{33,... | collective-permute-start | bytes 786440 | tf_op jit(solution)/shard_map/ppermute | solution.py:70
  24.7 5.0 %collective-permute-start = (bf16[128,1024]{1,0:T(8,128)(2,1)S(1)}, bf16[128,1024]{1,0:T(8,128)(2,1)S(1)}, u32[]{:S(2)}, u32[]{:S(2)}) collective-permute-start(bf16[128,1024]{1,0:T(8,128)(2,1)S(1)} %slice.4), channel_id=1, source_target_pairs={{0,32},{32,64},{64,96},{96,128},{128,160},{160,192},{192,224},{1,3... | collective-permute-start | bytes 786440 | tf_op jit(solution)/shard_map/ppermute | solution.py:70
  29.8 1.7 %shard_map.47.own_ref = bf16[64,2048]{1,0:T(8,128)(2,1)S(1)} custom-call(bf16[128,2368]{1,0:T(8,128)(2,1)S(1)} %bitcast.20), custom_call_target="tpu_custom_call" | custom-call | tf_op jit(solution)/shard_map/pallas_call | solution.py:117
  31.5 1.1 %collective-permute-done.1.side_ref = bf16[128,1024]{1,0:T(8,128)(2,1)S(1)} collective-permute-done((bf16[128,1024]{1,0:T(8,128)(2,1)S(1)}, bf16[128,1024]{1,0:T(8,128)(2,1)S(1)}, u32[]{:S(2)}, u32[]{:S(2)}) %collective-permute-start.1) | collective-permute-done | bytes 262176 | tf_op jit(solution)/shard_map/ppermute | solution.py:70
  32.6 1.7 %shard_map.48.right_ref = bf16[64,2048]{1,0:T(8,128)(2,1)S(1)} custom-call(bf16[128,1024]{1,0:T(8,128)(2,1)S(1)} %collective-permute-done.1.side_ref, bf16[128,2368]{1,0:T(8,128)(2,1)S(1)} %bitcast.21), custom_call_target="tpu_custom_call" | custom-call | tf_op jit(solution)/shard_map/pallas_call | solution.py:117
  34.4 0.0 collective-permute-done.side_ref
  34.4 1.7 %shard_map.46.left_ref = bf16[64,2048]{1,0:T(8,128)(2,1)S(1)} custom-call(bf16[128,1024]{1,0:T(8,128)(2,1)S(1)} %collective-permute-done.side_ref, bf16[128,2368]{1,0:T(8,128)(2,1)S(1)} %bitcast.22), custom_call_target="tpu_custom_call" | custom-call | tf_op jit(solution)/shard_map/pallas_call | solution.py:117
  36.1 3.3 %shard_map.49 = bf16[128,1024]{1,0:T(8,128)(2,1)S(1)} custom-call(bf16[64,2048]{1,0:T(8,128)(2,1)S(1)} %shard_map.46.left_ref, bf16[64,2048]{1,0:T(8,128)(2,1)S(1)} %shard_map.47.own_ref, bf16[64,2048]{1,0:T(8,128)(2,1)S(1)} %shard_map.48.right_ref, f32[1,4096]{1,0:T(1,128)S(1)} %or_select_fusion.keep_ref, bf16[128,2368]{1,0:T(8,128)(2,1)S(1)} %bitcast.23), custom_call_target="tpu_custom_call" | custom-call | tf_op jit(solution)/shard_map/pallas_call | solution.py:117
  39.4 12.5 %all_to_all.10 = bf16[16,8,1024]{2,1,0:T(8,128)(2,1)S(1)} all-to-all(bf16[16,8,1024]{2,1,0:T(8,128)(2,1)S(1)} %bitcast.24), channel_id=1, replica_groups=mesh['z'=8,'yh'=2,'core'=2,'ch'=8] {'yh','ch'}, dimensions={0} | all-to-all | bytes 524288 | tf_op jit(solution)/shard_map/all_to_all | solution.py:155
  51.9 0.2 copy.12
  52.1 0.8 %reshape.65 = bf16[8,32,512]{2,1,0:T(8,128)(2,1)} reshape(bf16[8,16,2,512]{3,2,1,0:T(2,128)(2,1)S(1)} %bitcast.27) | data formatting | bytes 524288 | tf_op jit(solution)/shard_map/reshape | solution.py:157
  (5 shorter events, 0.1 us)
Async XLA Ops:
  0.0 1.8 %copy-start = (bf16[8,32,512]{2,1,0:T(8,128)(2,1)S(1)}, bf16[8,32,512]{2,1,0:T(8,128)(2,1)}, u32[]{:S(2)}) copy-start(bf16[8,32,512]{2,1,0:T(8,128)(2,1)} %param.4) | copy-start | bytes 786436
  3.0 19.6 %all-to-all-start = ((bf16[16,8,2368]{2,1,0:T(8,128)(2,1)}), bf16[16,8,2368]{2,1,0:T(8,128)(2,1)S(1)}, u32[]{:S(2)}, u32[]{:S(2)}) async-start(bf16[16,8,2368]{2,1,0:T(8,128)(2,1)} %pad_maximum_fusion), calls=%async_computation | async-start | bytes 1245184 | tf_op jit(solution)/shard_map/all_to_all | solution.py:137
  22.7 9.9 %collective-permute-start.1 = (bf16[128,1024]{1,0:T(8,128)(2,1)S(1)}, bf16[128,1024]{1,0:T(8,128)(2,1)S(1)}, u32[]{:S(2)}, u32[]{:S(2)}) collective-permute-start(bf16[128,1024]{1,0:T(8,128)(2,1)S(1)} %slice.4), channel_id=1, source_target_pairs={{32,0},{64,32},{96,64},{128,96},{160,128},{192,160},{224,192},{33,... | collective-permute-start | bytes 786440 | tf_op jit(solution)/shard_map/ppermute | solution.py:70
  24.7 9.6 %collective-permute-start = (bf16[128,1024]{1,0:T(8,128)(2,1)S(1)}, bf16[128,1024]{1,0:T(8,128)(2,1)S(1)}, u32[]{:S(2)}, u32[]{:S(2)}) collective-permute-start(bf16[128,1024]{1,0:T(8,128)(2,1)S(1)} %slice.4), channel_id=1, source_target_pairs={{0,32},{32,64},{64,96},{96,128},{128,160},{160,192},{192,224},{1,3... | collective-permute-start | bytes 786440 | tf_op jit(solution)/shard_map/ppermute | solution.py:70

commit v17 on v16

--- a/solution.py
+++ b/solution.py
@@ -122,8 +122,8 @@
     )(*in_vmem(inputs))
 
 
-def local(volume, plane_a, plane_b, depth):
-    layers, out_part, chans = plane_a.shape[:3]
+def layers_of(volume, plane_a, plane_b, depth):
+    _, _, chans = plane_a.shape[:3]
     part, slab, flat = volume.shape
     members = lax.axis_size("yh") * lax.axis_size("ch")
     per = slab // members
@@ -163,7 +163,7 @@
         mesh.devices.reshape(slabs // 4, 2, 2, mesh.shape["ch"]), ("z", "yh", "core", "ch")
     )
     return jax.shard_map(
-        local,
+        layers_of,
         mesh=split,
         in_specs=(
             P("ch", SLAB, None),

time: 53.3 us -> 53.3 us (level)
  no operation moved by 1% of the time
where the time goes in v17:
time: 53.3 us; the launch traced here: 52.9 us
  starting transfers between devices  14.1 us (26%)
  waiting for transfers between devices  13.7 us (26%)
  blocking collectives  12.5 us (23%)
  Pallas kernels  8.44 us (16%)
  local copies, waits for them, and re-layouts  2.29 us (4%)
  other arithmetic  1.75 us (3%)
    all_to_all x1, waiting for transfers between devices, layers_of(): got = lax.all_to_all(sent, GROUP, split_axis=0, concat_axis=0, tiled=True)  12.6 us
    all_to_all x1, blocking collectives, layers_of(): lax.all_to_all(out.reshape(members, part, vol_cols), GROUP, split_axis=0,...  12.5 us
    pallas_call x4, Pallas kernels, run(): pl.pallas_call(functools.partial(kernel, **params), out_shape=out_shape,...  8.44 us
    ppermute x2, starting transfers between devices, shift_z(): return lax.ppermute(block, 'z', route)  7.05 us
    all_to_all x1, starting transfers between devices, layers_of(): got = lax.all_to_all(sent, GROUP, split_axis=0, concat_axis=0, tiled=True)  7.03 us
    ppermute x2, waiting for transfers between devices, shift_z(): return lax.ppermute(block, 'z', route)  1.15 us
  transfers between devices with their start and end apart: 3, of which 2 were waited for; matrix products, arithmetic and copies ran while one was open for 0% of the time, Pallas kernels for 6%

profile of v17, /device:TPU:96, one launch (start us, length us, event | category | flops | bytes accessed | tf_op | source)
XLA Modules:
  0.0 52.9 jit_solution(11518847936264698903)
XLA Ops:
  0.0 0.0 copy-start
  0.0 0.8 %maximum_bitcast_fusion = bf16[8,2,2,3,3,64]{5,0,4,3,1,2:T(8,128)(2,1)S(1)} fusion(bf16[1,2,8,64,3,3]{3,2,5,4,1,0:T(8,128)(2,1)} %bitcast.29, bf16[1,2,8,64,3,3]{3,2,5,4,1,0:T(8,128)(2,1)} %bitcast.30), kind=kLoop, calls=%fused_computation.2 | loop fusion | flops 18432 | bytes 73728 | tf_op jit(solution)/shard_map/transpose | solution.py:26
  0.9 0.1 reshape.60
  1.0 0.7 %copy.9 = bf16[8,2,3,64]{3,2,0,1:T(4,128)(2,1)S(1)} copy(bf16[8,2,3,64]{3,0,2,1:T(8,128)(2,1)} %bitcast.31) | data formatting | bytes 12288 | tf_op jit(solution)/shard_map/transpose | solution.py:28
  1.8 0.1 reshape.61
  1.8 0.0 copy-done
  1.8 0.1 reshape.58
  2.0 0.2 copy.7
  2.2 0.9 %pad_maximum_fusion = bf16[16,8,2368]{2,1,0:T(8,128)(2,1)} fusion(bf16[16,8,1344]{2,1,0:T(8,128)(2,1)S(1)} %broadcast_in_dim.17, bf16[16,8,1024]{2,1,0:T(8,128)(2,1)S(1)} %bitcast.25), kind=kLoop, calls=%fused_computation | loop fusion | flops 1212416 | bytes 1212416 | tf_op jit(solution)/shard_map/concatenate | solution.py:136
  3.0 7.0 %all-to-all-start = ((bf16[16,8,2368]{2,1,0:T(8,128)(2,1)}), bf16[16,8,2368]{2,1,0:T(8,128)(2,1)S(1)}, u32[]{:S(2)}, u32[]{:S(2)}) async-start(bf16[16,8,2368]{2,1,0:T(8,128)(2,1)} %pad_maximum_fusion), calls=%async_computation | async-start | bytes 1245184 | tf_op jit(solution)/shard_map/all_to_all | solution.py:137
  10.1 12.6 %all-to-all-done = bf16[16,8,2368]{2,1,0:T(8,128)(2,1)S(1)} async-done(((bf16[16,8,2368]{2,1,0:T(8,128)(2,1)}), bf16[16,8,2368]{2,1,0:T(8,128)(2,1)S(1)}, u32[]{:S(2)}, u32[]{:S(2)}) %all-to-all-start) | async-done | bytes 606240 | tf_op jit(solution)/shard_map/all_to_all | solution.py:137
  22.7 2.0 %collective-permute-start.1 = (bf16[128,1024]{1,0:T(8,128)(2,1)S(1)}, bf16[128,1024]{1,0:T(8,128)(2,1)S(1)}, u32[]{:S(2)}, u32[]{:S(2)}) collective-permute-start(bf16[128,1024]{1,0:T(8,128)(2,1)S(1)} %slice.4), channel_id=1, source_target_pairs={{32,0},{64,32},{96,64},{128,96},{160,128},{192,160},{224,192},{33,... | collective-permute-start | bytes 786440 | tf_op jit(solution)/shard_map/ppermute | solution.py:70
  24.7 5.0 %collective-permute-start = (bf16[128,1024]{1,0:T(8,128)(2,1)S(1)}, bf16[128,1024]{1,0:T(8,128)(2,1)S(1)}, u32[]{:S(2)}, u32[]{:S(2)}) collective-permute-start(bf16[128,1024]{1,0:T(8,128)(2,1)S(1)} %slice.4), channel_id=1, source_target_pairs={{0,32},{32,64},{64,96},{96,128},{128,160},{160,192},{192,224},{1,3... | collective-permute-start | bytes 786440 | tf_op jit(solution)/shard_map/ppermute | solution.py:70
  29.8 1.7 %shard_map.47.own_ref = bf16[64,2048]{1,0:T(8,128)(2,1)S(1)} custom-call(bf16[128,2368]{1,0:T(8,128)(2,1)S(1)} %bitcast.20), custom_call_target="tpu_custom_call" | custom-call | tf_op jit(solution)/shard_map/pallas_call | solution.py:117
  31.5 1.1 %collective-permute-done.1.side_ref = bf16[128,1024]{1,0:T(8,128)(2,1)S(1)} collective-permute-done((bf16[128,1024]{1,0:T(8,128)(2,1)S(1)}, bf16[128,1024]{1,0:T(8,128)(2,1)S(1)}, u32[]{:S(2)}, u32[]{:S(2)}) %collective-permute-start.1) | collective-permute-done | bytes 262176 | tf_op jit(solution)/shard_map/ppermute | solution.py:70
  32.6 1.7 %shard_map.48.right_ref = bf16[64,2048]{1,0:T(8,128)(2,1)S(1)} custom-call(bf16[128,1024]{1,0:T(8,128)(2,1)S(1)} %collective-permute-done.1.side_ref, bf16[128,2368]{1,0:T(8,128)(2,1)S(1)} %bitcast.21), custom_call_target="tpu_custom_call" | custom-call | tf_op jit(solution)/shard_map/pallas_call | solution.py:117
  34.4 0.0 collective-permute-done.side_ref
  34.4 1.7 %shard_map.46.left_ref = bf16[64,2048]{1,0:T(8,128)(2,1)S(1)} custom-call(bf16[128,1024]{1,0:T(8,128)(2,1)S(1)} %collective-permute-done.side_ref, bf16[128,2368]{1,0:T(8,128)(2,1)S(1)} %bitcast.22), custom_call_target="tpu_custom_call" | custom-call | tf_op jit(solution)/shard_map/pallas_call | solution.py:117
  36.1 3.3 %shard_map.49 = bf16[128,1024]{1,0:T(8,128)(2,1)S(1)} custom-call(bf16[64,2048]{1,0:T(8,128)(2,1)S(1)} %shard_map.46.left_ref, bf16[64,2048]{1,0:T(8,128)(2,1)S(1)} %shard_map.47.own_ref, bf16[64,2048]{1,0:T(8,128)(2,1)S(1)} %shard_map.48.right_ref, f32[1,4096]{1,0:T(1,128)S(1)} %or_select_fusion.keep_ref, bf16[128,2368]{1,0:T(8,128)(2,1)S(1)} %bitcast.23), custom_call_target="tpu_custom_call" | custom-call | tf_op jit(solution)/shard_map/pallas_call | solution.py:117
  39.4 12.5 %all_to_all.10 = bf16[16,8,1024]{2,1,0:T(8,128)(2,1)S(1)} all-to-all(bf16[16,8,1024]{2,1,0:T(8,128)(2,1)S(1)} %bitcast.24), channel_id=1, replica_groups=mesh['z'=8,'yh'=2,'core'=2,'ch'=8] {'yh','ch'}, dimensions={0} | all-to-all | bytes 524288 | tf_op jit(solution)/shard_map/all_to_all | solution.py:155
  51.9 0.2 copy.12
  52.1 0.8 %reshape.65 = bf16[8,32,512]{2,1,0:T(8,128)(2,1)} reshape(bf16[8,16,2,512]{3,2,1,0:T(2,128)(2,1)S(1)} %bitcast.27) | data formatting | bytes 524288 | tf_op jit(solution)/shard_map/reshape | solution.py:157
  (5 shorter events, 0.1 us)
Async XLA Ops:
  0.0 1.8 %copy-start = (bf16[8,32,512]{2,1,0:T(8,128)(2,1)S(1)}, bf16[8,32,512]{2,1,0:T(8,128)(2,1)}, u32[]{:S(2)}) copy-start(bf16[8,32,512]{2,1,0:T(8,128)(2,1)} %param.4) | copy-start | bytes 786436
  3.0 19.6 %all-to-all-start = ((bf16[16,8,2368]{2,1,0:T(8,128)(2,1)}), bf16[16,8,2368]{2,1,0:T(8,128)(2,1)S(1)}, u32[]{:S(2)}, u32[]{:S(2)}) async-start(bf16[16,8,2368]{2,1,0:T(8,128)(2,1)} %pad_maximum_fusion), calls=%async_computation | async-start | bytes 1245184 | tf_op jit(solution)/shard_map/all_to_all | solution.py:137
  22.7 9.9 %collective-permute-start.1 = (bf16[128,1024]{1,0:T(8,128)(2,1)S(1)}, bf16[128,1024]{1,0:T(8,128)(2,1)S(1)}, u32[]{:S(2)}, u32[]{:S(2)}) collective-permute-start(bf16[128,1024]{1,0:T(8,128)(2,1)S(1)} %slice.4), channel_id=1, source_target_pairs={{32,0},{64,32},{96,64},{128,96},{160,128},{192,160},{224,192},{33,... | collective-permute-start | bytes 786440 | tf_op jit(solution)/shard_map/ppermute | solution.py:70
  24.7 9.6 %collective-permute-start = (bf16[128,1024]{1,0:T(8,128)(2,1)S(1)}, bf16[128,1024]{1,0:T(8,128)(2,1)S(1)}, u32[]{:S(2)}, u32[]{:S(2)}) collective-permute-start(bf16[128,1024]{1,0:T(8,128)(2,1)S(1)} %slice.4), channel_id=1, source_target_pairs={{0,32},{32,64},{64,96},{96,128},{128,160},{160,192},{192,224},{1,3... | collective-permute-start | bytes 786440 | tf_op jit(solution)/shard_map/ppermute | solution.py:70

commit v18 on v16

--- a/solution.py
+++ b/solution.py
@@ -97,7 +97,7 @@
     return jnp.dot(src_ref[rows, at : at + 3 * chans], stacked, preferred_element_type=jnp.float32)
 
 
-def _rest_kernel(left_ref, own_ref, right_ref, keep_ref, src_ref, o_ref, *, vol_cols, chans):
+def _rest_kernel(left_ref, own_ref, right_ref, src_ref, o_ref, *, vol_cols, chans):
     w = vol_cols
     q = [left_ref[:, :w], left_ref[:, w:], own_ref[:, :w], own_ref[:, w:],
          right_ref[:, :w], right_ref[:, w:]]
@@ -105,7 +105,12 @@
         [jnp.concatenate(q[0:4], axis=1), jnp.concatenate(q[1:5], axis=1), jnp.concatenate(q[2:6], axis=1)],
         src_ref, 0, vol_cols, chans,
     )
-    total = jnp.where(keep_ref[...] > 0, total, 0.0)
+    z, last = lax.axis_index("z"), lax.axis_size("z") - 1
+    lane = lax.broadcasted_iota(jnp.int32, (1, 4 * w), 1)
+    outside = jnp.logical_or(
+        jnp.logical_and(lane < w, z == 0), jnp.logical_and(lane >= 3 * w, z == last)
+    )
+    total = jnp.where(outside, 0.0, total)
     h = jnp.maximum(total, 0.0).astype(jnp.bfloat16)
     s = _planes(h, src_ref, 1, vol_cols, chans)
     total = _depth([s[:, : 2 * w], s[:, w : 3 * w], s[:, 2 * w :]], src_ref, 1, vol_cols, chans)
@@ -139,17 +144,13 @@
     raw = src[:, :vol_cols]
     left = shift_z(raw, 1)
     right = shift_z(raw, -1)
-    z, last = lax.axis_index("z"), lax.axis_size("z") - 1
-    lane = lax.broadcasted_iota(jnp.int32, (1, 4 * vol_cols), 1)
-    outside = ((lane < vol_cols) & (z == 0)) | ((lane >= 3 * vol_cols) & (z == last))
-    keep = jnp.where(outside, 0.0, 1.0).astype(jnp.float32)
     shape = functools.partial(pltpu.VMEM, dtype=jnp.bfloat16)
     own = run(_own_kernel, [src], shape((chans, 2 * vol_cols)), vol_cols=vol_cols, chans=chans)
     pair = shape((chans, 2 * vol_cols))
     left = run(_side_kernel, [left, src], pair, vol_cols=vol_cols, chans=chans)
     right = run(_side_kernel, [right, src], pair, vol_cols=vol_cols, chans=chans)
     out = run(
-        _rest_kernel, [left, own, right, keep, src], shape((2 * chans, vol_cols)),
+        _rest_kernel, [left, own, right, src], shape((2 * chans, vol_cols)),
         vol_cols=vol_cols, chans=chans,
     )
     h = lax.all_to_all(out.reshape(members, part, vol_cols), GROUP, split_axis=0, concat_axis=0, tiled=True)

time: 53.3 us -> 51.7 us (0.970)
  blocking collectives: 12.5 us -> 31.4 us
  waiting for transfers between devices: 13.7 us -> 1.25 us
  starting transfers between devices: 14.1 us -> 7.05 us
  other arithmetic: 1.75 us -> 0.91 us
    all_to_all x0 -> x1, blocking collectives: none -> 19.4 us  [local(): got = lax.all_to_all(sent, GROUP, split_axis=0, concat_axis=0, tiled=True)]
    all_to_all x1 -> x0, waiting for transfers between devices: 12.6 us -> none  [local(): got = lax.all_to_all(sent, GROUP, split_axis=0, concat_axis=0, tiled=True)]
    all_to_all x1 -> x0, starting transfers between devices: 7.03 us -> none  [local(): got = lax.all_to_all(sent, GROUP, split_axis=0, concat_axis=0, tiled=True)]
    concatenate x1, other arithmetic: 0.88 us -> 0.05 us  [local(): sent = jnp.concatenate([sent_volume, sent_weights], axis=2)]
    all_to_all x1, blocking collectives: 12.5 us -> 12 us  [local(): lax.all_to_all(out.reshape(members, part, vol_cols), GROUP, split_axis=0,...]
  transfers between devices with their start and end apart: 3 -> 2, of which waited for: 2 -> 1; matrix products, arithmetic and copies ran while one was open for 0% -> 0% of each run, Pallas kernels for 6% -> 7%
where the time goes in v18:
time: 51.7 us; the launch traced here: 51.4 us
  blocking collectives  31.4 us (61%)
  Pallas kernels  8.45 us (16%)
  starting transfers between devices  7.05 us (14%)
  local copies, waits for them, and re-layouts  2.29 us (4%)
  waiting for transfers between devices  1.25 us (2%)
  other arithmetic  0.91 us (2%)
    all_to_all x1, blocking collectives, local(): got = lax.all_to_all(sent, GROUP, split_axis=0, concat_axis=0, tiled=True)  19.4 us
    all_to_all x1, blocking collectives, local(): lax.all_to_all(out.reshape(members, part, vol_cols), GROUP, split_axis=0,...  12 us
    pallas_call x4, Pallas kernels, run(): pl.pallas_call(functools.partial(kernel, **params), out_shape=out_shape,...  8.45 us
    ppermute x2, starting transfers between devices, shift_z(): return lax.ppermute(block, 'z', route)  7.05 us
    ppermute x2, waiting for transfers between devices, shift_z(): return lax.ppermute(block, 'z', route)  1.25 us
  transfers between devices with their start and end apart: 2, of which 1 were waited for; matrix products, arithmetic and copies ran while one was open for 0% of the time, Pallas kernels for 7%

profile of v18, /device:TPU:96, one launch (start us, length us, event | category | flops | bytes accessed | tf_op | source)
XLA Modules:
  0.0 51.4 jit_solution(431182650469088778)
XLA Ops:
  0.0 0.0 copy-start
  0.0 0.8 %maximum_bitcast_fusion = bf16[8,2,2,3,3,64]{5,0,4,3,1,2:T(8,128)(2,1)S(1)} fusion(bf16[1,2,8,64,3,3]{3,2,5,4,1,0:T(8,128)(2,1)} %bitcast.29, bf16[1,2,8,64,3,3]{3,2,5,4,1,0:T(8,128)(2,1)} %bitcast.30), kind=kLoop, calls=%fused_computation.2 | loop fusion | flops 18432 | bytes 73728 | tf_op jit(solution)/shard_map/transpose | solution.py:26
  0.9 0.1 reshape.28
  1.0 0.7 %copy.9 = bf16[8,2,3,64]{3,2,0,1:T(4,128)(2,1)S(1)} copy(bf16[8,2,3,64]{3,0,2,1:T(8,128)(2,1)} %bitcast.31) | data formatting | bytes 12288 | tf_op jit(solution)/shard_map/transpose | solution.py:28
  1.8 0.1 reshape.29
  1.8 0.0 copy-done
  1.8 0.1 reshape.26
  2.0 0.2 copy.7
  2.2 19.4 %all_to_all.10 = bf16[16,8,2368]{2,1,0:T(8,128)(2,1)S(1)} all-to-all(bf16[16,8,2368]{2,1,0:T(8,128)(2,1)S(1)} %pad_maximum_fusion), channel_id=1, replica_groups=mesh['z'=8,'yh'=2,'core'=2,'ch'=8] {'yh','ch'}, dimensions={0} | all-to-all | bytes 1212416 | tf_op jit(solution)/shard_map/all_to_all | solution.py:142
  21.7 2.0 %collective-permute-start.1 = (bf16[128,1024]{1,0:T(8,128)(2,1)S(1)}, bf16[128,1024]{1,0:T(8,128)(2,1)S(1)}, u32[]{:S(2)}, u32[]{:S(2)}) collective-permute-start(bf16[128,1024]{1,0:T(8,128)(2,1)S(1)} %slice.4), channel_id=1, source_target_pairs={{32,0},{64,32},{96,64},{128,96},{160,128},{192,160},{224,192},{33,... | collective-permute-start | bytes 786440 | tf_op jit(solution)/shard_map/ppermute | solution.py:70
  23.7 5.0 %collective-permute-start = (bf16[128,1024]{1,0:T(8,128)(2,1)S(1)}, bf16[128,1024]{1,0:T(8,128)(2,1)S(1)}, u32[]{:S(2)}, u32[]{:S(2)}) collective-permute-start(bf16[128,1024]{1,0:T(8,128)(2,1)S(1)} %slice.4), channel_id=1, source_target_pairs={{0,32},{32,64},{64,96},{96,128},{128,160},{160,192},{192,224},{1,3... | collective-permute-start | bytes 786440 | tf_op jit(solution)/shard_map/ppermute | solution.py:70
  28.7 1.7 %shard_map.47.own_ref = bf16[64,2048]{1,0:T(8,128)(2,1)S(1)} custom-call(bf16[128,2368]{1,0:T(8,128)(2,1)S(1)} %bitcast.20), custom_call_target="tpu_custom_call" | custom-call | tf_op jit(solution)/shard_map/pallas_call | solution.py:122
  30.4 1.2 %collective-permute-done.1.side_ref = bf16[128,1024]{1,0:T(8,128)(2,1)S(1)} collective-permute-done((bf16[128,1024]{1,0:T(8,128)(2,1)S(1)}, bf16[128,1024]{1,0:T(8,128)(2,1)S(1)}, u32[]{:S(2)}, u32[]{:S(2)}) %collective-permute-start.1) | collective-permute-done | bytes 262176 | tf_op jit(solution)/shard_map/ppermute | solution.py:70
  31.7 1.7 %shard_map.48.right_ref = bf16[64,2048]{1,0:T(8,128)(2,1)S(1)} custom-call(bf16[128,1024]{1,0:T(8,128)(2,1)S(1)} %collective-permute-done.1.side_ref, bf16[128,2368]{1,0:T(8,128)(2,1)S(1)} %bitcast.21), custom_call_target="tpu_custom_call" | custom-call | tf_op jit(solution)/shard_map/pallas_call | solution.py:122
  33.4 0.0 collective-permute-done.side_ref
  33.4 1.7 %shard_map.46.left_ref = bf16[64,2048]{1,0:T(8,128)(2,1)S(1)} custom-call(bf16[128,1024]{1,0:T(8,128)(2,1)S(1)} %collective-permute-done.side_ref, bf16[128,2368]{1,0:T(8,128)(2,1)S(1)} %bitcast.22), custom_call_target="tpu_custom_call" | custom-call | tf_op jit(solution)/shard_map/pallas_call | solution.py:122
  35.1 3.3 %shard_map.49 = bf16[128,1024]{1,0:T(8,128)(2,1)S(1)} custom-call(bf16[64,2048]{1,0:T(8,128)(2,1)S(1)} %shard_map.46.left_ref, bf16[64,2048]{1,0:T(8,128)(2,1)S(1)} %shard_map.47.own_ref, bf16[64,2048]{1,0:T(8,128)(2,1)S(1)} %shard_map.48.right_ref, bf16[128,2368]{1,0:T(8,128)(2,1)S(1)} %bitcast.23), custom_call_target="tpu_custom_call" | custom-call | tf_op jit(solution)/shard_map/pallas_call | solution.py:122
  38.5 12.0 %all_to_all.11 = bf16[16,8,1024]{2,1,0:T(8,128)(2,1)S(1)} all-to-all(bf16[16,8,1024]{2,1,0:T(8,128)(2,1)S(1)} %bitcast.24), channel_id=1, replica_groups=mesh['z'=8,'yh'=2,'core'=2,'ch'=8] {'yh','ch'}, dimensions={0} | all-to-all | bytes 524288 | tf_op jit(solution)/shard_map/all_to_all | solution.py:156
  50.4 0.2 copy.12
  50.6 0.8 %reshape.33 = bf16[8,32,512]{2,1,0:T(8,128)(2,1)} reshape(bf16[8,16,2,512]{3,2,1,0:T(2,128)(2,1)S(1)} %bitcast.27) | data formatting | bytes 524288 | tf_op jit(solution)/shard_map/reshape | solution.py:158
  (5 shorter events, 0.1 us)
Async XLA Ops:
  0.0 1.8 %copy-start = (bf16[8,32,512]{2,1,0:T(8,128)(2,1)S(1)}, bf16[8,32,512]{2,1,0:T(8,128)(2,1)}, u32[]{:S(2)}) copy-start(bf16[8,32,512]{2,1,0:T(8,128)(2,1)} %param.4) | copy-start | bytes 786436
  21.7 10.0 %collective-permute-start.1 = (bf16[128,1024]{1,0:T(8,128)(2,1)S(1)}, bf16[128,1024]{1,0:T(8,128)(2,1)S(1)}, u32[]{:S(2)}, u32[]{:S(2)}) collective-permute-start(bf16[128,1024]{1,0:T(8,128)(2,1)S(1)} %slice.4), channel_id=1, source_target_pairs={{32,0},{64,32},{96,64},{128,96},{160,128},{192,160},{224,192},{33,... | collective-permute-start | bytes 786440 | tf_op jit(solution)/shard_map/ppermute | solution.py:70
  23.7 9.7 %collective-permute-start = (bf16[128,1024]{1,0:T(8,128)(2,1)S(1)}, bf16[128,1024]{1,0:T(8,128)(2,1)S(1)}, u32[]{:S(2)}, u32[]{:S(2)}) collective-permute-start(bf16[128,1024]{1,0:T(8,128)(2,1)S(1)} %slice.4), channel_id=1, source_target_pairs={{0,32},{32,64},{64,96},{96,128},{128,160},{160,192},{192,224},{1,3... | collective-permute-start | bytes 786440 | tf_op jit(solution)/shard_map/ppermute | solution.py:70

commit v19 on v18

--- a/solution.py
+++ b/solution.py
@@ -97,9 +97,12 @@
     return jnp.dot(src_ref[rows, at : at + 3 * chans], stacked, preferred_element_type=jnp.float32)
 
 
-def _rest_kernel(left_ref, own_ref, right_ref, src_ref, o_ref, *, vol_cols, chans):
+def _rest_kernel(side_ref, own_ref, right_ref, src_ref, o_ref, *, vol_cols, chans):
     w = vol_cols
-    q = [left_ref[:, :w], left_ref[:, w:], own_ref[:, :w], own_ref[:, w:],
+    left = _planes(
+        jnp.concatenate([side_ref[:chans], side_ref[chans:]], axis=1), src_ref, 0, vol_cols, chans
+    )
+    q = [left[:, :w], left[:, w:], own_ref[:, :w], own_ref[:, w:],
          right_ref[:, :w], right_ref[:, w:]]
     total = _depth(
         [jnp.concatenate(q[0:4], axis=1), jnp.concatenate(q[1:5], axis=1), jnp.concatenate(q[2:6], axis=1)],
@@ -147,7 +150,6 @@
     shape = functools.partial(pltpu.VMEM, dtype=jnp.bfloat16)
     own = run(_own_kernel, [src], shape((chans, 2 * vol_cols)), vol_cols=vol_cols, chans=chans)
     pair = shape((chans, 2 * vol_cols))
-    left = run(_side_kernel, [left, src], pair, vol_cols=vol_cols, chans=chans)
     right = run(_side_kernel, [right, src], pair, vol_cols=vol_cols, chans=chans)
     out = run(
         _rest_kernel, [left, own, right, src], shape((2 * chans, vol_cols)),

time: 51.7 us -> 51.9 us (level)
    pallas_call x4 -> x3, Pallas kernels: 8.45 us -> 8.67 us  [run(): pl.pallas_call(functools.partial(kernel, **params), out_shape=out_shape,...]
where the time goes in v19:
time: 51.9 us; the launch traced here: 51.7 us
  blocking collectives  31.4 us (61%)
  Pallas kernels  8.67 us (17%)
  starting transfers between devices  7.05 us (14%)
  local copies, waits for them, and re-layouts  2.29 us (4%)
  waiting for transfers between devices  1.25 us (2%)
  other arithmetic  0.91 us (2%)
    all_to_all x1, blocking collectives, local(): got = lax.all_to_all(sent, GROUP, split_axis=0, concat_axis=0, tiled=True)  19.4 us
    all_to_all x1, blocking collectives, local(): lax.all_to_all(out.reshape(members, part, vol_cols), GROUP, split_axis=0,...  12 us
    pallas_call x3, Pallas kernels, run(): pl.pallas_call(functools.partial(kernel, **params), out_shape=out_shape,...  8.67 us
    ppermute x2, starting transfers between devices, shift_z(): return lax.ppermute(block, 'z', route)  7.05 us
    ppermute x2, waiting for transfers between devices, shift_z(): return lax.ppermute(block, 'z', route)  1.25 us
  transfers between devices with their start and end apart: 2, of which 1 were waited for; matrix products, arithmetic and copies ran while one was open for 0% of the time, Pallas kernels for 7%

profile of v19, /device:TPU:96, one launch (start us, length us, event | category | flops | bytes accessed | tf_op | source)
XLA Modules:
  0.0 51.7 jit_solution(4809209754663617173)
XLA Ops:
  0.0 0.0 copy-start
  0.0 0.8 %maximum_bitcast_fusion = bf16[8,2,2,3,3,64]{5,0,4,3,1,2:T(8,128)(2,1)S(1)} fusion(bf16[1,2,8,64,3,3]{3,2,5,4,1,0:T(8,128)(2,1)} %bitcast.28, bf16[1,2,8,64,3,3]{3,2,5,4,1,0:T(8,128)(2,1)} %bitcast.29), kind=kLoop, calls=%fused_computation.2 | loop fusion | flops 18432 | bytes 73728 | tf_op jit(solution)/shard_map/transpose | solution.py:26
  0.9 0.1 reshape.28
  1.0 0.7 %copy.9 = bf16[8,2,3,64]{3,2,0,1:T(4,128)(2,1)S(1)} copy(bf16[8,2,3,64]{3,0,2,1:T(8,128)(2,1)} %bitcast.30) | data formatting | bytes 12288 | tf_op jit(solution)/shard_map/transpose | solution.py:28
  1.8 0.1 reshape.29
  1.8 0.0 copy-done
  1.8 0.1 reshape.26
  2.0 0.2 copy.7
  2.2 19.4 %all_to_all.10 = bf16[16,8,2368]{2,1,0:T(8,128)(2,1)S(1)} all-to-all(bf16[16,8,2368]{2,1,0:T(8,128)(2,1)S(1)} %pad_maximum_fusion), channel_id=1, replica_groups=mesh['z'=8,'yh'=2,'core'=2,'ch'=8] {'yh','ch'}, dimensions={0} | all-to-all | bytes 1212416 | tf_op jit(solution)/shard_map/all_to_all | solution.py:145
  21.7 2.0 %collective-permute-start.1 = (bf16[128,1024]{1,0:T(8,128)(2,1)S(1)}, bf16[128,1024]{1,0:T(8,128)(2,1)S(1)}, u32[]{:S(2)}, u32[]{:S(2)}) collective-permute-start(bf16[128,1024]{1,0:T(8,128)(2,1)S(1)} %slice.4), channel_id=1, source_target_pairs={{32,0},{64,32},{96,64},{128,96},{160,128},{192,160},{224,192},{33,... | collective-permute-start | bytes 786440 | tf_op jit(solution)/shard_map/ppermute | solution.py:70
  23.7 5.0 %collective-permute-start = (bf16[128,1024]{1,0:T(8,128)(2,1)S(1)}, bf16[128,1024]{1,0:T(8,128)(2,1)S(1)}, u32[]{:S(2)}, u32[]{:S(2)}) collective-permute-start(bf16[128,1024]{1,0:T(8,128)(2,1)S(1)} %slice.4), channel_id=1, source_target_pairs={{0,32},{32,64},{64,96},{96,128},{128,160},{160,192},{192,224},{1,3... | collective-permute-start | bytes 786440 | tf_op jit(solution)/shard_map/ppermute | solution.py:70
  28.7 1.7 %shard_map.46.own_ref = bf16[64,2048]{1,0:T(8,128)(2,1)S(1)} custom-call(bf16[128,2368]{1,0:T(8,128)(2,1)S(1)} %bitcast.20), custom_call_target="tpu_custom_call" | custom-call | tf_op jit(solution)/shard_map/pallas_call | solution.py:125
  30.4 1.2 %collective-permute-done.1.side_ref = bf16[128,1024]{1,0:T(8,128)(2,1)S(1)} collective-permute-done((bf16[128,1024]{1,0:T(8,128)(2,1)S(1)}, bf16[128,1024]{1,0:T(8,128)(2,1)S(1)}, u32[]{:S(2)}, u32[]{:S(2)}) %collective-permute-start.1) | collective-permute-done | bytes 262176 | tf_op jit(solution)/shard_map/ppermute | solution.py:70
  31.7 1.7 %shard_map.47.right_ref = bf16[64,2048]{1,0:T(8,128)(2,1)S(1)} custom-call(bf16[128,1024]{1,0:T(8,128)(2,1)S(1)} %collective-permute-done.1.side_ref, bf16[128,2368]{1,0:T(8,128)(2,1)S(1)} %bitcast.21), custom_call_target="tpu_custom_call" | custom-call | tf_op jit(solution)/shard_map/pallas_call | solution.py:125
  33.4 0.0 collective-permute-done.side_ref
  33.4 5.3 %shard_map.48 = bf16[128,1024]{1,0:T(8,128)(2,1)S(1)} custom-call(bf16[128,1024]{1,0:T(8,128)(2,1)S(1)} %collective-permute-done.side_ref, bf16[64,2048]{1,0:T(8,128)(2,1)S(1)} %shard_map.46.own_ref, bf16[64,2048]{1,0:T(8,128)(2,1)S(1)} %shard_map.47.right_ref, bf16[128,2368]{1,0:T(8,128)(2,1)S(1)} %bitcast.22), custom_call_target="tpu_custom_call" | custom-call | tf_op jit(solution)/shard_map/pallas_call | solution.py:125
  38.7 12.0 %all_to_all.11 = bf16[16,8,1024]{2,1,0:T(8,128)(2,1)S(1)} all-to-all(bf16[16,8,1024]{2,1,0:T(8,128)(2,1)S(1)} %bitcast.23), channel_id=1, replica_groups=mesh['z'=8,'yh'=2,'core'=2,'ch'=8] {'yh','ch'}, dimensions={0} | all-to-all | bytes 524288 | tf_op jit(solution)/shard_map/all_to_all | solution.py:158
  50.6 0.2 copy.12
  50.9 0.8 %reshape.33 = bf16[8,32,512]{2,1,0:T(8,128)(2,1)} reshape(bf16[8,16,2,512]{3,2,1,0:T(2,128)(2,1)S(1)} %bitcast.26) | data formatting | bytes 524288 | tf_op jit(solution)/shard_map/reshape | solution.py:160
  (5 shorter events, 0.1 us)
Async XLA Ops:
  0.0 1.8 %copy-start = (bf16[8,32,512]{2,1,0:T(8,128)(2,1)S(1)}, bf16[8,32,512]{2,1,0:T(8,128)(2,1)}, u32[]{:S(2)}) copy-start(bf16[8,32,512]{2,1,0:T(8,128)(2,1)} %param.4) | copy-start | bytes 786436
  21.7 10.0 %collective-permute-start.1 = (bf16[128,1024]{1,0:T(8,128)(2,1)S(1)}, bf16[128,1024]{1,0:T(8,128)(2,1)S(1)}, u32[]{:S(2)}, u32[]{:S(2)}) collective-permute-start(bf16[128,1024]{1,0:T(8,128)(2,1)S(1)} %slice.4), channel_id=1, source_target_pairs={{32,0},{64,32},{96,64},{128,96},{160,128},{192,160},{224,192},{33,... | collective-permute-start | bytes 786440 | tf_op jit(solution)/shard_map/ppermute | solution.py:70
  23.7 9.7 %collective-permute-start = (bf16[128,1024]{1,0:T(8,128)(2,1)S(1)}, bf16[128,1024]{1,0:T(8,128)(2,1)S(1)}, u32[]{:S(2)}, u32[]{:S(2)}) collective-permute-start(bf16[128,1024]{1,0:T(8,128)(2,1)S(1)} %slice.4), channel_id=1, source_target_pairs={{0,32},{32,64},{64,96},{96,128},{128,160},{160,192},{192,224},{1,3... | collective-permute-start | bytes 786440 | tf_op jit(solution)/shard_map/ppermute | solution.py:70

commit v20 on v18

--- a/solution.py
+++ b/solution.py
@@ -118,6 +118,12 @@
     o_ref[...] = jnp.concatenate([h[:, :w], h[:, w:]], axis=0)
 
 
+def _place_kernel(h_ref, o_ref, *, per, flat):
+    for m in range(h_ref.shape[0]):
+        for r in range(per):
+            o_ref[:, m * per + r, :] = h_ref[m, :, r * flat : (r + 1) * flat]
+
+
 def run(kernel, inputs, out_shape, **params):
     return pl.pallas_call(
         functools.partial(kernel, **params),
@@ -154,8 +160,11 @@
         vol_cols=vol_cols, chans=chans,
     )
     h = lax.all_to_all(out.reshape(members, part, vol_cols), GROUP, split_axis=0, concat_axis=0, tiled=True)
-    h = jnp.transpose(h.reshape(members, part, per, flat), (1, 0, 2, 3))
-    return h.reshape(part, slab, flat)
+    return pl.pallas_call(
+        functools.partial(_place_kernel, per=per, flat=flat),
+        out_shape=jax.ShapeDtypeStruct((part, slab, flat), jnp.bfloat16),
+        in_specs=[ANYWHERE_VMEM],
+    )(*in_vmem([h]))
 
 
 def solution(mesh):

time: 51.7 us -> 51.7 us (level)
  local copies, waits for them, and re-layouts: 2.29 us -> 1.28 us
  Pallas kernels: 8.45 us -> 9.45 us
    reshape x2 -> x0, local copies, waits for them, and re-layouts: 1.01 us -> none  [the longest x1 0.8 us: local(): return h.reshape(part, slab, flat)]
    pallas_call x0 -> x1, Pallas kernels: none -> 1.01 us  [local(): pl.pallas_call(functools.partial(_place_kernel, per=per, flat=flat), out_...]
where the time goes in v20:
time: 51.7 us; the launch traced here: 51.4 us
  blocking collectives  31.4 us (61%)
  Pallas kernels  9.45 us (18%)
  starting transfers between devices  7.05 us (14%)
  local copies, waits for them, and re-layouts  1.28 us (2%)
  waiting for transfers between devices  1.25 us (2%)
  other arithmetic  0.91 us (2%)
    all_to_all x1, blocking collectives, local(): got = lax.all_to_all(sent, GROUP, split_axis=0, concat_axis=0, tiled=True)  19.4 us
    all_to_all x1, blocking collectives, local(): lax.all_to_all(out.reshape(members, part, vol_cols), GROUP, split_axis=0,...  12 us
    pallas_call x4, Pallas kernels, run(): pl.pallas_call(functools.partial(kernel, **params), out_shape=out_shape,...  8.45 us
    ppermute x2, starting transfers between devices, shift_z(): return lax.ppermute(block, 'z', route)  7.05 us
    ppermute x2, waiting for transfers between devices, shift_z(): return lax.ppermute(block, 'z', route)  1.25 us
  transfers between devices with their start and end apart: 2, of which 1 were waited for; matrix products, arithmetic and copies ran while one was open for 0% of the time, Pallas kernels for 7%

profile of v20, /device:TPU:96, one launch (start us, length us, event | category | flops | bytes accessed | tf_op | source)
XLA Modules:
  0.0 51.4 jit_solution(2822143562643923257)
XLA Ops:
  0.0 0.0 copy-start
  0.0 0.8 %maximum_bitcast_fusion = bf16[8,2,2,3,3,64]{5,0,4,3,1,2:T(8,128)(2,1)S(1)} fusion(bf16[1,2,8,64,3,3]{3,2,5,4,1,0:T(8,128)(2,1)} %bitcast.23, bf16[1,2,8,64,3,3]{3,2,5,4,1,0:T(8,128)(2,1)} %bitcast.24), kind=kLoop, calls=%fused_computation.1 | loop fusion | flops 18432 | bytes 73728 | tf_op jit(solution)/shard_map/transpose | solution.py:26
  0.9 0.1 reshape.22
  1.0 0.7 %copy.8 = bf16[8,2,3,64]{3,2,0,1:T(4,128)(2,1)S(1)} copy(bf16[8,2,3,64]{3,0,2,1:T(8,128)(2,1)} %bitcast.25) | data formatting | bytes 12288 | tf_op jit(solution)/shard_map/transpose | solution.py:28
  1.8 0.1 reshape.23
  1.8 0.0 copy-done
  1.8 0.1 reshape.20
  2.0 0.2 copy.6
  2.2 19.4 %all_to_all.10 = bf16[16,8,2368]{2,1,0:T(8,128)(2,1)S(1)} all-to-all(bf16[16,8,2368]{2,1,0:T(8,128)(2,1)S(1)} %pad_maximum_fusion), channel_id=1, replica_groups=mesh['z'=8,'yh'=2,'core'=2,'ch'=8] {'yh','ch'}, dimensions={0} | all-to-all | bytes 1212416 | tf_op jit(solution)/shard_map/all_to_all | solution.py:148
  21.7 2.0 %collective-permute-start.1 = (bf16[128,1024]{1,0:T(8,128)(2,1)S(1)}, bf16[128,1024]{1,0:T(8,128)(2,1)S(1)}, u32[]{:S(2)}, u32[]{:S(2)}) collective-permute-start(bf16[128,1024]{1,0:T(8,128)(2,1)S(1)} %slice.4), channel_id=1, source_target_pairs={{32,0},{64,32},{96,64},{128,96},{160,128},{192,160},{224,192},{33,... | collective-permute-start | bytes 786440 | tf_op jit(solution)/shard_map/ppermute | solution.py:70
  23.7 5.0 %collective-permute-start = (bf16[128,1024]{1,0:T(8,128)(2,1)S(1)}, bf16[128,1024]{1,0:T(8,128)(2,1)S(1)}, u32[]{:S(2)}, u32[]{:S(2)}) collective-permute-start(bf16[128,1024]{1,0:T(8,128)(2,1)S(1)} %slice.4), channel_id=1, source_target_pairs={{0,32},{32,64},{64,96},{96,128},{128,160},{160,192},{192,224},{1,3... | collective-permute-start | bytes 786440 | tf_op jit(solution)/shard_map/ppermute | solution.py:70
  28.7 1.7 %shard_map.47.own_ref = bf16[64,2048]{1,0:T(8,128)(2,1)S(1)} custom-call(bf16[128,2368]{1,0:T(8,128)(2,1)S(1)} %bitcast.16), custom_call_target="tpu_custom_call" | custom-call | tf_op jit(solution)/shard_map/pallas_call | solution.py:128
  30.4 1.2 %collective-permute-done.1.side_ref = bf16[128,1024]{1,0:T(8,128)(2,1)S(1)} collective-permute-done((bf16[128,1024]{1,0:T(8,128)(2,1)S(1)}, bf16[128,1024]{1,0:T(8,128)(2,1)S(1)}, u32[]{:S(2)}, u32[]{:S(2)}) %collective-permute-start.1) | collective-permute-done | bytes 262176 | tf_op jit(solution)/shard_map/ppermute | solution.py:70
  31.7 1.7 %shard_map.48.right_ref = bf16[64,2048]{1,0:T(8,128)(2,1)S(1)} custom-call(bf16[128,1024]{1,0:T(8,128)(2,1)S(1)} %collective-permute-done.1.side_ref, bf16[128,2368]{1,0:T(8,128)(2,1)S(1)} %bitcast.17), custom_call_target="tpu_custom_call" | custom-call | tf_op jit(solution)/shard_map/pallas_call | solution.py:128
  33.4 0.0 collective-permute-done.side_ref
  33.4 1.7 %shard_map.46.left_ref = bf16[64,2048]{1,0:T(8,128)(2,1)S(1)} custom-call(bf16[128,1024]{1,0:T(8,128)(2,1)S(1)} %collective-permute-done.side_ref, bf16[128,2368]{1,0:T(8,128)(2,1)S(1)} %bitcast.18), custom_call_target="tpu_custom_call" | custom-call | tf_op jit(solution)/shard_map/pallas_call | solution.py:128
  35.1 3.3 %shard_map.49 = bf16[128,1024]{1,0:T(8,128)(2,1)S(1)} custom-call(bf16[64,2048]{1,0:T(8,128)(2,1)S(1)} %shard_map.46.left_ref, bf16[64,2048]{1,0:T(8,128)(2,1)S(1)} %shard_map.47.own_ref, bf16[64,2048]{1,0:T(8,128)(2,1)S(1)} %shard_map.48.right_ref, bf16[128,2368]{1,0:T(8,128)(2,1)S(1)} %bitcast.19), custom_call_target="tpu_custom_call" | custom-call | tf_op jit(solution)/shard_map/pallas_call | solution.py:128
  38.5 12.0 %all_to_all.11.h_ref = bf16[16,8,1024]{2,1,0:T(8,128)(2,1)S(1)} all-to-all(bf16[16,8,1024]{2,1,0:T(8,128)(2,1)S(1)} %bitcast.20), channel_id=1, replica_groups=mesh['z'=8,'yh'=2,'core'=2,'ch'=8] {'yh','ch'}, dimensions={0} | all-to-all | bytes 524288 | tf_op jit(solution)/shard_map/all_to_all | solution.py:162
  50.4 1.0 %shard_map.50 = bf16[8,32,512]{2,1,0:T(8,128)(2,1)} custom-call(bf16[16,8,1024]{2,1,0:T(8,128)(2,1)S(1)} %all_to_all.11.h_ref), custom_call_target="tpu_custom_call" | custom-call | tf_op jit(solution)/shard_map/pallas_call | solution.py:163
  (5 shorter events, 0.1 us)
Async XLA Ops:
  0.0 1.8 %copy-start = (bf16[8,32,512]{2,1,0:T(8,128)(2,1)S(1)}, bf16[8,32,512]{2,1,0:T(8,128)(2,1)}, u32[]{:S(2)}) copy-start(bf16[8,32,512]{2,1,0:T(8,128)(2,1)} %param.4) | copy-start | bytes 786436
  21.7 10.0 %collective-permute-start.1 = (bf16[128,1024]{1,0:T(8,128)(2,1)S(1)}, bf16[128,1024]{1,0:T(8,128)(2,1)S(1)}, u32[]{:S(2)}, u32[]{:S(2)}) collective-permute-start(bf16[128,1024]{1,0:T(8,128)(2,1)S(1)} %slice.4), channel_id=1, source_target_pairs={{32,0},{64,32},{96,64},{128,96},{160,128},{192,160},{224,192},{33,... | collective-permute-start | bytes 786440 | tf_op jit(solution)/shard_map/ppermute | solution.py:70
  23.7 9.7 %collective-permute-start = (bf16[128,1024]{1,0:T(8,128)(2,1)S(1)}, bf16[128,1024]{1,0:T(8,128)(2,1)S(1)}, u32[]{:S(2)}, u32[]{:S(2)}) collective-permute-start(bf16[128,1024]{1,0:T(8,128)(2,1)S(1)} %slice.4), channel_id=1, source_target_pairs={{0,32},{32,64},{64,96},{96,128},{128,160},{160,192},{192,224},{1,3... | collective-permute-start | bytes 786440 | tf_op jit(solution)/shard_map/ppermute | solution.py:70
